TPU v7x, 256 devices: a whole 4x4x8 slice. The times are simulated.
256 devices in a mesh: seq: 8 (over x, core), vocab: 32 (over z, y).
Axes of the slice: x: 4, y: 4, z: 8, core: 2. Of those that a mesh axis runs over, the one named last changes fastest.
Arguments:
- hidden: bfloat16 [2048, 4096], P('seq'), may hold values from -48 to 48
- head_weight: bfloat16 [4096, 65536], P('seq', 'vocab'), may hold values from -0.09375 to 0.09375
- queries: float32 [16, 65536], P(None, 'vocab'), may hold values from 0 to 1, as said below
- passage_lengths: int32 [32], replicated, may hold values from 1 to 192, 2048 in all
- pairing: int32 [32], replicated, may hold values from 0 to 15
- doc_freq: int32 [65536], P('vocab'), may hold values from 0 to 4194304
Outputs:
- grad_hidden: bfloat16 [2048, 4096], P('seq', 'vocab')
- losses: float32 [2], replicated
Inputs may be any that keep to these rules, and one draw needn't show every extreme that they name: `queries`: entries are nonnegative.
All inputs are finite; a program needn't handle non-finite values.
Results may differ from a plain program's by a relative error of at most 0.0039.
Values may be sent and summed in bfloat16 or wider, within the bound.
No kernel may reach another device: no remote copies, remote signals or barrier semaphores. Data moves between devices by JAX's collectives and lax.ppermute only.
A program may use at most 128 MiB of HBM per device.

v0:
```python
import jax
import jax.numpy as jnp
from jax import lax
from jax.sharding import PartitionSpec as P

DOCS = 4194304


sharpness = 8.0
loss_scale = 16384.0
flops_weight = 32.0
highest = lax.Precision.HIGHEST


def softmax_terms(scores, pair_rows):
    onehot = (jnp.arange(scores.shape[0], dtype=jnp.int32)[:, None] == pair_rows[None, :]).astype(
        jnp.float32
    )
    peak_score = jnp.max(scores, axis=0)
    shifted = jnp.exp(scores - peak_score[None, :])
    denominator = jnp.sum(shifted, axis=0)
    log_total = peak_score + jnp.log(denominator)
    losses_each = log_total - jnp.sum(onehot * scores, axis=0)
    return (losses_each, shifted / denominator[None, :] - onehot)


def per_device(hidden, head_weight, queries, passage_lengths, pairing, doc_freq):
    tok_rows = hidden.shape[0]
    vocab_cols = head_weight.shape[1]
    passages = passage_lengths.shape[0]
    vocab_total = vocab_cols * lax.axis_size("vocab")
    finish = jnp.cumsum(passage_lengths)
    starts = finish - passage_lengths
    position = lax.axis_index("seq") * tok_rows + jnp.arange(tok_rows, dtype=jnp.int32)
    member = (
        (position[None, :] >= starts[:, None]) & (position[None, :] < finish[:, None])
    ).astype(jnp.float32)
    counts = passage_lengths.astype(jnp.float32)
    weights_df = jnp.log(1.0 + DOCS / (1.0 + doc_freq.astype(jnp.float32)))
    flops_grad = loss_scale * flops_weight * 2.0 / (vocab_total * passages)
    full_head = lax.all_gather(head_weight, "seq", axis=0, tiled=True)
    logits = jnp.dot(hidden, full_head, preferred_element_type=jnp.float32)
    lifted = 1.0 + jax.nn.relu(logits)
    squared = lifted * lifted
    fourth = squared * squared
    powered = fourth * fourth
    local_sums = jnp.dot(member, powered, precision=highest)
    totals = lax.psum(local_sums, "seq")
    pooled = (jnp.log(totals) - jnp.log(counts)[:, None]) / sharpness
    col_mean = jnp.sum(pooled, axis=0) / passages
    flops_part = jnp.sum(weights_df * col_mean * col_mean) / vocab_total
    scores, flops_value = lax.psum(
        (jnp.dot(queries, pooled.T, precision=highest), flops_part), "vocab"
    )
    losses_each, probs = softmax_terms(scores, pairing)
    contrast = jnp.mean(losses_each)
    dscores = probs * (loss_scale / passages)
    dpooled = jnp.dot(dscores.T, queries, precision=highest) + flops_grad * weights_df * col_mean
    factor = dpooled / totals
    spread = lax.dot_general(member, factor, (((0,), (0,)), ((), ())), precision=highest)
    seventh = fourth * squared * lifted
    dlogits = jnp.where(logits > 0, spread * seventh, 0.0).astype(jnp.bfloat16)
    grad_cols = lax.psum_scatter(
        lax.dot_general(
            full_head, dlogits, (((1,), (1,)), ((), ())), preferred_element_type=jnp.float32
        ),
        "vocab",
        scatter_dimension=0,
        tiled=True,
    )
    losses = jnp.stack([contrast, flops_value])
    return (grad_cols.T.astype(jnp.bfloat16), losses)


def solution(mesh):
    placed = (P("seq", None), P("seq", "vocab"), P(None, "vocab"), P(), P(), P("vocab"))
    return jax.shard_map(
        per_device, mesh=mesh, in_specs=placed, out_specs=(P("seq", "vocab"), P()), check_vma=False
    )
```

profile of v0, /device:TPU:2, one launch (start us, length us, event | category | flops | bytes accessed | tf_op | source)
XLA Modules:
  0.0 500.4 jit_solution(3179952712906589109)
XLA Ops:
  7.2 0.0 copy-start
  7.2 0.0 copy-start.3
  7.2 0.0 all-gather.2.cloned.1.call-start
  7.2 0.7 all-gather.2.cloned.1.call-update
  7.9 0.0 all-reduce.3.cloned.1.call-start
  8.0 0.0 copy-done.3
  8.0 0.1 copy.9
  8.1 0.1 reduce-window.8
  8.1 0.1 reduce
  8.3 91.6 %all-gather.2.cloned.1.call-done = bf16[4096,2048]{1,0:T(8,128)(2,1)} async-done(((bf16[512,2048]{1,0:T(8,128)(2,1)}), bf16[4096,2048]{1,0:T(8,128)(2,1)}) %all-gather.2.cloned.1.call-update) | async-done | bytes 16777232 | tf_op jit(solution)/shard_map/all_gather | solution.py:41
  99.9 0.0 copy-done
  99.9 8.1 %fusion.31 = f32[256,2048]{1,0:T(8,128)S(1)} fusion(bf16[256,4096]{1,0:T(8,128)(2,1)S(1)} %copy-done, bf16[4096,2048]{1,0:T(8,128)(2,1)} %all-gather.2.cloned.1.call-done), kind=kOutput, calls=%fused_computation.51 | convolution fusion | flops 4294967296 | bytes 20971520 | tf_op jit(solution)/shard_map/dot_general | solution.py:42
  108.0 0.0 copy-start.5
  108.0 1.3 copy-done.5
  109.4 0.0 copy-start.2
  109.4 0.0 copy-start.1
  109.4 0.0 copy-start.4
  109.4 1.9 fusion.3
  111.3 0.0 all-reduce.3.cloned.1.call-update
  111.3 0.0 reduce-scatter.2.cloned.1.call-start
  111.4 64.3 %all-reduce.3.cloned.1.call-done = f32[32,2048]{1,0:T(8,128)} async-done(((f32[32,2048]{1,0:T(8,128)}), f32[32,2048]{1,0:T(8,128)}) %all-reduce.3.cloned.1.call-update) | async-done | bytes 262160 | tf_op jit(solution)/shard_map/psum | solution.py:48
  175.6 1.1 fusion.8
  176.7 0.0 copy-done.2
  176.7 0.6 fusion.17
  178.0 0.0 copy-done.1
  178.0 1.3 convolution_bitcast_fusion.1
  179.3 78.1 %all-reduce = (f32[16,32]{1,0:T(8,128)S(1)}, f32[1]{0:T(128)}) all-reduce(f32[16,32]{1,0:T(8,128)S(1)} %convolution_bitcast_fusion.1, f32[1]{0:T(128)} %bitcast.5), channel_id=1, replica_groups=mesh['seq'=8,'vocab'=32] {'vocab'}, use_global_device_ids=true, to_apply=%region_2.3 | all-reduce | flops 513 | bytes 4104 | tf_op jit(solution)/shard_map/psum | solution.py:52
  257.4 0.0 copy-done.4
  257.5 1.4 fusion.2
  258.8 3.2 fusion.1
  262.0 10.1 %convolution_bitcast_fusion = f32[4096,256]{0,1:T(8,128)} fusion(bf16[256,2048]{1,0:T(8,128)(2,1)S(1)} %fusion.1, bf16[4096,2048]{1,0:T(8,128)(2,1)} %all-gather.2.cloned.1.call-done), kind=kOutput, calls=%fused_computation | convolution fusion | flops 4294967296 | bytes 22020096 | tf_op jit(solution)/shard_map/dot_general | solution.py:64
  272.1 0.0 reduce-scatter.2.cloned.1.call-update
  272.1 0.6 subtract_reduce_fusion
  273.4 1.2 pad_maximum_fusion
  274.6 217.8 %reduce-scatter.2.cloned.1.call-done = f32[128,256]{0,1:T(8,128)} async-done(((f32[4096,256]{0,1:T(8,128)}), f32[128,256]{0,1:T(8,128)}) %reduce-scatter.2.cloned.1.call-update) | async-done | bytes 131088 | tf_op jit(solution)/shard_map/reduce_scatter | solution.py:63
  492.4 1.5 convert_bitcast_fusion
  (5 shorter events, 0.1 us)
Async XLA Ops:
  7.2 92.7 %copy-start = (bf16[256,4096]{1,0:T(8,128)(2,1)S(1)}, bf16[256,4096]{1,0:T(8,128)(2,1)}, u32[]{:S(2)}) copy-start(bf16[256,4096]{1,0:T(8,128)(2,1)} %param.6) | copy-start | bytes 6291460
  7.2 0.8 copy-start.3
  7.2 92.7 %all-gather.2.cloned.1.call-start = ((), (), s32[]{:S(2)}) async-start(), calls=%async_computation.1 | async-start | bytes 18874368 | tf_op jit(solution)/shard_map/all_gather | solution.py:41
  7.9 167.7 %all-reduce.3.cloned.1.call-start = ((), (), s32[]{:S(2)}) async-start(), calls=%async_computation.2 | async-start | bytes 524288 | tf_op jit(solution)/shard_map/psum | solution.py:48
  108.0 1.4 copy-start.5
  109.4 67.3 %copy-start.2 = (s32[2048]{0:T(1024)S(1)}, s32[2048]{0:T(1024)}, u32[]{:S(2)}) copy-start(s32[2048]{0:T(1024)} %param.11) | copy-start | bytes 24580
  109.4 68.6 %copy-start.1 = (f32[16,2048]{1,0:T(8,128)S(1)}, f32[16,2048]{1,0:T(8,128)}, u32[]{:S(2)}) copy-start(f32[16,2048]{1,0:T(8,128)} %param.8) | copy-start | bytes 393220
  109.4 148.1 %copy-start.4 = (s32[32]{0:T(128)S(1)}, s32[32]{0:T(128)}, u32[]{:S(2)}) copy-start(s32[32]{0:T(128)} %param.10) | copy-start | bytes 388
  111.3 381.1 %reduce-scatter.2.cloned.1.call-start = ((), (), s32[]{:S(2)}) async-start(), calls=%async_computation.3 | async-start | bytes 4325376 | tf_op jit(solution)/shard_map/reduce_scatter | solution.py:63
Sparse Core Ops, SparseCore 0:
  9.9 89.9 all-gather.1
  111.4 64.1 all-reduce.2
  272.3 220.0 reduce-scatter.1
where the time goes:
time: 501 us; the launch traced here: 500 us
  waiting for transfers between devices  374 us (75%)
  blocking collectives  78.1 us (16%)
  matrix products  25.9 us (5%)
  between operations  15.1 us (3%)
  other arithmetic  5.3 us (1%)
    reduce_scatter x1, waiting for transfers between devices, per_device(): lax.psum_scatter(lax.dot_general(full_head, dlogits, (((1,), (1,)), ((),...  218 us
    all_gather x1, waiting for transfers between devices, per_device(): full_head = lax.all_gather(head_weight, 'seq', axis=0, tiled=True)  91.6 us
    psum x1, blocking collectives, per_device(): lax.psum((jnp.dot(queries, pooled.T, precision=highest), flops_part), 'vo...  78.1 us
    psum x1, waiting for transfers between devices, per_device(): totals = lax.psum(local_sums, 'seq')  64.3 us
    dot_general x1, matrix products, per_device(): lax.dot_general(full_head, dlogits, (((1,), (1,)), ((), ())), preferred_e...  10.1 us
  transfers between devices with their start and end apart: 3, of which 3 were waited for; matrix products, arithmetic and copies ran while one was open for 0% of the time, Pallas kernels for 0%

commit v1 on v0

v1 whole, which is shorter than its diff:
```python
import jax
import jax.numpy as jnp
from jax import lax
from jax.sharding import Mesh, PartitionSpec as P

DOCS = 4194304


sharpness = 8.0
loss_scale = 16384.0
flops_weight = 32.0
highest = lax.Precision.HIGHEST

SEQ = ("sx", "sc")
VOC = ("vz", "vy")


def butterfly(x, axes_sizes):
    for ax, n in axes_sizes:
        d = 1
        while d < n:
            x = jax.tree.map(
                lambda a: a + lax.ppermute(a, ax, [(i, i ^ d) for i in range(n)]), x
            )
            d *= 2
    return x


def softmax_terms(scores, pair_rows):
    onehot = (jnp.arange(scores.shape[0], dtype=jnp.int32)[:, None] == pair_rows[None, :]).astype(
        jnp.float32
    )
    peak_score = jnp.max(scores, axis=0)
    shifted = jnp.exp(scores - peak_score[None, :])
    denominator = jnp.sum(shifted, axis=0)
    log_total = peak_score + jnp.log(denominator)
    losses_each = log_total - jnp.sum(onehot * scores, axis=0)
    return (losses_each, shifted / denominator[None, :] - onehot)


def per_device(sizes, hidden, head_weight, queries, passage_lengths, pairing, doc_freq):
    n_sx, n_sc, n_vz, n_vy = sizes
    tok_rows = hidden.shape[0]
    vocab_cols = head_weight.shape[1]
    passages = passage_lengths.shape[0]
    vocab_total = vocab_cols * n_vz * n_vy
    finish = jnp.cumsum(passage_lengths)
    starts = finish - passage_lengths
    seq_index = lax.axis_index("sx") * n_sc + lax.axis_index("sc")
    position = seq_index * tok_rows + jnp.arange(tok_rows, dtype=jnp.int32)
    member = (
        (position[None, :] >= starts[:, None]) & (position[None, :] < finish[:, None])
    ).astype(jnp.float32)
    counts = passage_lengths.astype(jnp.float32)
    weights_df = jnp.log(1.0 + DOCS / (1.0 + doc_freq.astype(jnp.float32)))
    flops_grad = loss_scale * flops_weight * 2.0 / (vocab_total * passages)
    full_head = lax.all_gather(head_weight, SEQ, axis=0, tiled=True)
    logits = jnp.dot(hidden, full_head, preferred_element_type=jnp.float32)
    lifted = 1.0 + jax.nn.relu(logits)
    squared = lifted * lifted
    fourth = squared * squared
    powered = fourth * fourth
    local_sums = jnp.dot(member, powered, precision=highest)
    totals = butterfly(local_sums, [("sc", n_sc), ("sx", n_sx)])
    pooled = (jnp.log(totals) - jnp.log(counts)[:, None]) / sharpness
    col_mean = jnp.sum(pooled, axis=0) / passages
    flops_part = jnp.sum(weights_df * col_mean * col_mean) / vocab_total
    score_part = jnp.dot(queries, pooled.T, precision=highest)
    flops_row = jnp.where(jnp.arange(passages) == 0, flops_part, 0.0)[None, :]
    summed = butterfly(
        jnp.concatenate([score_part, flops_row], axis=0), [("vy", n_vy), ("vz", n_vz)]
    )
    scores, flops_value = summed[:-1], summed[-1, 0]
    losses_each, probs = softmax_terms(scores, pairing)
    contrast = jnp.mean(losses_each)
    dscores = probs * (loss_scale / passages)
    dpooled = jnp.dot(dscores.T, queries, precision=highest) + flops_grad * weights_df * col_mean
    factor = dpooled / totals
    spread = lax.dot_general(member, factor, (((0,), (0,)), ((), ())), precision=highest)
    seventh = fourth * squared * lifted
    dlogits = jnp.where(logits > 0, spread * seventh, 0.0).astype(jnp.bfloat16)
    partial = lax.dot_general(
        full_head, dlogits, (((1,), (1,)), ((), ())), preferred_element_type=jnp.float32
    )
    grad_cols = lax.psum_scatter(
        lax.psum_scatter(partial, "vz", scatter_dimension=0, tiled=True),
        "vy",
        scatter_dimension=0,
        tiled=True,
    )
    losses = jnp.stack([contrast, flops_value])
    return (grad_cols.T.astype(jnp.bfloat16), losses)


def solution(mesh):
    n_seq, n_voc = mesh.devices.shape
    n_sc = 2
    n_vy = 4
    sizes = (n_seq // n_sc, n_sc, n_voc // n_vy, n_vy)
    mesh4 = Mesh(mesh.devices.reshape(sizes), ("sx", "sc", "vz", "vy"))
    placed = (P(SEQ, None), P(SEQ, VOC), P(None, VOC), P(), P(), P(VOC))
    return jax.shard_map(
        lambda *a: per_device(sizes, *a),
        mesh=mesh4,
        in_specs=placed,
        out_specs=(P(SEQ, VOC), P()),
        check_vma=False,
    )
```

time: 501 us -> 263 us (0.52)
  waiting for transfers between devices: 374 us -> 199 us
  blocking collectives: 78.1 us -> 0 us
  starting transfers between devices: 0.12 us -> 16.9 us
    reduce_scatter x1 -> x2, waiting for transfers between devices: 218 us -> 78.8 us  [the longest x1 56.4 us: per_device(): lax.psum_scatter(partial, 'vz', scatter_dimension=0, tiled=True)]
    psum x1 -> x0, blocking collectives: 78.1 us -> none  [per_device(): lax.psum((jnp.dot(queries, pooled.T, precision=highest), flops_part), 'vo...]
    psum x1 -> x0, waiting for transfers between devices: 64.3 us -> none  [per_device(): totals = lax.psum(local_sums, 'seq')]
    ppermute x0 -> x8, waiting for transfers between devices: none -> 27.4 us  [butterfly(): lax.ppermute(a, ax, [(i, i ^ d) for i in range(n)])]
    ppermute x0 -> x8, starting transfers between devices: none -> 16.8 us  [butterfly(): lax.ppermute(a, ax, [(i, i ^ d) for i in range(n)])]
  transfers between devices with their start and end apart: 3 -> 11, of which waited for: 3 -> 11; matrix products, arithmetic and copies ran while one was open for 0% -> 1% of each run, Pallas kernels for 0% -> 0%
where the time goes in v1:
time: 263 us
  waiting for transfers between devices  199 us (76%)
  matrix products  26.8 us (10%)
  starting transfers between devices  16.9 us (6%)
  between operations  15.2 us (6%)
  other arithmetic  4.5 us (2%)
    all_gather x1, waiting for transfers between devices, per_device(): full_head = lax.all_gather(head_weight, SEQ, axis=0, tiled=True)  91.6 us
    reduce_scatter x1, waiting for transfers between devices, per_device(): lax.psum_scatter(partial, 'vz', scatter_dimension=0, tiled=True)  56.4 us
    ppermute x8, waiting for transfers between devices, butterfly(): lax.ppermute(a, ax, [(i, i ^ d) for i in range(n)])  27.4 us
    reduce_scatter x1, waiting for transfers between devices, per_device(): lax.psum_scatter(lax.psum_scatter(partial, 'vz', scatter_dimension=0, til...  22.4 us
    ppermute x8, starting transfers between devices, butterfly(): lax.ppermute(a, ax, [(i, i ^ d) for i in range(n)])  16.8 us
    dot_general x1, matrix products, per_device(): lax.dot_general(full_head, dlogits, (((1,), (1,)), ((), ())), preferred_e...  12.6 us
    dot_general x1, matrix products, per_device(): logits = jnp.dot(hidden, full_head, preferred_element_type=jnp.float32)  8.11 us
  transfers between devices with their start and end apart: 11, of which 11 were waited for; matrix products, arithmetic and copies ran while one was open for 1% of the time, Pallas kernels for 0%

profile of v1, /device:TPU:2, one launch (start us, length us, event | category | flops | bytes accessed | tf_op | source)
XLA Modules:
  0.0 262.7 jit_solution(11981062270143876375)
XLA Ops:
  7.2 0.0 copy-start
  7.2 0.0 copy-start.3
  7.2 0.0 all-gather.2.cloned.1.call-start
  7.2 0.7 all-gather.2.cloned.1.call-update
  7.9 0.0 reduce-scatter.3.cloned.1.call-start
  8.0 0.0 copy-done.3
  8.0 0.1 copy.9
  8.1 0.1 reduce-window.8
  8.1 0.1 reduce
  8.3 91.6 %all-gather.2.cloned.1.call-done = bf16[4096,2048]{1,0:T(8,128)(2,1)} async-done(((bf16[512,2048]{1,0:T(8,128)(2,1)}), bf16[4096,2048]{1,0:T(8,128)(2,1)}) %all-gather.2.cloned.1.call-update) | async-done | bytes 16777232 | tf_op jit(solution)/shard_map/all_gather | solution.py:57
  99.9 0.0 copy-done
  99.9 8.1 %fusion.33 = f32[256,2048]{1,0:T(8,128)S(1)} fusion(bf16[256,4096]{1,0:T(8,128)(2,1)S(1)} %copy-done, bf16[4096,2048]{1,0:T(8,128)(2,1)} %all-gather.2.cloned.1.call-done), kind=kOutput, calls=%fused_computation.56 | convolution fusion | flops 4294967296 | bytes 20971520 | tf_op jit(solution)/shard_map/dot_general | solution.py:58
  108.0 0.0 copy-start.5
  108.0 0.0 copy-start.2
  108.0 0.0 copy-start.1
  108.1 1.2 fusion.3
  109.3 0.0 copy-start.4
  109.3 0.3 collective-permute-start
  109.6 1.3 collective-permute-done
  110.9 1.0 collective-permute-start.1
  111.9 7.6 %collective-permute-done.1 = f32[32,2048]{1,0:T(8,128)S(1)} collective-permute-done((f32[32,2048]{1,0:T(8,128)S(1)}, f32[32,2048]{1,0:T(8,128)S(1)}, u32[]{:S(2)}, u32[]{:S(2)}) %collective-permute-start.1) | collective-permute-done | bytes 262176 | tf_op jit(solution)/shard_map/ppermute | solution.py:23
  119.5 0.0 copy-done.5
  119.5 1.0 collective-permute-start.2
  120.6 8.2 %collective-permute-done.2 = f32[32,2048]{1,0:T(8,128)S(1)} collective-permute-done((f32[32,2048]{1,0:T(8,128)S(1)}, f32[32,2048]{1,0:T(8,128)S(1)}, u32[]{:S(2)}, u32[]{:S(2)}) %collective-permute-start.2) | collective-permute-done | bytes 262176 | tf_op jit(solution)/shard_map/ppermute | solution.py:23
  128.7 0.1 fusion.8
  128.8 0.0 copy-done.2
  128.9 0.6 fusion.17
  130.1 0.0 copy-done.1
  130.2 0.4 convolution_bitcast_fusion.1
  130.5 0.1 pad_maximum_fusion
  130.6 1.6 collective-permute-start.3
  132.1 2.2 collective-permute-done.3
  134.4 3.0 %collective-permute-start.4 = (f32[17,32]{1,0:T(8,128)S(1)}, f32[17,32]{1,0:T(8,128)S(1)}, u32[]{:S(2)}, u32[]{:S(2)}) collective-permute-start(f32[17,32]{1,0:T(8,128)S(1)} %fusion.32), channel_id=1, source_target_pairs={{0,2},{1,3},{2,0},{3,1},{4,6},{5,7},{6,4},{7,5},{8,10},{9,11},{10,... | collective-permute-start | bytes 6536 | tf_op jit(solution)/shard_map/ppermute | solution.py:23
  137.4 2.2 collective-permute-done.4
  139.6 1.6 collective-permute-start.5
  141.1 2.1 collective-permute-done.5
  143.3 2.5 collective-permute-start.6
  145.8 2.1 collective-permute-done.6
  147.9 5.7 %collective-permute-start.7 = (f32[17,32]{1,0:T(8,128)S(1)}, f32[17,32]{1,0:T(8,128)S(1)}, u32[]{:S(2)}, u32[]{:S(2)}) collective-permute-start(f32[17,32]{1,0:T(8,128)S(1)} %add.77), channel_id=1, source_target_pairs={{0,16},{4,20},{8,24},{12,28},{16,0},{20,4},{24,8},{28,12},{1,17},{... | collective-permute-start | bytes 6536 | tf_op jit(solution)/shard_map/ppermute | solution.py:23
  153.6 1.9 collective-permute-done.7
  155.5 0.0 copy-done.4
  155.5 0.4 fusion.2
  156.0 4.2 %fusion.1 = bf16[256,2048]{1,0:T(8,128)(2,1)} fusion(f32[32,2048]{1,0:T(8,128)S(1)} %fusion.2, f32[256,2048]{1,0:T(8,128)} %copy-done.5, s32[256]{0:T(256)S(1)} %iota_add_fusion, s32[32]{0:T(128)S(1)} %reduce, s32[32]{0:T(128)S(1)} %sub.25), kind=kOutput, calls=%fused_computation.5 | convolution fusion | flops 206594048 | bytes 3409152 | tf_op jit(solution)/shard_map/dot_general | solution.py:79
  160.1 12.6 %convolution_bitcast_fusion = f32[4096,256]{0,1:T(8,128)} fusion(bf16[256,2048]{1,0:T(8,128)(2,1)} %fusion.1, bf16[4096,2048]{1,0:T(8,128)(2,1)} %all-gather.2.cloned.1.call-done), kind=kOutput, calls=%fused_computation | convolution fusion | flops 4294967296 | bytes 22020096 | tf_op jit(solution)/shard_map/dot_general | solution.py:82
  172.7 0.0 reduce-scatter.3.cloned.1.call-update
  172.7 0.0 reduce-scatter.5.cloned.1.call-start
  172.7 56.4 %reduce-scatter.3.cloned.1.call-done = f32[512,256]{0,1:T(8,128)} async-done(((f32[4096,256]{0,1:T(8,128)}), f32[512,256]{0,1:T(8,128)}) %reduce-scatter.3.cloned.1.call-update) | async-done | bytes 524304 | tf_op jit(solution)/shard_map/reduce_scatter | solution.py:86
  229.2 0.0 reduce-scatter.5.cloned.1.call-update
  229.2 0.5 slice.9
  229.7 0.6 subtract_reduce_fusion
  231.0 1.2 pad_maximum_fusion.1
  232.2 22.4 %reduce-scatter.5.cloned.1.call-done = f32[128,256]{0,1:T(8,128)} async-done(((f32[512,256]{0,1:T(8,128)}), f32[128,256]{0,1:T(8,128)}) %reduce-scatter.5.cloned.1.call-update) | async-done | bytes 131088 | tf_op jit(solution)/shard_map/reduce_scatter | solution.py:85
  254.6 1.5 convert_bitcast_fusion
  (13 shorter events, 0.2 us)
Async XLA Ops:
  7.2 92.7 %copy-start = (bf16[256,4096]{1,0:T(8,128)(2,1)S(1)}, bf16[256,4096]{1,0:T(8,128)(2,1)}, u32[]{:S(2)}) copy-start(bf16[256,4096]{1,0:T(8,128)(2,1)} %param.6) | copy-start | bytes 6291460
  7.2 0.8 copy-start.3
  7.2 92.7 %all-gather.2.cloned.1.call-start = ((), (), s32[]{:S(2)}) async-start(), calls=%async_computation.2 | async-start | bytes 18874368 | tf_op jit(solution)/shard_map/all_gather | solution.py:57
  7.9 221.3 %reduce-scatter.3.cloned.1.call-start = ((), (), s32[]{:S(2)}) async-start(), calls=%async_computation.3 | async-start | bytes 4718592 | tf_op jit(solution)/shard_map/reduce_scatter | solution.py:86
  108.0 11.5 %copy-start.5 = (f32[256,2048]{1,0:T(8,128)}, f32[256,2048]{1,0:T(8,128)S(1)}, u32[]{:S(2)}) copy-start(f32[256,2048]{1,0:T(8,128)S(1)} %fusion.33) | copy-start | bytes 6291460
  108.0 20.8 %copy-start.2 = (s32[2048]{0:T(1024)S(1)}, s32[2048]{0:T(1024)}, u32[]{:S(2)}) copy-start(s32[2048]{0:T(1024)} %param.11) | copy-start | bytes 24580
  108.0 22.1 %copy-start.1 = (f32[16,2048]{1,0:T(8,128)S(1)}, f32[16,2048]{1,0:T(8,128)}, u32[]{:S(2)}) copy-start(f32[16,2048]{1,0:T(8,128)} %param.8) | copy-start | bytes 393220
  109.3 46.2 %copy-start.4 = (s32[32]{0:T(128)S(1)}, s32[32]{0:T(128)}, u32[]{:S(2)}) copy-start(s32[32]{0:T(128)} %param.10) | copy-start | bytes 388
  109.3 1.6 collective-permute-start
  110.9 8.5 %collective-permute-start.1 = (f32[32,2048]{1,0:T(8,128)S(1)}, f32[32,2048]{1,0:T(8,128)S(1)}, u32[]{:S(2)}, u32[]{:S(2)}) collective-permute-start(f32[32,2048]{1,0:T(8,128)S(1)} %add.69), channel_id=1, source_target_pairs={{0,64},{64,0},{128,192},{192,128},{1,65},{65,1},{129,193},{193,129... | collective-permute-start | bytes 786440 | tf_op jit(solution)/shard_map/ppermute | solution.py:23
  119.5 9.2 %collective-permute-start.2 = (f32[32,2048]{1,0:T(8,128)S(1)}, f32[32,2048]{1,0:T(8,128)S(1)}, u32[]{:S(2)}, u32[]{:S(2)}) collective-permute-start(f32[32,2048]{1,0:T(8,128)S(1)} %add.70), channel_id=1, source_target_pairs={{0,128},{64,192},{128,0},{192,64},{1,129},{65,193},{129,1},{193,65... | collective-permute-start | bytes 786440 | tf_op jit(solution)/shard_map/ppermute | solution.py:23
  130.6 3.8 %collective-permute-start.3 = (f32[17,32]{1,0:T(8,128)S(1)}, f32[17,32]{1,0:T(8,128)S(1)}, u32[]{:S(2)}, u32[]{:S(2)}) collective-permute-start(f32[17,32]{1,0:T(8,128)S(1)} %pad_maximum_fusion), channel_id=1, source_target_pairs={{0,1},{1,0},{2,3},{3,2},{4,5},{5,4},{6,7},{7,6},{8,9},{9,8},{10,11... | collective-permute-start | bytes 6536 | tf_op jit(solution)/shard_map/ppermute | solution.py:23
  134.4 5.2 %collective-permute-start.4 = (f32[17,32]{1,0:T(8,128)S(1)}, f32[17,32]{1,0:T(8,128)S(1)}, u32[]{:S(2)}, u32[]{:S(2)}) collective-permute-start(f32[17,32]{1,0:T(8,128)S(1)} %fusion.32), channel_id=1, source_target_pairs={{0,2},{1,3},{2,0},{3,1},{4,6},{5,7},{6,4},{7,5},{8,10},{9,11},{10,... | collective-permute-start | bytes 6536 | tf_op jit(solution)/shard_map/ppermute | solution.py:23
  139.6 3.7 %collective-permute-start.5 = (f32[17,32]{1,0:T(8,128)S(1)}, f32[17,32]{1,0:T(8,128)S(1)}, u32[]{:S(2)}, u32[]{:S(2)}) collective-permute-start(f32[17,32]{1,0:T(8,128)S(1)} %add.75), channel_id=1, source_target_pairs={{0,4},{4,0},{8,12},{12,8},{16,20},{20,16},{24,28},{28,24},{1,5},{5... | collective-permute-start | bytes 6536 | tf_op jit(solution)/shard_map/ppermute | solution.py:23
  143.3 4.6 %collective-permute-start.6 = (f32[17,32]{1,0:T(8,128)S(1)}, f32[17,32]{1,0:T(8,128)S(1)}, u32[]{:S(2)}, u32[]{:S(2)}) collective-permute-start(f32[17,32]{1,0:T(8,128)S(1)} %add.76), channel_id=1, source_target_pairs={{0,8},{4,12},{8,0},{12,4},{16,24},{20,28},{24,16},{28,20},{1,9},{5... | collective-permute-start | bytes 6536 | tf_op jit(solution)/shard_map/ppermute | solution.py:23
  147.9 7.6 %collective-permute-start.7 = (f32[17,32]{1,0:T(8,128)S(1)}, f32[17,32]{1,0:T(8,128)S(1)}, u32[]{:S(2)}, u32[]{:S(2)}) collective-permute-start(f32[17,32]{1,0:T(8,128)S(1)} %add.77), channel_id=1, source_target_pairs={{0,16},{4,20},{8,24},{12,28},{16,0},{20,4},{24,8},{28,12},{1,17},{... | collective-permute-start | bytes 6536 | tf_op jit(solution)/shard_map/ppermute | solution.py:23
  172.7 81.9 %reduce-scatter.5.cloned.1.call-start = ((), (), s32[]{:S(2)}) async-start(), calls=%async_computation.4 | async-start | bytes 655360 | tf_op jit(solution)/shard_map/reduce_scatter | solution.py:85
Sparse Core Ops, SparseCore 0:
  9.9 89.9 all-gather.1
  172.8 56.3 reduce-scatter.2
  231.7 22.8 reduce-scatter.4

commit v2 on v1

--- a/solution.py
+++ b/solution.py
@@ -23,6 +23,19 @@
                 lambda a: a + lax.ppermute(a, ax, [(i, i ^ d) for i in range(n)]), x
             )
             d *= 2
+    return x
+
+
+def halving_scatter(x, ax, n):
+    me = lax.axis_index(ax)
+    d = n // 2
+    while d >= 1:
+        h = x.shape[0] // 2
+        bit = (me // d) % 2
+        keep = lax.dynamic_slice_in_dim(x, bit * h, h, 0)
+        send = lax.dynamic_slice_in_dim(x, (1 - bit) * h, h, 0)
+        x = keep + lax.ppermute(send, ax, [(i, i ^ d) for i in range(n)])
+        d //= 2
     return x
 
 
@@ -82,11 +95,8 @@
     partial = lax.dot_general(
         full_head, dlogits, (((1,), (1,)), ((), ())), preferred_element_type=jnp.float32
     )
-    grad_cols = lax.psum_scatter(
-        lax.psum_scatter(partial, "vz", scatter_dimension=0, tiled=True),
-        "vy",
-        scatter_dimension=0,
-        tiled=True,
+    grad_cols = halving_scatter(
+        lax.psum_scatter(partial, "vz", scatter_dimension=0, tiled=True), "vy", n_vy
     )
     losses = jnp.stack([contrast, flops_value])
     return (grad_cols.T.astype(jnp.bfloat16), losses)

time: 263 us -> 250 us (0.951)
  waiting for transfers between devices: 199 us -> 183 us
  starting transfers between devices: 16.9 us -> 21.5 us
  matrix products: 26.8 us -> 23.5 us
    reduce_scatter x1 -> x0, waiting for transfers between devices: 22.4 us -> none  [per_device(): lax.psum_scatter(lax.psum_scatter(partial, 'vz', scatter_dimension=0, til...]
    ppermute x0 -> x2, waiting for transfers between devices: none -> 6.97 us  [halving_scatter(): x = keep + lax.ppermute(send, ax, [(i, i ^ d) for i in range(n)])]
    ppermute x0 -> x2, starting transfers between devices: none -> 4.68 us  [halving_scatter(): x = keep + lax.ppermute(send, ax, [(i, i ^ d) for i in range(n)])]
  transfers between devices with their start and end apart: 11 -> 12, of which waited for: 11 -> 12; matrix products, arithmetic and copies ran while one was open for 1% -> 1% of each run, Pallas kernels for 0% -> 0%
where the time goes in v2:
time: 250 us
  waiting for transfers between devices  183 us (73%)
  matrix products  23.5 us (9%)
  starting transfers between devices  21.5 us (9%)
  between operations  15.6 us (6%)
  other arithmetic  4.59 us (2%)
    all_gather x1, waiting for transfers between devices, per_device(): full_head = lax.all_gather(head_weight, SEQ, axis=0, tiled=True)  91.6 us
    reduce_scatter x1, waiting for transfers between devices, per_device(): lax.psum_scatter(partial, 'vz', scatter_dimension=0, tiled=True)  56.4 us
    ppermute x8, waiting for transfers between devices, butterfly(): lax.ppermute(a, ax, [(i, i ^ d) for i in range(n)])  27.5 us
    ppermute x8, starting transfers between devices, butterfly(): lax.ppermute(a, ax, [(i, i ^ d) for i in range(n)])  16.8 us
    dot_general x1, matrix products, per_device(): lax.dot_general(full_head, dlogits, (((1,), (1,)), ((), ())), preferred_e...  10.2 us
    dot_general x1, matrix products, per_device(): logits = jnp.dot(hidden, full_head, preferred_element_type=jnp.float32)  8.11 us
    ppermute x2, waiting for transfers between devices, halving_scatter(): x = keep + lax.ppermute(send, ax, [(i, i ^ d) for i in range(n)])  6.97 us
  transfers between devices with their start and end apart: 12, of which 12 were waited for; matrix products, arithmetic and copies ran while one was open for 1% of the time, Pallas kernels for 0%

profile of v2, /device:TPU:2, one launch (start us, length us, event | category | flops | bytes accessed | tf_op | source)
XLA Modules:
  0.0 250.0 jit_solution(2995127937940913010)
XLA Ops:
  7.2 0.0 copy-start
  7.2 0.0 copy-start.3
  7.2 0.0 all-gather.2.cloned.1.call-start
  7.2 0.7 all-gather.2.cloned.1.call-update
  7.9 0.0 reduce-scatter.2.cloned.1.call-start
  8.0 0.0 copy-done.3
  8.0 0.1 copy.9
  8.1 0.1 reduce-window.8
  8.1 0.1 reduce
  8.3 91.6 %all-gather.2.cloned.1.call-done = bf16[4096,2048]{1,0:T(8,128)(2,1)} async-done(((bf16[512,2048]{1,0:T(8,128)(2,1)}), bf16[4096,2048]{1,0:T(8,128)(2,1)}) %all-gather.2.cloned.1.call-update) | async-done | bytes 16777232 | tf_op jit(solution)/shard_map/all_gather | solution.py:70
  99.9 0.0 copy-done
  99.9 8.1 %fusion.34 = f32[256,2048]{1,0:T(8,128)S(1)} fusion(bf16[256,4096]{1,0:T(8,128)(2,1)S(1)} %copy-done, bf16[4096,2048]{1,0:T(8,128)(2,1)} %all-gather.2.cloned.1.call-done), kind=kOutput, calls=%fused_computation.60 | convolution fusion | flops 4294967296 | bytes 20971520 | tf_op jit(solution)/shard_map/dot_general | solution.py:71
  108.0 0.0 copy-start.5
  108.0 0.0 copy-start.2
  108.0 0.0 copy-start.1
  108.1 1.2 fusion.3
  109.3 0.0 copy-start.4
  109.3 0.3 collective-permute-start
  109.6 1.3 collective-permute-done
  110.9 1.0 collective-permute-start.1
  111.9 7.5 %collective-permute-done.1 = f32[32,2048]{1,0:T(8,128)S(1)} collective-permute-done((f32[32,2048]{1,0:T(8,128)S(1)}, f32[32,2048]{1,0:T(8,128)S(1)}, u32[]{:S(2)}, u32[]{:S(2)}) %collective-permute-start.1) | collective-permute-done | bytes 262176 | tf_op jit(solution)/shard_map/ppermute | solution.py:23
  119.5 0.0 copy-done.5
  119.5 1.0 collective-permute-start.2
  120.6 8.2 %collective-permute-done.2 = f32[32,2048]{1,0:T(8,128)S(1)} collective-permute-done((f32[32,2048]{1,0:T(8,128)S(1)}, f32[32,2048]{1,0:T(8,128)S(1)}, u32[]{:S(2)}, u32[]{:S(2)}) %collective-permute-start.2) | collective-permute-done | bytes 262176 | tf_op jit(solution)/shard_map/ppermute | solution.py:23
  128.7 0.1 fusion.8
  128.9 0.0 copy-done.2
  128.9 0.6 fusion.18
  130.1 0.0 copy-done.1
  130.2 0.4 convolution_bitcast_fusion.1
  130.5 0.1 pad_maximum_fusion
  130.6 1.6 collective-permute-start.3
  132.1 2.2 collective-permute-done.3
  134.4 3.0 %collective-permute-start.4 = (f32[17,32]{1,0:T(8,128)S(1)}, f32[17,32]{1,0:T(8,128)S(1)}, u32[]{:S(2)}, u32[]{:S(2)}) collective-permute-start(f32[17,32]{1,0:T(8,128)S(1)} %fusion.33), channel_id=1, source_target_pairs={{0,2},{1,3},{2,0},{3,1},{4,6},{5,7},{6,4},{7,5},{8,10},{9,11},{10,... | collective-permute-start | bytes 6536 | tf_op jit(solution)/shard_map/ppermute | solution.py:23
  137.4 2.2 collective-permute-done.4
  139.6 1.5 collective-permute-start.5
  141.1 2.1 collective-permute-done.5
  143.3 2.5 %collective-permute-start.6 = (f32[17,32]{1,0:T(8,128)S(1)}, f32[17,32]{1,0:T(8,128)S(1)}, u32[]{:S(2)}, u32[]{:S(2)}) collective-permute-start(f32[17,32]{1,0:T(8,128)S(1)} %add.101), channel_id=1, source_target_pairs={{0,8},{4,12},{8,0},{12,4},{16,24},{20,28},{24,16},{28,20},{1,9},{5... | collective-permute-start | bytes 6536 | tf_op jit(solution)/shard_map/ppermute | solution.py:23
  145.8 2.1 collective-permute-done.6
  147.9 5.7 %collective-permute-start.7 = (f32[17,32]{1,0:T(8,128)S(1)}, f32[17,32]{1,0:T(8,128)S(1)}, u32[]{:S(2)}, u32[]{:S(2)}) collective-permute-start(f32[17,32]{1,0:T(8,128)S(1)} %add.102), channel_id=1, source_target_pairs={{0,16},{4,20},{8,24},{12,28},{16,0},{20,4},{24,8},{28,12},{1,17},{... | collective-permute-start | bytes 6536 | tf_op jit(solution)/shard_map/ppermute | solution.py:23
  153.6 1.9 collective-permute-done.7
  155.5 0.0 copy-done.4
  155.5 0.4 fusion.2
  156.0 3.2 %fusion.1 = bf16[256,2048]{1,0:T(8,128)(2,1)S(1)} fusion(f32[32,2048]{1,0:T(8,128)S(1)} %fusion.2, f32[256,2048]{1,0:T(8,128)} %copy-done.5, s32[256]{0:T(256)S(1)} %iota_add_fusion, s32[32]{0:T(128)S(1)} %reduce, s32[32]{0:T(128)S(1)} %sub.36), kind=kOutput, calls=%fused_computation.5 | convolution fusion | flops 206594048 | bytes 3409152 | tf_op jit(solution)/shard_map/dot_general | solution.py:92
  159.2 10.2 %convolution_bitcast_fusion = f32[4096,256]{0,1:T(8,128)} fusion(bf16[256,2048]{1,0:T(8,128)(2,1)S(1)} %fusion.1, bf16[4096,2048]{1,0:T(8,128)(2,1)} %all-gather.2.cloned.1.call-done), kind=kOutput, calls=%fused_computation | convolution fusion | flops 4294967296 | bytes 22020096 | tf_op jit(solution)/shard_map/dot_general | solution.py:95
  169.3 0.0 reduce-scatter.2.cloned.1.call-update
  169.4 56.4 %reduce-scatter.2.cloned.1.call-done = f32[512,256]{0,1:T(8,128)} async-done(((f32[4096,256]{0,1:T(8,128)}), f32[512,256]{0,1:T(8,128)}) %reduce-scatter.2.cloned.1.call-update) | async-done | bytes 524304 | tf_op jit(solution)/shard_map/reduce_scatter | solution.py:99
  225.8 1.0 constant_dynamic-slice_fusion.1
  226.8 3.1 %collective-permute-start.8 = (f32[256,256]{0,1:T(8,128)S(1)}, f32[256,256]{0,1:T(8,128)S(1)}, u32[]{:S(2)}, u32[]{:S(2)}) collective-permute-start(f32[256,256]{0,1:T(8,128)S(1)} %constant_dynamic-slice_fusion.1), channel_id=1, source_target_pairs={{0,2},{1,3},{2,0},{3,1},{4,6},{5,7},{6,4},{7,5},{8,10},{9,11},{10,... | collective-permute-start | bytes 786440 | tf_op jit(solution)/shard_map/ppermute | solution.py:37
  229.9 6.5 %collective-permute-done.8 = f32[256,256]{0,1:T(8,128)S(1)} collective-permute-done((f32[256,256]{0,1:T(8,128)S(1)}, f32[256,256]{0,1:T(8,128)S(1)}, u32[]{:S(2)}, u32[]{:S(2)}) %collective-permute-start.8) | collective-permute-done | bytes 262176 | tf_op jit(solution)/shard_map/ppermute | solution.py:37
  236.4 1.0 dynamic-slice_add_fusion
  237.4 1.6 collective-permute-start.9
  239.0 0.6 subtract_reduce_fusion
  239.6 0.5 slice.9
  240.7 1.2 pad_maximum_fusion.1
  242.0 0.5 collective-permute-done.9
  242.5 0.6 fusion.11
  (14 shorter events, 0.2 us)
Async XLA Ops:
  7.2 92.7 %copy-start = (bf16[256,4096]{1,0:T(8,128)(2,1)S(1)}, bf16[256,4096]{1,0:T(8,128)(2,1)}, u32[]{:S(2)}) copy-start(bf16[256,4096]{1,0:T(8,128)(2,1)} %param.6) | copy-start | bytes 6291460
  7.2 0.8 copy-start.3
  7.2 92.7 %all-gather.2.cloned.1.call-start = ((), (), s32[]{:S(2)}) async-start(), calls=%async_computation.1 | async-start | bytes 18874368 | tf_op jit(solution)/shard_map/all_gather | solution.py:70
  7.9 217.9 %reduce-scatter.2.cloned.1.call-start = ((), (), s32[]{:S(2)}) async-start(), calls=%async_computation.2 | async-start | bytes 4718592 | tf_op jit(solution)/shard_map/reduce_scatter | solution.py:99
  108.0 11.5 %copy-start.5 = (f32[256,2048]{1,0:T(8,128)}, f32[256,2048]{1,0:T(8,128)S(1)}, u32[]{:S(2)}) copy-start(f32[256,2048]{1,0:T(8,128)S(1)} %fusion.34) | copy-start | bytes 6291460
  108.0 20.8 %copy-start.2 = (s32[2048]{0:T(1024)S(1)}, s32[2048]{0:T(1024)}, u32[]{:S(2)}) copy-start(s32[2048]{0:T(1024)} %param.11) | copy-start | bytes 24580
  108.0 22.1 %copy-start.1 = (f32[16,2048]{1,0:T(8,128)S(1)}, f32[16,2048]{1,0:T(8,128)}, u32[]{:S(2)}) copy-start(f32[16,2048]{1,0:T(8,128)} %param.8) | copy-start | bytes 393220
  109.3 46.2 %copy-start.4 = (s32[32]{0:T(128)S(1)}, s32[32]{0:T(128)}, u32[]{:S(2)}) copy-start(s32[32]{0:T(128)} %param.10) | copy-start | bytes 388
  109.3 1.6 collective-permute-start
  110.9 8.6 %collective-permute-start.1 = (f32[32,2048]{1,0:T(8,128)S(1)}, f32[32,2048]{1,0:T(8,128)S(1)}, u32[]{:S(2)}, u32[]{:S(2)}) collective-permute-start(f32[32,2048]{1,0:T(8,128)S(1)} %add.94), channel_id=1, source_target_pairs={{0,64},{64,0},{128,192},{192,128},{1,65},{65,1},{129,193},{193,129... | collective-permute-start | bytes 786440 | tf_op jit(solution)/shard_map/ppermute | solution.py:23
  119.5 9.2 %collective-permute-start.2 = (f32[32,2048]{1,0:T(8,128)S(1)}, f32[32,2048]{1,0:T(8,128)S(1)}, u32[]{:S(2)}, u32[]{:S(2)}) collective-permute-start(f32[32,2048]{1,0:T(8,128)S(1)} %add.95), channel_id=1, source_target_pairs={{0,128},{64,192},{128,0},{192,64},{1,129},{65,193},{129,1},{193,65... | collective-permute-start | bytes 786440 | tf_op jit(solution)/shard_map/ppermute | solution.py:23
  130.6 3.8 %collective-permute-start.3 = (f32[17,32]{1,0:T(8,128)S(1)}, f32[17,32]{1,0:T(8,128)S(1)}, u32[]{:S(2)}, u32[]{:S(2)}) collective-permute-start(f32[17,32]{1,0:T(8,128)S(1)} %pad_maximum_fusion), channel_id=1, source_target_pairs={{0,1},{1,0},{2,3},{3,2},{4,5},{5,4},{6,7},{7,6},{8,9},{9,8},{10,11... | collective-permute-start | bytes 6536 | tf_op jit(solution)/shard_map/ppermute | solution.py:23
  134.4 5.2 %collective-permute-start.4 = (f32[17,32]{1,0:T(8,128)S(1)}, f32[17,32]{1,0:T(8,128)S(1)}, u32[]{:S(2)}, u32[]{:S(2)}) collective-permute-start(f32[17,32]{1,0:T(8,128)S(1)} %fusion.33), channel_id=1, source_target_pairs={{0,2},{1,3},{2,0},{3,1},{4,6},{5,7},{6,4},{7,5},{8,10},{9,11},{10,... | collective-permute-start | bytes 6536 | tf_op jit(solution)/shard_map/ppermute | solution.py:23
  139.6 3.7 %collective-permute-start.5 = (f32[17,32]{1,0:T(8,128)S(1)}, f32[17,32]{1,0:T(8,128)S(1)}, u32[]{:S(2)}, u32[]{:S(2)}) collective-permute-start(f32[17,32]{1,0:T(8,128)S(1)} %add.100), channel_id=1, source_target_pairs={{0,4},{4,0},{8,12},{12,8},{16,20},{20,16},{24,28},{28,24},{1,5},{5... | collective-permute-start | bytes 6536 | tf_op jit(solution)/shard_map/ppermute | solution.py:23
  143.3 4.6 %collective-permute-start.6 = (f32[17,32]{1,0:T(8,128)S(1)}, f32[17,32]{1,0:T(8,128)S(1)}, u32[]{:S(2)}, u32[]{:S(2)}) collective-permute-start(f32[17,32]{1,0:T(8,128)S(1)} %add.101), channel_id=1, source_target_pairs={{0,8},{4,12},{8,0},{12,4},{16,24},{20,28},{24,16},{28,20},{1,9},{5... | collective-permute-start | bytes 6536 | tf_op jit(solution)/shard_map/ppermute | solution.py:23
  147.9 7.6 %collective-permute-start.7 = (f32[17,32]{1,0:T(8,128)S(1)}, f32[17,32]{1,0:T(8,128)S(1)}, u32[]{:S(2)}, u32[]{:S(2)}) collective-permute-start(f32[17,32]{1,0:T(8,128)S(1)} %add.102), channel_id=1, source_target_pairs={{0,16},{4,20},{8,24},{12,28},{16,0},{20,4},{24,8},{28,12},{1,17},{... | collective-permute-start | bytes 6536 | tf_op jit(solution)/shard_map/ppermute | solution.py:23
  226.8 9.6 %collective-permute-start.8 = (f32[256,256]{0,1:T(8,128)S(1)}, f32[256,256]{0,1:T(8,128)S(1)}, u32[]{:S(2)}, u32[]{:S(2)}) collective-permute-start(f32[256,256]{0,1:T(8,128)S(1)} %constant_dynamic-slice_fusion.1), channel_id=1, source_target_pairs={{0,2},{1,3},{2,0},{3,1},{4,6},{5,7},{6,4},{7,5},{8,10},{9,11},{10,... | collective-permute-start | bytes 786440 | tf_op jit(solution)/shard_map/ppermute | solution.py:37
  237.4 5.1 %collective-permute-start.9 = (f32[128,256]{0,1:T(8,128)S(1)}, f32[128,256]{0,1:T(8,128)S(1)}, u32[]{:S(2)}, u32[]{:S(2)}) collective-permute-start(f32[128,256]{0,1:T(8,128)S(1)} %constant_dynamic-slice_fusion), channel_id=1, source_target_pairs={{0,1},{1,0},{2,3},{3,2},{4,5},{5,4},{6,7},{7,6},{8,9},{9,8},{10,11... | collective-permute-start | bytes 393224 | tf_op jit(solution)/shard_map/ppermute | solution.py:37
Sparse Core Ops, SparseCore 0:
  9.9 89.9 all-gather.1
  169.5 56.3 reduce-scatter.1

commit v3 on v2

--- a/solution.py
+++ b/solution.py
@@ -13,6 +13,7 @@
 
 SEQ = ("sx", "sc")
 VOC = ("vz", "vy")
+GROUPS = 2
 
 
 def butterfly(x, axes_sizes):
@@ -92,12 +93,21 @@
     spread = lax.dot_general(member, factor, (((0,), (0,)), ((), ())), precision=highest)
     seventh = fourth * squared * lifted
     dlogits = jnp.where(logits > 0, spread * seventh, 0.0).astype(jnp.bfloat16)
-    partial = lax.dot_general(
-        full_head, dlogits, (((1,), (1,)), ((), ())), preferred_element_type=jnp.float32
-    )
-    grad_cols = halving_scatter(
-        lax.psum_scatter(partial, "vz", scatter_dimension=0, tiled=True), "vy", n_vy
-    )
+    n_out = n_vz * n_vy
+    width = full_head.shape[0] // n_out
+    grouped = full_head.reshape(n_out, GROUPS, width // GROUPS, vocab_cols)
+    pieces = []
+    for g in range(GROUPS):
+        rows = grouped[:, g].reshape(-1, vocab_cols)
+        partial = lax.dot_general(
+            rows, dlogits, (((1,), (1,)), ((), ())), preferred_element_type=jnp.float32
+        )
+        pieces.append(
+            halving_scatter(
+                lax.psum_scatter(partial, "vz", scatter_dimension=0, tiled=True), "vy", n_vy
+            )
+        )
+    grad_cols = jnp.concatenate(pieces, axis=0)
     losses = jnp.stack([contrast, flops_value])
     return (grad_cols.T.astype(jnp.bfloat16), losses)
 

time: 250 us -> 276 us (1.10)
  local copies, waits for them, and re-layouts: 1.62 us -> 13.5 us
  waiting for transfers between devices: 183 us -> 191 us
  starting transfers between devices: 21.5 us -> 26.5 us
    reduce_scatter x1 -> x2, waiting for transfers between devices: 56.4 us -> 68.5 us  [per_device(): lax.psum_scatter(partial, 'vz', scatter_dimension=0, tiled=True)]
    slice x0 -> x1, local copies, waits for them, and re-layouts: none -> 9.88 us  [per_device(): rows = grouped[:, g].reshape(-1, vocab_cols)]
    ppermute x2 -> x4, starting transfers between devices: 4.68 us -> 9.57 us  [halving_scatter(): x = keep + lax.ppermute(send, ax, [(i, i ^ d) for i in range(n)])]
    ppermute x2 -> x4, waiting for transfers between devices: 6.97 us -> 4.85 us  [halving_scatter(): x = keep + lax.ppermute(send, ax, [(i, i ^ d) for i in range(n)])]
    dot_general x1 -> x2, matrix products: 10.2 us -> 11.1 us  [per_device(): lax.dot_general(rows, dlogits, (((1,), (1,)), ((), ())), preferred_elemen...]
  transfers between devices with their start and end apart: 12 -> 15, of which waited for: 12 -> 12; matrix products, arithmetic and copies ran while one was open for 1% -> 9% of each run, Pallas kernels for 0% -> 0%
where the time goes in v3:
time: 276 us; the launch traced here: 275 us
  waiting for transfers between devices  191 us (69%)
  starting transfers between devices  26.5 us (10%)
  matrix products  22.8 us (8%)
  between operations  15.3 us (6%)
  local copies, waits for them, and re-layouts  13.5 us (5%)
  other arithmetic  5.72 us (2%)
    all_gather x1, waiting for transfers between devices, per_device(): full_head = lax.all_gather(head_weight, SEQ, axis=0, tiled=True)  91.6 us
    reduce_scatter x2, waiting for transfers between devices, per_device(): lax.psum_scatter(partial, 'vz', scatter_dimension=0, tiled=True)  68.5 us
    ppermute x8, waiting for transfers between devices, butterfly(): lax.ppermute(a, ax, [(i, i ^ d) for i in range(n)])  25.6 us
    ppermute x8, starting transfers between devices, butterfly(): lax.ppermute(a, ax, [(i, i ^ d) for i in range(n)])  16.8 us
    dot_general x2, matrix products, per_device(): lax.dot_general(rows, dlogits, (((1,), (1,)), ((), ())), preferred_elemen...  11.1 us
    slice x1, local copies, waits for them, and re-layouts, per_device(): rows = grouped[:, g].reshape(-1, vocab_cols)  9.88 us
    ppermute x4, starting transfers between devices, halving_scatter(): x = keep + lax.ppermute(send, ax, [(i, i ^ d) for i in range(n)])  9.57 us
    dot_general x1, matrix products, per_device(): logits = jnp.dot(hidden, full_head, preferred_element_type=jnp.float32)  8.11 us
  transfers between devices with their start and end apart: 15, of which 12 were waited for; matrix products, arithmetic and copies ran while one was open for 9% of the time, Pallas kernels for 0%

profile of v3, /device:TPU:2, one launch (start us, length us, event | category | flops | bytes accessed | tf_op | source)
XLA Modules:
  0.0 275.1 jit_solution(13790768649974117661)
XLA Ops:
  7.2 0.0 copy-start
  7.2 0.0 all-gather.2.cloned.1.call-start
  7.2 0.7 all-gather.2.cloned.1.call-update
  7.9 0.0 reduce-scatter.5.cloned.1.call-start
  8.0 0.0 copy-done.3
  8.0 0.1 copy.9
  8.1 0.1 reduce-window.8
  8.1 0.1 reduce
  8.3 91.6 %all-gather.2.cloned.1.call-done = bf16[4096,2048]{1,0:T(8,128)(2,1)} async-done(((bf16[512,2048]{1,0:T(8,128)(2,1)}), bf16[4096,2048]{1,0:T(8,128)(2,1)}) %all-gather.2.cloned.1.call-update) | async-done | bytes 16777232 | tf_op jit(solution)/shard_map/all_gather | solution.py:71
  99.9 8.1 %fusion.34 = f32[256,2048]{1,0:T(8,128)S(1)} fusion(bf16[256,4096]{1,0:T(8,128)(2,1)S(1)} %copy-done, bf16[4096,2048]{1,0:T(8,128)(2,1)} %all-gather.2.cloned.1.call-done), kind=kOutput, calls=%fused_computation.66 | convolution fusion | flops 4294967296 | bytes 20971520 | tf_op jit(solution)/shard_map/dot_general | solution.py:72
  108.0 0.0 copy-start.2
  108.0 0.0 copy-start.1
  108.1 1.2 fusion.3
  109.3 0.3 collective-permute-start
  109.6 1.3 collective-permute-done
  110.9 1.0 collective-permute-start.1
  111.9 7.6 %collective-permute-done.1 = f32[32,2048]{1,0:T(8,128)S(1)} collective-permute-done((f32[32,2048]{1,0:T(8,128)S(1)}, f32[32,2048]{1,0:T(8,128)S(1)}, u32[]{:S(2)}, u32[]{:S(2)}) %collective-permute-start.1) | collective-permute-done | bytes 262176 | tf_op jit(solution)/shard_map/ppermute | solution.py:24
  119.5 1.0 collective-permute-start.2
  120.6 8.2 %collective-permute-done.2 = f32[32,2048]{1,0:T(8,128)S(1)} collective-permute-done((f32[32,2048]{1,0:T(8,128)S(1)}, f32[32,2048]{1,0:T(8,128)S(1)}, u32[]{:S(2)}, u32[]{:S(2)}) %collective-permute-start.2) | collective-permute-done | bytes 262176 | tf_op jit(solution)/shard_map/ppermute | solution.py:24
  128.7 0.1 fusion.8
  128.8 0.6 fusion.17
  130.1 0.4 convolution_bitcast_fusion.2
  130.5 0.1 pad_maximum_fusion
  130.6 1.6 collective-permute-start.3
  132.1 2.2 collective-permute-done.3
  134.3 3.0 %collective-permute-start.4 = (f32[17,32]{1,0:T(8,128)S(1)}, f32[17,32]{1,0:T(8,128)S(1)}, u32[]{:S(2)}, u32[]{:S(2)}) collective-permute-start(f32[17,32]{1,0:T(8,128)S(1)} %fusion.32), channel_id=1, source_target_pairs={{0,2},{1,3},{2,0},{3,1},{4,6},{5,7},{6,4},{7,5},{8,10},{9,11},{10,... | collective-permute-start | bytes 6536 | tf_op jit(solution)/shard_map/ppermute | solution.py:24
  137.4 2.2 collective-permute-done.4
  139.5 1.6 collective-permute-start.5
  141.1 2.1 collective-permute-done.5
  143.2 2.5 collective-permute-start.6
  145.8 2.1 collective-permute-done.6
  147.8 5.7 %collective-permute-start.7 = (f32[17,32]{1,0:T(8,128)S(1)}, f32[17,32]{1,0:T(8,128)S(1)}, u32[]{:S(2)}, u32[]{:S(2)}) collective-permute-start(f32[17,32]{1,0:T(8,128)S(1)} %add.116), channel_id=1, source_target_pairs={{0,16},{4,20},{8,24},{12,28},{16,0},{20,4},{24,8},{28,12},{1,17},{... | collective-permute-start | bytes 6536 | tf_op jit(solution)/shard_map/ppermute | solution.py:24
  153.6 9.9 %fusion.33 = (bf16[32,1,64,2048]{3,2,1,0:T(8,128)(2,1)}, bf16[32,1,64,2048]{3,2,1,0:T(8,128)(2,1)S(1)}) fusion(bf16[32,2,64,2048]{3,2,1,0:T(8,128)(2,1)} %bitcast.23), kind=kLoop, calls=%fused_computation.65 | loop fusion | bytes 33554432 | tf_op jit(solution)/shard_map/slice | solution.py:101
  163.5 0.0 collective-permute-done.7
  163.5 0.4 fusion.2
  164.0 1.6 fusion.1
  165.7 1.0 copy-done.7
  166.6 3.7 %convolution_bitcast_fusion = f32[2048,256]{0,1:T(8,128)} fusion(bf16[256,2048]{1,0:T(8,128)(2,1)S(1)} %fusion.1, bf16[2048,2048]{1,0:T(8,128)(2,1)S(1)} %bitcast.25), kind=kOutput, calls=%fused_computation.2 | convolution fusion | flops 2147483648 | bytes 11534336 | tf_op jit(solution)/shard_map/dot_general | solution.py:102
  170.3 0.0 reduce-scatter.5.cloned.1.call-update
  170.3 0.0 reduce-scatter.3.cloned.1.call-start
  170.4 7.4 %convolution_bitcast_fusion.1 = f32[2048,256]{0,1:T(8,128)} fusion(bf16[256,2048]{1,0:T(8,128)(2,1)} %copy-done.7, bf16[2048,2048]{1,0:T(8,128)(2,1)} %bitcast.24), kind=kOutput, calls=%fused_computation.3 | convolution fusion | flops 2147483648 | bytes 11534336 | tf_op jit(solution)/shard_map/dot_general | solution.py:102
  177.8 0.0 reduce-scatter.3.cloned.1.call-update
  177.9 0.5 slice.19
  178.4 0.6 subtract_reduce_fusion
  179.6 29.8 %reduce-scatter.5.cloned.1.call-done = f32[256,256]{0,1:T(8,128)} async-done(((f32[2048,256]{0,1:T(8,128)}), f32[256,256]{0,1:T(8,128)}) %reduce-scatter.5.cloned.1.call-update) | async-done | bytes 262160 | tf_op jit(solution)/shard_map/reduce_scatter | solution.py:107
  209.4 0.9 constant_dynamic-slice_fusion.1
  210.3 3.1 %collective-permute-start.10 = (f32[128,256]{0,1:T(8,128)S(1)}, f32[128,256]{0,1:T(8,128)S(1)}, u32[]{:S(2)}, u32[]{:S(2)}) collective-permute-start(f32[128,256]{0,1:T(8,128)S(1)} %constant_dynamic-slice_fusion.1), channel_id=1, source_target_pairs={{0,2},{1,3},{2,0},{3,1},{4,6},{5,7},{6,4},{7,5},{8,10},{9,11},{10,... | collective-permute-start | bytes 393224 | tf_op jit(solution)/shard_map/ppermute | solution.py:38
  213.4 1.2 pad_maximum_fusion.1
  214.6 38.7 %reduce-scatter.3.cloned.1.call-done = f32[256,256]{0,1:T(8,128)} async-done(((f32[2048,256]{0,1:T(8,128)}), f32[256,256]{0,1:T(8,128)}) %reduce-scatter.3.cloned.1.call-update) | async-done | bytes 262160 | tf_op jit(solution)/shard_map/reduce_scatter | solution.py:107
  253.3 0.9 constant_dynamic-slice_fusion.3
  254.3 3.2 %collective-permute-start.8 = (f32[128,256]{0,1:T(8,128)S(1)}, f32[128,256]{0,1:T(8,128)S(1)}, u32[]{:S(2)}, u32[]{:S(2)}) collective-permute-start(f32[128,256]{0,1:T(8,128)S(1)} %constant_dynamic-slice_fusion.3), channel_id=1, source_target_pairs={{0,2},{1,3},{2,0},{3,1},{4,6},{5,7},{6,4},{7,5},{8,10},{9,11},{10,... | collective-permute-start | bytes 393224 | tf_op jit(solution)/shard_map/ppermute | solution.py:38
  257.4 0.0 collective-permute-done.10
  257.4 0.9 dynamic-slice_add_fusion
  258.3 0.1 constant_dynamic-slice_fusion
  258.4 0.4 collective-permute-start.11
  258.8 2.0 collective-permute-done.8
  260.8 0.9 dynamic-slice_add_fusion.1
  261.7 0.1 constant_dynamic-slice_fusion.2
  261.8 3.0 %collective-permute-start.9 = (f32[64,256]{0,1:T(8,128)S(1)}, f32[64,256]{0,1:T(8,128)S(1)}, u32[]{:S(2)}, u32[]{:S(2)}) collective-permute-start(f32[64,256]{0,1:T(8,128)S(1)} %constant_dynamic-slice_fusion.2), channel_id=1, source_target_pairs={{0,1},{1,0},{2,3},{3,2},{4,5},{5,4},{6,7},{7,6},{8,9},{9,8},{10,11... | collective-permute-start | bytes 196616 | tf_op jit(solution)/shard_map/ppermute | solution.py:38
  264.8 0.0 collective-permute-done.11
  264.8 0.1 add_convert_fusion
  264.9 2.8 %collective-permute-done.9 = f32[64,256]{0,1:T(8,128)S(1)} collective-permute-done((f32[64,256]{0,1:T(8,128)S(1)}, f32[64,256]{0,1:T(8,128)S(1)}, u32[]{:S(2)}, u32[]{:S(2)}) %collective-permute-start.9) | collective-permute-done | bytes 65568 | tf_op jit(solution)/shard_map/ppermute | solution.py:38
  267.8 0.1 add_convert_fusion.1
  267.9 0.7 maximum_bitcast_fusion
  (24 shorter events, 0.2 us)
Async XLA Ops:
  7.2 92.7 %copy-start = (bf16[256,4096]{1,0:T(8,128)(2,1)S(1)}, bf16[256,4096]{1,0:T(8,128)(2,1)}, u32[]{:S(2)}) copy-start(bf16[256,4096]{1,0:T(8,128)(2,1)} %param.6) | copy-start | bytes 6291460
  7.2 0.8 copy-start.3
  7.2 92.7 %all-gather.2.cloned.1.call-start = ((), (), s32[]{:S(2)}) async-start(), calls=%async_computation.2 | async-start | bytes 18874368 | tf_op jit(solution)/shard_map/all_gather | solution.py:71
  7.9 201.5 %reduce-scatter.5.cloned.1.call-start = ((), (), s32[]{:S(2)}) async-start(), calls=%async_computation.4 | async-start | bytes 2359296 | tf_op jit(solution)/shard_map/reduce_scatter | solution.py:107
  108.0 11.5 %copy-start.5 = (f32[256,2048]{1,0:T(8,128)}, f32[256,2048]{1,0:T(8,128)S(1)}, u32[]{:S(2)}) copy-start(f32[256,2048]{1,0:T(8,128)S(1)} %fusion.34) | copy-start | bytes 6291460
  108.0 20.8 %copy-start.2 = (s32[2048]{0:T(1024)S(1)}, s32[2048]{0:T(1024)}, u32[]{:S(2)}) copy-start(s32[2048]{0:T(1024)} %param.11) | copy-start | bytes 24580
  108.0 22.1 %copy-start.1 = (f32[16,2048]{1,0:T(8,128)S(1)}, f32[16,2048]{1,0:T(8,128)}, u32[]{:S(2)}) copy-start(f32[16,2048]{1,0:T(8,128)} %param.8) | copy-start | bytes 393220
  109.3 1.6 collective-permute-start
  110.9 8.5 %collective-permute-start.1 = (f32[32,2048]{1,0:T(8,128)S(1)}, f32[32,2048]{1,0:T(8,128)S(1)}, u32[]{:S(2)}, u32[]{:S(2)}) collective-permute-start(f32[32,2048]{1,0:T(8,128)S(1)} %add.108), channel_id=1, source_target_pairs={{0,64},{64,0},{128,192},{192,128},{1,65},{65,1},{129,193},{193,129... | collective-permute-start | bytes 786440 | tf_op jit(solution)/shard_map/ppermute | solution.py:24
  119.5 9.2 %collective-permute-start.2 = (f32[32,2048]{1,0:T(8,128)S(1)}, f32[32,2048]{1,0:T(8,128)S(1)}, u32[]{:S(2)}, u32[]{:S(2)}) collective-permute-start(f32[32,2048]{1,0:T(8,128)S(1)} %add.109), channel_id=1, source_target_pairs={{0,128},{64,192},{128,0},{192,64},{1,129},{65,193},{129,1},{193,65... | collective-permute-start | bytes 786440 | tf_op jit(solution)/shard_map/ppermute | solution.py:24
  130.6 3.8 %collective-permute-start.3 = (f32[17,32]{1,0:T(8,128)S(1)}, f32[17,32]{1,0:T(8,128)S(1)}, u32[]{:S(2)}, u32[]{:S(2)}) collective-permute-start(f32[17,32]{1,0:T(8,128)S(1)} %pad_maximum_fusion), channel_id=1, source_target_pairs={{0,1},{1,0},{2,3},{3,2},{4,5},{5,4},{6,7},{7,6},{8,9},{9,8},{10,11... | collective-permute-start | bytes 6536 | tf_op jit(solution)/shard_map/ppermute | solution.py:24
  134.3 5.2 %collective-permute-start.4 = (f32[17,32]{1,0:T(8,128)S(1)}, f32[17,32]{1,0:T(8,128)S(1)}, u32[]{:S(2)}, u32[]{:S(2)}) collective-permute-start(f32[17,32]{1,0:T(8,128)S(1)} %fusion.32), channel_id=1, source_target_pairs={{0,2},{1,3},{2,0},{3,1},{4,6},{5,7},{6,4},{7,5},{8,10},{9,11},{10,... | collective-permute-start | bytes 6536 | tf_op jit(solution)/shard_map/ppermute | solution.py:24
  139.5 3.7 %collective-permute-start.5 = (f32[17,32]{1,0:T(8,128)S(1)}, f32[17,32]{1,0:T(8,128)S(1)}, u32[]{:S(2)}, u32[]{:S(2)}) collective-permute-start(f32[17,32]{1,0:T(8,128)S(1)} %add.114), channel_id=1, source_target_pairs={{0,4},{4,0},{8,12},{12,8},{16,20},{20,16},{24,28},{28,24},{1,5},{5... | collective-permute-start | bytes 6536 | tf_op jit(solution)/shard_map/ppermute | solution.py:24
  143.2 4.6 %collective-permute-start.6 = (f32[17,32]{1,0:T(8,128)S(1)}, f32[17,32]{1,0:T(8,128)S(1)}, u32[]{:S(2)}, u32[]{:S(2)}) collective-permute-start(f32[17,32]{1,0:T(8,128)S(1)} %add.115), channel_id=1, source_target_pairs={{0,8},{4,12},{8,0},{12,4},{16,24},{20,28},{24,16},{28,20},{1,9},{5... | collective-permute-start | bytes 6536 | tf_op jit(solution)/shard_map/ppermute | solution.py:24
  147.8 15.6 %collective-permute-start.7 = (f32[17,32]{1,0:T(8,128)S(1)}, f32[17,32]{1,0:T(8,128)S(1)}, u32[]{:S(2)}, u32[]{:S(2)}) collective-permute-start(f32[17,32]{1,0:T(8,128)S(1)} %add.116), channel_id=1, source_target_pairs={{0,16},{4,20},{8,24},{12,28},{16,0},{20,4},{24,8},{28,12},{1,17},{... | collective-permute-start | bytes 6536 | tf_op jit(solution)/shard_map/ppermute | solution.py:24
  153.6 9.9 %copy-start.4 = (s32[32]{0:T(128)S(1)}, s32[32]{0:T(128)}, u32[]{:S(2)}) copy-start(s32[32]{0:T(128)} %param.10) | copy-start | bytes 388
  153.6 10.4 %copy-start.6 = (f32[256,2048]{1,0:T(8,128)S(1)}, f32[256,2048]{1,0:T(8,128)}, u32[]{:S(2)}) copy-start(f32[256,2048]{1,0:T(8,128)} %copy-done.5) | copy-start | bytes 6291460
  165.6 1.0 copy-start.7
  170.3 83.0 %reduce-scatter.3.cloned.1.call-start = ((), (), s32[]{:S(2)}) async-start(), calls=%async_computation.3 | async-start | bytes 2359296 | tf_op jit(solution)/shard_map/reduce_scatter | solution.py:107
  210.3 47.1 %collective-permute-start.10 = (f32[128,256]{0,1:T(8,128)S(1)}, f32[128,256]{0,1:T(8,128)S(1)}, u32[]{:S(2)}, u32[]{:S(2)}) collective-permute-start(f32[128,256]{0,1:T(8,128)S(1)} %constant_dynamic-slice_fusion.1), channel_id=1, source_target_pairs={{0,2},{1,3},{2,0},{3,1},{4,6},{5,7},{6,4},{7,5},{8,10},{9,11},{10,... | collective-permute-start | bytes 393224 | tf_op jit(solution)/shard_map/ppermute | solution.py:38
  254.3 6.6 %collective-permute-start.8 = (f32[128,256]{0,1:T(8,128)S(1)}, f32[128,256]{0,1:T(8,128)S(1)}, u32[]{:S(2)}, u32[]{:S(2)}) collective-permute-start(f32[128,256]{0,1:T(8,128)S(1)} %constant_dynamic-slice_fusion.3), channel_id=1, source_target_pairs={{0,2},{1,3},{2,0},{3,1},{4,6},{5,7},{6,4},{7,5},{8,10},{9,11},{10,... | collective-permute-start | bytes 393224 | tf_op jit(solution)/shard_map/ppermute | solution.py:38
  258.4 6.4 %collective-permute-start.11 = (f32[64,256]{0,1:T(8,128)S(1)}, f32[64,256]{0,1:T(8,128)S(1)}, u32[]{:S(2)}, u32[]{:S(2)}) collective-permute-start(f32[64,256]{0,1:T(8,128)S(1)} %constant_dynamic-slice_fusion), channel_id=1, source_target_pairs={{0,1},{1,0},{2,3},{3,2},{4,5},{5,4},{6,7},{7,6},{8,9},{9,8},{10,11... | collective-permute-start | bytes 196616 | tf_op jit(solution)/shard_map/ppermute | solution.py:38
  261.8 5.9 %collective-permute-start.9 = (f32[64,256]{0,1:T(8,128)S(1)}, f32[64,256]{0,1:T(8,128)S(1)}, u32[]{:S(2)}, u32[]{:S(2)}) collective-permute-start(f32[64,256]{0,1:T(8,128)S(1)} %constant_dynamic-slice_fusion.2), channel_id=1, source_target_pairs={{0,1},{1,0},{2,3},{3,2},{4,5},{5,4},{6,7},{7,6},{8,9},{9,8},{10,11... | collective-permute-start | bytes 196616 | tf_op jit(solution)/shard_map/ppermute | solution.py:38
Sparse Core Ops, SparseCore 0:
  9.9 89.9 all-gather.1
  170.5 38.8 reduce-scatter.4
  212.0 41.3 reduce-scatter.2

commit v4 on v2

--- a/solution.py
+++ b/solution.py
@@ -74,7 +74,18 @@
     fourth = squared * squared
     powered = fourth * fourth
     local_sums = jnp.dot(member, powered, precision=highest)
-    totals = butterfly(local_sums, [("sc", n_sc), ("sx", n_sx)])
+    chip_sums = butterfly(local_sums, [("sc", n_sc)])
+    core = lax.axis_index("sc")
+    half_cols = vocab_cols // n_sc
+    mine = butterfly(
+        lax.dynamic_slice_in_dim(chip_sums, core * half_cols, half_cols, 1), [("sx", n_sx)]
+    )
+    theirs = lax.ppermute(mine, "sc", [(0, 1), (1, 0)])
+    totals = jnp.where(
+        core == 0,
+        jnp.concatenate([mine, theirs], axis=1),
+        jnp.concatenate([theirs, mine], axis=1),
+    )
     pooled = (jnp.log(totals) - jnp.log(counts)[:, None]) / sharpness
     col_mean = jnp.sum(pooled, axis=0) / passages
     flops_part = jnp.sum(weights_df * col_mean * col_mean) / vocab_total

time: 250 us -> 246 us (0.984)
  waiting for transfers between devices: 183 us -> 179 us
    ppermute x8, waiting for transfers between devices: 27.5 us -> 21.8 us  [butterfly(): lax.ppermute(a, ax, [(i, i ^ d) for i in range(n)])]
  transfers between devices with their start and end apart: 12 -> 13, of which waited for: 12 -> 13; matrix products, arithmetic and copies ran while one was open for 1% -> 1% of each run, Pallas kernels for 0% -> 0%
where the time goes in v4:
time: 246 us
  waiting for transfers between devices  179 us (73%)
  starting transfers between devices  21.9 us (9%)
  matrix products  21.9 us (9%)
  between operations  15.6 us (6%)
  other arithmetic  4.57 us (2%)
  local copies, waits for them, and re-layouts  2.96 us (1%)
    all_gather x1, waiting for transfers between devices, per_device(): full_head = lax.all_gather(head_weight, SEQ, axis=0, tiled=True)  91.6 us
    reduce_scatter x1, waiting for transfers between devices, per_device(): lax.psum_scatter(partial, 'vz', scatter_dimension=0, tiled=True)  56.6 us
    ppermute x8, waiting for transfers between devices, butterfly(): lax.ppermute(a, ax, [(i, i ^ d) for i in range(n)])  21.8 us
    ppermute x8, starting transfers between devices, butterfly(): lax.ppermute(a, ax, [(i, i ^ d) for i in range(n)])  17.1 us
    dot_general x1, matrix products, per_device(): lax.dot_general(full_head, dlogits, (((1,), (1,)), ((), ())), preferred_e...  10.2 us
    dot_general x1, matrix products, per_device(): logits = jnp.dot(hidden, full_head, preferred_element_type=jnp.float32)  8.11 us
    ppermute x2, waiting for transfers between devices, halving_scatter(): x = keep + lax.ppermute(send, ax, [(i, i ^ d) for i in range(n)])  6.96 us
  transfers between devices with their start and end apart: 13, of which 13 were waited for; matrix products, arithmetic and copies ran while one was open for 1% of the time, Pallas kernels for 0%

profile of v4, /device:TPU:2, one launch (start us, length us, event | category | flops | bytes accessed | tf_op | source)
XLA Modules:
  0.0 245.9 jit_solution(7510672723683249618)
XLA Ops:
  7.2 0.0 copy-start
  7.2 0.0 copy-start.2
  7.2 0.0 all-gather.2.cloned.1.call-start
  7.2 0.7 all-gather.2.cloned.1.call-update
  7.9 0.0 reduce-scatter.2.cloned.1.call-start
  8.0 0.0 copy-done.2
  8.0 0.1 copy.9
  8.1 0.1 reduce-window.8
  8.1 0.1 reduce
  8.3 91.6 %all-gather.2.cloned.1.call-done = bf16[4096,2048]{1,0:T(8,128)(2,1)} async-done(((bf16[512,2048]{1,0:T(8,128)(2,1)}), bf16[4096,2048]{1,0:T(8,128)(2,1)}) %all-gather.2.cloned.1.call-update) | async-done | bytes 16777232 | tf_op jit(solution)/shard_map/all_gather | solution.py:70
  99.9 0.0 copy-done
  99.9 8.1 %fusion.35 = f32[256,2048]{1,0:T(8,128)S(1)} fusion(bf16[256,4096]{1,0:T(8,128)(2,1)S(1)} %copy-done, bf16[4096,2048]{1,0:T(8,128)(2,1)} %all-gather.2.cloned.1.call-done), kind=kOutput, calls=%fused_computation.63 | convolution fusion | flops 4294967296 | bytes 20971520 | tf_op jit(solution)/shard_map/dot_general | solution.py:71
  108.0 0.0 copy-start.5
  108.0 1.3 copy-done.5
  109.4 0.0 copy-start.1
  109.4 0.0 copy-start.4
  109.4 0.0 copy-start.3
  109.4 1.2 fusion.3
  110.6 0.3 collective-permute-start
  110.9 1.3 collective-permute-done
  112.2 1.0 collective-permute-start.1
  113.2 4.7 %collective-permute-done.1 = f32[32,1024]{1,0:T(8,128)S(1)} collective-permute-done((f32[32,1024]{1,0:T(8,128)S(1)}, f32[32,1024]{1,0:T(8,128)S(1)}, u32[]{:S(2)}, u32[]{:S(2)}) %collective-permute-start.1) | collective-permute-done | bytes 131104 | tf_op jit(solution)/shard_map/ppermute | solution.py:23
  118.0 1.0 collective-permute-start.2
  119.0 5.5 %collective-permute-done.2 = f32[32,1024]{1,0:T(8,128)S(1)} collective-permute-done((f32[32,1024]{1,0:T(8,128)S(1)}, f32[32,1024]{1,0:T(8,128)S(1)}, u32[]{:S(2)}, u32[]{:S(2)}) %collective-permute-start.2) | collective-permute-done | bytes 131104 | tf_op jit(solution)/shard_map/ppermute | solution.py:23
  124.6 0.1 collective-permute-start.3
  124.7 1.3 collective-permute-done.3
  126.0 0.1 fusion.8
  126.1 0.0 copy-done.1
  126.1 0.6 fusion.18
  127.4 0.0 copy-start.6
  127.4 0.0 copy-done.4
  127.4 0.4 convolution_bitcast_fusion.1
  127.8 0.1 pad_maximum_fusion
  127.8 1.6 collective-permute-start.4
  129.4 2.2 collective-permute-done.4
  131.6 3.0 %collective-permute-start.5 = (f32[17,32]{1,0:T(8,128)S(1)}, f32[17,32]{1,0:T(8,128)S(1)}, u32[]{:S(2)}, u32[]{:S(2)}) collective-permute-start(f32[17,32]{1,0:T(8,128)S(1)} %fusion.34), channel_id=1, source_target_pairs={{0,2},{1,3},{2,0},{3,1},{4,6},{5,7},{6,4},{7,5},{8,10},{9,11},{10,... | collective-permute-start | bytes 6536 | tf_op jit(solution)/shard_map/ppermute | solution.py:23
  134.7 2.2 collective-permute-done.5
  136.8 1.6 collective-permute-start.6
  138.4 2.1 collective-permute-done.6
  140.5 2.5 %collective-permute-start.7 = (f32[17,32]{1,0:T(8,128)S(1)}, f32[17,32]{1,0:T(8,128)S(1)}, u32[]{:S(2)}, u32[]{:S(2)}) collective-permute-start(f32[17,32]{1,0:T(8,128)S(1)} %add.105), channel_id=1, source_target_pairs={{0,8},{4,12},{8,0},{12,4},{16,24},{20,28},{24,16},{28,20},{1,9},{5... | collective-permute-start | bytes 6536 | tf_op jit(solution)/shard_map/ppermute | solution.py:23
  143.1 2.0 collective-permute-done.7
  145.1 6.0 %collective-permute-start.8 = (f32[17,32]{1,0:T(8,128)S(1)}, f32[17,32]{1,0:T(8,128)S(1)}, u32[]{:S(2)}, u32[]{:S(2)}) collective-permute-start(f32[17,32]{1,0:T(8,128)S(1)} %add.106), channel_id=1, source_target_pairs={{0,16},{4,20},{8,24},{12,28},{16,0},{20,4},{24,8},{28,12},{1,17},{... | collective-permute-start | bytes 6536 | tf_op jit(solution)/shard_map/ppermute | solution.py:23
  151.1 1.7 collective-permute-done.8
  152.8 0.0 copy-done.3
  152.9 0.4 fusion.2
  153.3 0.0 copy-done.6
  153.3 1.6 fusion.1
  154.9 10.2 %convolution_bitcast_fusion = f32[4096,256]{0,1:T(8,128)} fusion(bf16[256,2048]{1,0:T(8,128)(2,1)S(1)} %fusion.1, bf16[4096,2048]{1,0:T(8,128)(2,1)} %all-gather.2.cloned.1.call-done), kind=kOutput, calls=%fused_computation | convolution fusion | flops 4294967296 | bytes 22020096 | tf_op jit(solution)/shard_map/dot_general | solution.py:106
  165.1 0.0 reduce-scatter.2.cloned.1.call-update
  165.2 56.6 %reduce-scatter.2.cloned.1.call-done = f32[512,256]{0,1:T(8,128)} async-done(((f32[4096,256]{0,1:T(8,128)}), f32[512,256]{0,1:T(8,128)}) %reduce-scatter.2.cloned.1.call-update) | async-done | bytes 524304 | tf_op jit(solution)/shard_map/reduce_scatter | solution.py:110
  221.8 1.0 constant_dynamic-slice_fusion.1
  222.8 3.1 %collective-permute-start.9 = (f32[256,256]{0,1:T(8,128)S(1)}, f32[256,256]{0,1:T(8,128)S(1)}, u32[]{:S(2)}, u32[]{:S(2)}) collective-permute-start(f32[256,256]{0,1:T(8,128)S(1)} %constant_dynamic-slice_fusion.1), channel_id=1, source_target_pairs={{0,2},{1,3},{2,0},{3,1},{4,6},{5,7},{6,4},{7,5},{8,10},{9,11},{10,... | collective-permute-start | bytes 786440 | tf_op jit(solution)/shard_map/ppermute | solution.py:37
  225.9 6.5 %collective-permute-done.9 = f32[256,256]{0,1:T(8,128)S(1)} collective-permute-done((f32[256,256]{0,1:T(8,128)S(1)}, f32[256,256]{0,1:T(8,128)S(1)}, u32[]{:S(2)}, u32[]{:S(2)}) %collective-permute-start.9) | collective-permute-done | bytes 262176 | tf_op jit(solution)/shard_map/ppermute | solution.py:37
  232.3 1.0 dynamic-slice_add_fusion
  233.4 1.6 collective-permute-start.10
  234.9 0.6 subtract_reduce_fusion
  235.5 0.5 slice.9
  236.7 1.2 pad_maximum_fusion.1
  237.9 0.5 collective-permute-done.10
  238.4 0.6 fusion.11
  (15 shorter events, 0.2 us)
Async XLA Ops:
  7.2 92.7 %copy-start = (bf16[256,4096]{1,0:T(8,128)(2,1)S(1)}, bf16[256,4096]{1,0:T(8,128)(2,1)}, u32[]{:S(2)}) copy-start(bf16[256,4096]{1,0:T(8,128)(2,1)} %param.6) | copy-start | bytes 6291460
  7.2 0.8 copy-start.2
  7.2 92.7 %all-gather.2.cloned.1.call-start = ((), (), s32[]{:S(2)}) async-start(), calls=%async_computation.1 | async-start | bytes 18874368 | tf_op jit(solution)/shard_map/all_gather | solution.py:70
  7.9 213.9 %reduce-scatter.2.cloned.1.call-start = ((), (), s32[]{:S(2)}) async-start(), calls=%async_computation.2 | async-start | bytes 4718592 | tf_op jit(solution)/shard_map/reduce_scatter | solution.py:110
  108.0 1.4 copy-start.5
  109.4 16.7 %copy-start.1 = (s32[2048]{0:T(1024)S(1)}, s32[2048]{0:T(1024)}, u32[]{:S(2)}) copy-start(s32[2048]{0:T(1024)} %param.11) | copy-start | bytes 24580
  109.4 18.0 %copy-start.4 = (f32[16,2048]{1,0:T(8,128)S(1)}, f32[16,2048]{1,0:T(8,128)}, u32[]{:S(2)}) copy-start(f32[16,2048]{1,0:T(8,128)} %param.8) | copy-start | bytes 393220
  109.4 43.5 %copy-start.3 = (s32[32]{0:T(128)S(1)}, s32[32]{0:T(128)}, u32[]{:S(2)}) copy-start(s32[32]{0:T(128)} %param.10) | copy-start | bytes 388
  110.6 1.6 collective-permute-start
  112.2 5.7 %collective-permute-start.1 = (f32[32,1024]{1,0:T(8,128)S(1)}, f32[32,1024]{1,0:T(8,128)S(1)}, u32[]{:S(2)}, u32[]{:S(2)}) collective-permute-start(f32[32,1024]{1,0:T(8,128)S(1)} %dynamic-slice_add_fusion.1), channel_id=1, source_target_pairs={{0,64},{64,0},{128,192},{192,128},{1,65},{65,1},{129,193},{193,129... | collective-permute-start | bytes 393224 | tf_op jit(solution)/shard_map/ppermute | solution.py:23
  118.0 6.6 %collective-permute-start.2 = (f32[32,1024]{1,0:T(8,128)S(1)}, f32[32,1024]{1,0:T(8,128)S(1)}, u32[]{:S(2)}, u32[]{:S(2)}) collective-permute-start(f32[32,1024]{1,0:T(8,128)S(1)} %add.99), channel_id=1, source_target_pairs={{0,128},{64,192},{128,0},{192,64},{1,129},{65,193},{129,1},{193,65... | collective-permute-start | bytes 393224 | tf_op jit(solution)/shard_map/ppermute | solution.py:23
  124.6 1.4 collective-permute-start.3
  127.4 25.9 %copy-start.6 = (f32[256,2048]{1,0:T(8,128)S(1)}, f32[256,2048]{1,0:T(8,128)}, u32[]{:S(2)}) copy-start(f32[256,2048]{1,0:T(8,128)} %copy-done.5) | copy-start | bytes 6291460
  127.8 3.8 %collective-permute-start.4 = (f32[17,32]{1,0:T(8,128)S(1)}, f32[17,32]{1,0:T(8,128)S(1)}, u32[]{:S(2)}, u32[]{:S(2)}) collective-permute-start(f32[17,32]{1,0:T(8,128)S(1)} %pad_maximum_fusion), channel_id=1, source_target_pairs={{0,1},{1,0},{2,3},{3,2},{4,5},{5,4},{6,7},{7,6},{8,9},{9,8},{10,11... | collective-permute-start | bytes 6536 | tf_op jit(solution)/shard_map/ppermute | solution.py:23
  131.6 5.2 %collective-permute-start.5 = (f32[17,32]{1,0:T(8,128)S(1)}, f32[17,32]{1,0:T(8,128)S(1)}, u32[]{:S(2)}, u32[]{:S(2)}) collective-permute-start(f32[17,32]{1,0:T(8,128)S(1)} %fusion.34), channel_id=1, source_target_pairs={{0,2},{1,3},{2,0},{3,1},{4,6},{5,7},{6,4},{7,5},{8,10},{9,11},{10,... | collective-permute-start | bytes 6536 | tf_op jit(solution)/shard_map/ppermute | solution.py:23
  136.8 3.7 %collective-permute-start.6 = (f32[17,32]{1,0:T(8,128)S(1)}, f32[17,32]{1,0:T(8,128)S(1)}, u32[]{:S(2)}, u32[]{:S(2)}) collective-permute-start(f32[17,32]{1,0:T(8,128)S(1)} %add.104), channel_id=1, source_target_pairs={{0,4},{4,0},{8,12},{12,8},{16,20},{20,16},{24,28},{28,24},{1,5},{5... | collective-permute-start | bytes 6536 | tf_op jit(solution)/shard_map/ppermute | solution.py:23
  140.5 4.6 %collective-permute-start.7 = (f32[17,32]{1,0:T(8,128)S(1)}, f32[17,32]{1,0:T(8,128)S(1)}, u32[]{:S(2)}, u32[]{:S(2)}) collective-permute-start(f32[17,32]{1,0:T(8,128)S(1)} %add.105), channel_id=1, source_target_pairs={{0,8},{4,12},{8,0},{12,4},{16,24},{20,28},{24,16},{28,20},{1,9},{5... | collective-permute-start | bytes 6536 | tf_op jit(solution)/shard_map/ppermute | solution.py:23
  145.1 7.7 %collective-permute-start.8 = (f32[17,32]{1,0:T(8,128)S(1)}, f32[17,32]{1,0:T(8,128)S(1)}, u32[]{:S(2)}, u32[]{:S(2)}) collective-permute-start(f32[17,32]{1,0:T(8,128)S(1)} %add.106), channel_id=1, source_target_pairs={{0,16},{4,20},{8,24},{12,28},{16,0},{20,4},{24,8},{28,12},{1,17},{... | collective-permute-start | bytes 6536 | tf_op jit(solution)/shard_map/ppermute | solution.py:23
  222.8 9.6 %collective-permute-start.9 = (f32[256,256]{0,1:T(8,128)S(1)}, f32[256,256]{0,1:T(8,128)S(1)}, u32[]{:S(2)}, u32[]{:S(2)}) collective-permute-start(f32[256,256]{0,1:T(8,128)S(1)} %constant_dynamic-slice_fusion.1), channel_id=1, source_target_pairs={{0,2},{1,3},{2,0},{3,1},{4,6},{5,7},{6,4},{7,5},{8,10},{9,11},{10,... | collective-permute-start | bytes 786440 | tf_op jit(solution)/shard_map/ppermute | solution.py:37
  233.4 5.1 %collective-permute-start.10 = (f32[128,256]{0,1:T(8,128)S(1)}, f32[128,256]{0,1:T(8,128)S(1)}, u32[]{:S(2)}, u32[]{:S(2)}) collective-permute-start(f32[128,256]{0,1:T(8,128)S(1)} %constant_dynamic-slice_fusion), channel_id=1, source_target_pairs={{0,1},{1,0},{2,3},{3,2},{4,5},{5,4},{6,7},{7,6},{8,9},{9,8},{10,11... | collective-permute-start | bytes 393224 | tf_op jit(solution)/shard_map/ppermute | solution.py:37
Sparse Core Ops, SparseCore 0:
  9.9 89.9 all-gather.1
  165.2 56.5 reduce-scatter.1

commit v5 on v4

--- a/solution.py
+++ b/solution.py
@@ -13,6 +13,7 @@
 
 SEQ = ("sx", "sc")
 VOC = ("vz", "vy")
+SC_ROWS = 96
 
 
 def butterfly(x, axes_sizes):
@@ -106,9 +107,15 @@
     partial = lax.dot_general(
         full_head, dlogits, (((1,), (1,)), ((), ())), preferred_element_type=jnp.float32
     )
-    grad_cols = halving_scatter(
-        lax.psum_scatter(partial, "vz", scatter_dimension=0, tiled=True), "vy", n_vy
+    width = partial.shape[0] // (n_vz * n_vy)
+    blocks = partial.reshape(n_vz, n_vy, width, partial.shape[1])
+    native_part = blocks[:, :, :SC_ROWS].reshape(-1, partial.shape[1])
+    permute_part = blocks[:, :, SC_ROWS:].transpose(1, 0, 2, 3).reshape(-1, partial.shape[1])
+    side = halving_scatter(halving_scatter(permute_part, "vy", n_vy), "vz", n_vz)
+    main = halving_scatter(
+        lax.psum_scatter(native_part, "vz", scatter_dimension=0, tiled=True), "vy", n_vy
     )
+    grad_cols = jnp.concatenate([main, side], axis=0)
     losses = jnp.stack([contrast, flops_value])
     return (grad_cols.T.astype(jnp.bfloat16), losses)
 

time: 246 us -> 256 us (1.041)
  waiting for transfers between devices: 179 us -> 145 us
  local copies, waits for them, and re-layouts: 2.96 us -> 26.3 us
  starting transfers between devices: 21.9 us -> 37.3 us
  matrix products: 21.9 us -> 25.2 us
    reduce_scatter x1, waiting for transfers between devices: 56.6 us -> 5.68 us  [per_device(): lax.psum_scatter(native_part, 'vz', scatter_dimension=0, tiled=True)]
    ppermute x2 -> x7, waiting for transfers between devices: 6.96 us -> 23.5 us  [halving_scatter(): x = keep + lax.ppermute(send, ax, [(i, i ^ d) for i in range(n)])]
    ppermute x2 -> x7, starting transfers between devices: 4.67 us -> 20.1 us  [halving_scatter(): x = keep + lax.ppermute(send, ax, [(i, i ^ d) for i in range(n)])]
    unnamed x14 -> x19, local copies, waits for them, and re-layouts: 1.38 us -> 11.5 us
    slice x0 -> x1, local copies, waits for them, and re-layouts: none -> 6.39 us  [per_device(): blocks[:, :, SC_ROWS:].transpose(1, 0, 2, 3).reshape(-1, partial.shape[1])]
    reshape x0 -> x1, local copies, waits for them, and re-layouts: none -> 6.02 us  [per_device(): blocks = partial.reshape(n_vz, n_vy, width, partial.shape[1])]
  transfers between devices with their start and end apart: 13 -> 18, of which waited for: 13 -> 16; matrix products, arithmetic and copies ran while one was open for 1% -> 7% of each run, Pallas kernels for 0% -> 0%
where the time goes in v5:
time: 256 us; the launch traced here: 255 us
  waiting for transfers between devices  145 us (57%)
  starting transfers between devices  37.3 us (15%)
  local copies, waits for them, and re-layouts  26.3 us (10%)
  matrix products  25.2 us (10%)
  between operations  15.6 us (6%)
  other arithmetic  6.04 us (2%)
    all_gather x1, waiting for transfers between devices, per_device(): full_head = lax.all_gather(head_weight, SEQ, axis=0, tiled=True)  91.6 us
    ppermute x7, waiting for transfers between devices, halving_scatter(): x = keep + lax.ppermute(send, ax, [(i, i ^ d) for i in range(n)])  23.5 us
    ppermute x8, waiting for transfers between devices, butterfly(): lax.ppermute(a, ax, [(i, i ^ d) for i in range(n)])  21.8 us
    ppermute x7, starting transfers between devices, halving_scatter(): x = keep + lax.ppermute(send, ax, [(i, i ^ d) for i in range(n)])  20.1 us
    ppermute x8, starting transfers between devices, butterfly(): lax.ppermute(a, ax, [(i, i ^ d) for i in range(n)])  17.1 us
    dot_general x1, matrix products, per_device(): lax.dot_general(full_head, dlogits, (((1,), (1,)), ((), ())), preferred_e...  12.6 us
    unnamed x19, local copies, waits for them, and re-layouts  11.5 us
    dot_general x1, matrix products, per_device(): logits = jnp.dot(hidden, full_head, preferred_element_type=jnp.float32)  8.11 us
  transfers between devices with their start and end apart: 18, of which 16 were waited for; matrix products, arithmetic and copies ran while one was open for 7% of the time, Pallas kernels for 0%

profile of v5, /device:TPU:2, one launch (start us, length us, event | category | flops | bytes accessed | tf_op | source)
XLA Modules:
  0.0 255.2 jit_solution(9924981513900726814)
XLA Ops:
  7.2 0.0 copy-start
  7.2 0.0 all-gather.2.cloned.1.call-start
  7.2 0.7 all-gather.2.cloned.1.call-update
  7.9 0.0 reduce-scatter.2.cloned.1.call-start
  8.0 0.1 copy.10
  8.1 0.1 reduce-window.8
  8.1 0.1 reduce
  8.3 91.6 %all-gather.2.cloned.1.call-done = bf16[4096,2048]{1,0:T(8,128)(2,1)} async-done(((bf16[512,2048]{1,0:T(8,128)(2,1)}), bf16[4096,2048]{1,0:T(8,128)(2,1)}) %all-gather.2.cloned.1.call-update) | async-done | bytes 16777232 | tf_op jit(solution)/shard_map/all_gather | solution.py:71
  99.9 8.1 %fusion.34 = f32[256,2048]{1,0:T(8,128)S(1)} fusion(bf16[256,4096]{1,0:T(8,128)(2,1)S(1)} %copy-done, bf16[4096,2048]{1,0:T(8,128)(2,1)} %all-gather.2.cloned.1.call-done), kind=kOutput, calls=%fused_computation.73 | convolution fusion | flops 4294967296 | bytes 20971520 | tf_op jit(solution)/shard_map/dot_general | solution.py:72
  108.0 1.3 copy-done.6
  109.4 1.2 fusion.3
  110.6 0.3 collective-permute-start
  110.9 1.3 collective-permute-done
  112.2 1.0 collective-permute-start.1
  113.2 4.7 %collective-permute-done.1 = f32[32,1024]{1,0:T(8,128)S(1)} collective-permute-done((f32[32,1024]{1,0:T(8,128)S(1)}, f32[32,1024]{1,0:T(8,128)S(1)}, u32[]{:S(2)}, u32[]{:S(2)}) %collective-permute-start.1) | collective-permute-done | bytes 131104 | tf_op jit(solution)/shard_map/ppermute | solution.py:24
  118.0 1.0 collective-permute-start.2
  119.0 5.5 %collective-permute-done.2 = f32[32,1024]{1,0:T(8,128)S(1)} collective-permute-done((f32[32,1024]{1,0:T(8,128)S(1)}, f32[32,1024]{1,0:T(8,128)S(1)}, u32[]{:S(2)}, u32[]{:S(2)}) %collective-permute-start.2) | collective-permute-done | bytes 131104 | tf_op jit(solution)/shard_map/ppermute | solution.py:24
  124.6 0.1 collective-permute-start.3
  124.7 1.3 collective-permute-done.3
  126.0 0.1 fusion.8
  126.1 0.6 fusion.17
  127.4 0.4 convolution_bitcast_fusion.1
  127.8 0.1 pad_maximum_fusion
  127.8 1.6 collective-permute-start.4
  129.4 2.2 collective-permute-done.4
  131.6 3.0 %collective-permute-start.5 = (f32[17,32]{1,0:T(8,128)S(1)}, f32[17,32]{1,0:T(8,128)S(1)}, u32[]{:S(2)}, u32[]{:S(2)}) collective-permute-start(f32[17,32]{1,0:T(8,128)S(1)} %fusion.33), channel_id=1, source_target_pairs={{0,2},{1,3},{2,0},{3,1},{4,6},{5,7},{6,4},{7,5},{8,10},{9,11},{10,... | collective-permute-start | bytes 6536 | tf_op jit(solution)/shard_map/ppermute | solution.py:24
  134.6 2.2 collective-permute-done.5
  136.8 1.6 collective-permute-start.6
  138.4 2.1 collective-permute-done.6
  140.5 2.5 collective-permute-start.7
  143.1 2.0 collective-permute-done.7
  145.1 6.0 %collective-permute-start.8 = (f32[17,32]{1,0:T(8,128)S(1)}, f32[17,32]{1,0:T(8,128)S(1)}, u32[]{:S(2)}, u32[]{:S(2)}) collective-permute-start(f32[17,32]{1,0:T(8,128)S(1)} %add.165), channel_id=1, source_target_pairs={{0,16},{4,20},{8,24},{12,28},{16,0},{20,4},{24,8},{28,12},{1,17},{... | collective-permute-start | bytes 6536 | tf_op jit(solution)/shard_map/ppermute | solution.py:24
  151.1 1.7 collective-permute-done.8
  152.9 0.4 fusion.2
  153.3 2.6 %fusion.1 = bf16[256,2048]{1,0:T(8,128)(2,1)} fusion(f32[32,2048]{1,0:T(8,128)S(1)} %fusion.2, f32[256,2048]{1,0:T(8,128)S(1)} %copy-done.7, s32[256]{0:T(256)S(1)} %iota_add_fusion, s32[32]{0:T(128)S(1)} %reduce, s32[32]{0:T(128)S(1)} %sub.56), kind=kOutput, calls=%fused_computation.5 | convolution fusion | flops 206594048 | bytes 3409152 | tf_op jit(solution)/shard_map/dot_general | solution.py:104
  155.9 12.6 %convolution_bitcast_fusion = f32[4096,256]{0,1:T(8,128)} fusion(bf16[256,2048]{1,0:T(8,128)(2,1)} %fusion.1, bf16[4096,2048]{1,0:T(8,128)(2,1)} %all-gather.2.cloned.1.call-done), kind=kOutput, calls=%fused_computation | convolution fusion | flops 4294967296 | bytes 22020096 | tf_op jit(solution)/shard_map/dot_general | solution.py:107
  168.5 6.0 %reshape.57 = f32[8,4,128,256]{2,1,0,3:T(4,128)} reshape(f32[4096,256]{0,1:T(8,128)} %convolution_bitcast_fusion) | data formatting | bytes 8388608 | tf_op jit(solution)/shard_map/reshape | solution.py:111
  174.5 5.1 %copy.14 = f32[8,4,96,256]{3,2,1,0:T(8,128)} copy(f32[8,4,96,256]{2,1,0,3:T(4,128)} %bitcast.23) | data formatting | bytes 6291456
  179.5 0.0 reduce-scatter.2.cloned.1.call-update
  179.6 6.4 %slice.18 = f32[8,4,32,256]{2,1,0,3:T(4,128)} slice(f32[8,4,128,256]{2,1,0,3:T(4,128)} %reshape.57), slice={[0:8], [0:4], [96:128], [0:256]} | slice | bytes 2097152 | tf_op jit(solution)/shard_map/slice | solution.py:113
  186.0 3.5 %copy.15 = f32[8,4,32,256]{3,2,0,1:T(8,128)S(1)} copy(f32[8,4,32,256]{2,1,0,3:T(4,128)} %slice.18) | data formatting | bytes 2097152
  189.5 0.8 constant_dynamic-slice_fusion.4
  190.4 3.0 %collective-permute-start.11 = (f32[512,256]{1,0:T(8,128)}, f32[512,256]{1,0:T(8,128)}, u32[]{:S(2)}, u32[]{:S(2)}) collective-permute-start(f32[512,256]{1,0:T(8,128)} %constant_dynamic-slice_fusion.4), channel_id=1, source_target_pairs={{0,2},{1,3},{2,0},{3,1},{4,6},{5,7},{6,4},{7,5},{8,10},{9,11},{10,... | collective-permute-start | bytes 1572872 | tf_op jit(solution)/shard_map/ppermute | solution.py:38
  193.4 9.1 %collective-permute-done.11 = f32[512,256]{1,0:T(8,128)} collective-permute-done((f32[512,256]{1,0:T(8,128)}, f32[512,256]{1,0:T(8,128)}, u32[]{:S(2)}, u32[]{:S(2)}) %collective-permute-start.11) | collective-permute-done | bytes 524320 | tf_op jit(solution)/shard_map/ppermute | solution.py:38
  202.4 1.1 dynamic-slice_add_fusion
  203.6 0.8 copy-done.1
  204.4 1.6 collective-permute-start.12
  206.0 4.9 %collective-permute-done.12 = f32[256,256]{1,0:T(8,128)S(1)} collective-permute-done((f32[256,256]{1,0:T(8,128)S(1)}, f32[256,256]{1,0:T(8,128)S(1)}, u32[]{:S(2)}, u32[]{:S(2)}) %collective-permute-start.12) | collective-permute-done | bytes 262176 | tf_op jit(solution)/shard_map/ppermute | solution.py:38
  210.8 1.0 dynamic-slice_add_fusion.1
  211.8 6.0 %collective-permute-start.13 = (f32[128,256]{1,0:T(8,128)S(1)}, f32[128,256]{1,0:T(8,128)S(1)}, u32[]{:S(2)}, u32[]{:S(2)}) collective-permute-start(f32[128,256]{1,0:T(8,128)S(1)} %constant_dynamic-slice_fusion.2), channel_id=1, source_target_pairs={{0,16},{4,20},{8,24},{12,28},{16,0},{20,4},{24,8},{28,12},{1,17},{... | collective-permute-start | bytes 393224 | tf_op jit(solution)/shard_map/ppermute | solution.py:38
  217.8 0.6 subtract_reduce_fusion
  218.4 0.5 slice.19
  219.6 1.2 pad_maximum_fusion.1
  220.8 4.1 %collective-permute-done.13 = f32[128,256]{1,0:T(8,128)S(1)} collective-permute-done((f32[128,256]{1,0:T(8,128)S(1)}, f32[128,256]{1,0:T(8,128)S(1)}, u32[]{:S(2)}, u32[]{:S(2)}) %collective-permute-start.13) | collective-permute-done | bytes 131104 | tf_op jit(solution)/shard_map/ppermute | solution.py:38
  225.0 3.0 %collective-permute-start.14 = (f32[64,256]{1,0:T(8,128)S(1)}, f32[64,256]{1,0:T(8,128)S(1)}, u32[]{:S(2)}, u32[]{:S(2)}) collective-permute-start(f32[64,256]{1,0:T(8,128)S(1)} %constant_dynamic-slice_fusion.1), channel_id=1, source_target_pairs={{0,8},{4,12},{8,0},{12,4},{16,24},{20,28},{24,16},{28,20},{1,9},{5... | collective-permute-start | bytes 196616 | tf_op jit(solution)/shard_map/ppermute | solution.py:38
  228.0 5.7 %reduce-scatter.2.cloned.1.call-done = f32[384,256]{1,0:T(8,128)} async-done(((f32[3072,256]{1,0:T(8,128)}), f32[384,256]{1,0:T(8,128)}) %reduce-scatter.2.cloned.1.call-update) | async-done | bytes 393232 | tf_op jit(solution)/shard_map/reduce_scatter | solution.py:116
  233.7 0.9 constant_dynamic-slice_fusion.6
  234.6 3.2 %collective-permute-start.9 = (f32[192,256]{1,0:T(8,128)S(1)}, f32[192,256]{1,0:T(8,128)S(1)}, u32[]{:S(2)}, u32[]{:S(2)}) collective-permute-start(f32[192,256]{1,0:T(8,128)S(1)} %constant_dynamic-slice_fusion.6), channel_id=1, source_target_pairs={{0,2},{1,3},{2,0},{3,1},{4,6},{5,7},{6,4},{7,5},{8,10},{9,11},{10,... | collective-permute-start | bytes 589832 | tf_op jit(solution)/shard_map/ppermute | solution.py:38
  237.8 1.7 collective-permute-start.15
  239.5 2.3 collective-permute-done.9
  241.9 1.0 dynamic-slice_add_fusion.2
  242.9 1.6 collective-permute-start.10
  244.5 3.1 %collective-permute-done.10 = f32[96,256]{1,0:T(8,128)S(1)} collective-permute-done((f32[96,256]{1,0:T(8,128)S(1)}, f32[96,256]{1,0:T(8,128)S(1)}, u32[]{:S(2)}, u32[]{:S(2)}) %collective-permute-start.10) | collective-permute-done | bytes 98336 | tf_op jit(solution)/shard_map/ppermute | solution.py:38
  247.6 0.7 copy.13
  (39 shorter events, 0.3 us)
Async XLA Ops:
  7.2 92.7 %copy-start = (bf16[256,4096]{1,0:T(8,128)(2,1)S(1)}, bf16[256,4096]{1,0:T(8,128)(2,1)}, u32[]{:S(2)}) copy-start(bf16[256,4096]{1,0:T(8,128)(2,1)} %param.6) | copy-start | bytes 6291460
  7.2 0.8 copy-start.3
  7.2 92.7 %all-gather.2.cloned.1.call-start = ((), (), s32[]{:S(2)}) async-start(), calls=%async_computation.1 | async-start | bytes 18874368 | tf_op jit(solution)/shard_map/all_gather | solution.py:71
  7.9 225.7 %reduce-scatter.2.cloned.1.call-start = ((), (), s32[]{:S(2)}) async-start(), calls=%async_computation.2 | async-start | bytes 3538944 | tf_op jit(solution)/shard_map/reduce_scatter | solution.py:116
  108.0 1.3 copy-start.6
  109.4 16.7 %copy-start.2 = (s32[2048]{0:T(1024)S(1)}, s32[2048]{0:T(1024)}, u32[]{:S(2)}) copy-start(s32[2048]{0:T(1024)} %param.11) | copy-start | bytes 24580
  109.4 18.0 %copy-start.5 = (f32[16,2048]{1,0:T(8,128)S(1)}, f32[16,2048]{1,0:T(8,128)}, u32[]{:S(2)}) copy-start(f32[16,2048]{1,0:T(8,128)} %param.8) | copy-start | bytes 393220
  109.4 43.5 %copy-start.4 = (s32[32]{0:T(128)S(1)}, s32[32]{0:T(128)}, u32[]{:S(2)}) copy-start(s32[32]{0:T(128)} %param.10) | copy-start | bytes 388
  110.6 1.6 collective-permute-start
  112.2 5.7 %collective-permute-start.1 = (f32[32,1024]{1,0:T(8,128)S(1)}, f32[32,1024]{1,0:T(8,128)S(1)}, u32[]{:S(2)}, u32[]{:S(2)}) collective-permute-start(f32[32,1024]{1,0:T(8,128)S(1)} %dynamic-slice_add_fusion.3), channel_id=1, source_target_pairs={{0,64},{64,0},{128,192},{192,128},{1,65},{65,1},{129,193},{193,129... | collective-permute-start | bytes 393224 | tf_op jit(solution)/shard_map/ppermute | solution.py:24
  118.0 6.6 %collective-permute-start.2 = (f32[32,1024]{1,0:T(8,128)S(1)}, f32[32,1024]{1,0:T(8,128)S(1)}, u32[]{:S(2)}, u32[]{:S(2)}) collective-permute-start(f32[32,1024]{1,0:T(8,128)S(1)} %add.158), channel_id=1, source_target_pairs={{0,128},{64,192},{128,0},{192,64},{1,129},{65,193},{129,1},{193,65... | collective-permute-start | bytes 393224 | tf_op jit(solution)/shard_map/ppermute | solution.py:24
  124.6 1.4 collective-permute-start.3
  127.4 25.9 %copy-start.7 = (f32[256,2048]{1,0:T(8,128)S(1)}, f32[256,2048]{1,0:T(8,128)}, u32[]{:S(2)}) copy-start(f32[256,2048]{1,0:T(8,128)} %copy-done.6) | copy-start | bytes 6291460
  127.8 3.8 %collective-permute-start.4 = (f32[17,32]{1,0:T(8,128)S(1)}, f32[17,32]{1,0:T(8,128)S(1)}, u32[]{:S(2)}, u32[]{:S(2)}) collective-permute-start(f32[17,32]{1,0:T(8,128)S(1)} %pad_maximum_fusion), channel_id=1, source_target_pairs={{0,1},{1,0},{2,3},{3,2},{4,5},{5,4},{6,7},{7,6},{8,9},{9,8},{10,11... | collective-permute-start | bytes 6536 | tf_op jit(solution)/shard_map/ppermute | solution.py:24
  131.6 5.2 %collective-permute-start.5 = (f32[17,32]{1,0:T(8,128)S(1)}, f32[17,32]{1,0:T(8,128)S(1)}, u32[]{:S(2)}, u32[]{:S(2)}) collective-permute-start(f32[17,32]{1,0:T(8,128)S(1)} %fusion.33), channel_id=1, source_target_pairs={{0,2},{1,3},{2,0},{3,1},{4,6},{5,7},{6,4},{7,5},{8,10},{9,11},{10,... | collective-permute-start | bytes 6536 | tf_op jit(solution)/shard_map/ppermute | solution.py:24
  136.8 3.7 %collective-permute-start.6 = (f32[17,32]{1,0:T(8,128)S(1)}, f32[17,32]{1,0:T(8,128)S(1)}, u32[]{:S(2)}, u32[]{:S(2)}) collective-permute-start(f32[17,32]{1,0:T(8,128)S(1)} %add.163), channel_id=1, source_target_pairs={{0,4},{4,0},{8,12},{12,8},{16,20},{20,16},{24,28},{28,24},{1,5},{5... | collective-permute-start | bytes 6536 | tf_op jit(solution)/shard_map/ppermute | solution.py:24
  140.5 4.6 %collective-permute-start.7 = (f32[17,32]{1,0:T(8,128)S(1)}, f32[17,32]{1,0:T(8,128)S(1)}, u32[]{:S(2)}, u32[]{:S(2)}) collective-permute-start(f32[17,32]{1,0:T(8,128)S(1)} %add.164), channel_id=1, source_target_pairs={{0,8},{4,12},{8,0},{12,4},{16,24},{20,28},{24,16},{28,20},{1,9},{5... | collective-permute-start | bytes 6536 | tf_op jit(solution)/shard_map/ppermute | solution.py:24
  145.1 7.7 %collective-permute-start.8 = (f32[17,32]{1,0:T(8,128)S(1)}, f32[17,32]{1,0:T(8,128)S(1)}, u32[]{:S(2)}, u32[]{:S(2)}) collective-permute-start(f32[17,32]{1,0:T(8,128)S(1)} %add.165), channel_id=1, source_target_pairs={{0,16},{4,20},{8,24},{12,28},{16,0},{20,4},{24,8},{28,12},{1,17},{... | collective-permute-start | bytes 6536 | tf_op jit(solution)/shard_map/ppermute | solution.py:24
  190.4 12.1 %collective-permute-start.11 = (f32[512,256]{1,0:T(8,128)}, f32[512,256]{1,0:T(8,128)}, u32[]{:S(2)}, u32[]{:S(2)}) collective-permute-start(f32[512,256]{1,0:T(8,128)} %constant_dynamic-slice_fusion.4), channel_id=1, source_target_pairs={{0,2},{1,3},{2,0},{3,1},{4,6},{5,7},{6,4},{7,5},{8,10},{9,11},{10,... | collective-permute-start | bytes 1572872 | tf_op jit(solution)/shard_map/ppermute | solution.py:38
  203.6 0.8 copy-start.1
  204.4 6.5 %collective-permute-start.12 = (f32[256,256]{1,0:T(8,128)S(1)}, f32[256,256]{1,0:T(8,128)S(1)}, u32[]{:S(2)}, u32[]{:S(2)}) collective-permute-start(f32[256,256]{1,0:T(8,128)S(1)} %constant_dynamic-slice_fusion.3), channel_id=1, source_target_pairs={{0,1},{1,0},{2,3},{3,2},{4,5},{5,4},{6,7},{7,6},{8,9},{9,8},{10,11... | collective-permute-start | bytes 786440 | tf_op jit(solution)/shard_map/ppermute | solution.py:38
  211.8 13.1 %collective-permute-start.13 = (f32[128,256]{1,0:T(8,128)S(1)}, f32[128,256]{1,0:T(8,128)S(1)}, u32[]{:S(2)}, u32[]{:S(2)}) collective-permute-start(f32[128,256]{1,0:T(8,128)S(1)} %constant_dynamic-slice_fusion.2), channel_id=1, source_target_pairs={{0,16},{4,20},{8,24},{12,28},{16,0},{20,4},{24,8},{28,12},{1,17},{... | collective-permute-start | bytes 393224 | tf_op jit(solution)/shard_map/ppermute | solution.py:38
  225.0 12.8 %collective-permute-start.14 = (f32[64,256]{1,0:T(8,128)S(1)}, f32[64,256]{1,0:T(8,128)S(1)}, u32[]{:S(2)}, u32[]{:S(2)}) collective-permute-start(f32[64,256]{1,0:T(8,128)S(1)} %constant_dynamic-slice_fusion.1), channel_id=1, source_target_pairs={{0,8},{4,12},{8,0},{12,4},{16,24},{20,28},{24,16},{28,20},{1,9},{5... | collective-permute-start | bytes 196616 | tf_op jit(solution)/shard_map/ppermute | solution.py:38
  234.6 7.3 %collective-permute-start.9 = (f32[192,256]{1,0:T(8,128)S(1)}, f32[192,256]{1,0:T(8,128)S(1)}, u32[]{:S(2)}, u32[]{:S(2)}) collective-permute-start(f32[192,256]{1,0:T(8,128)S(1)} %constant_dynamic-slice_fusion.6), channel_id=1, source_target_pairs={{0,2},{1,3},{2,0},{3,1},{4,6},{5,7},{6,4},{7,5},{8,10},{9,11},{10,... | collective-permute-start | bytes 589832 | tf_op jit(solution)/shard_map/ppermute | solution.py:38
  237.8 6.6 %collective-permute-start.15 = (f32[32,256]{1,0:T(8,128)S(1)}, f32[32,256]{1,0:T(8,128)S(1)}, u32[]{:S(2)}, u32[]{:S(2)}) collective-permute-start(f32[32,256]{1,0:T(8,128)S(1)} %constant_dynamic-slice_fusion), channel_id=1, source_target_pairs={{0,4},{4,0},{8,12},{12,8},{16,20},{20,16},{24,28},{28,24},{1,5},{5... | collective-permute-start | bytes 98312 | tf_op jit(solution)/shard_map/ppermute | solution.py:38
  242.9 4.7 %collective-permute-start.10 = (f32[96,256]{1,0:T(8,128)S(1)}, f32[96,256]{1,0:T(8,128)S(1)}, u32[]{:S(2)}, u32[]{:S(2)}) collective-permute-start(f32[96,256]{1,0:T(8,128)S(1)} %constant_dynamic-slice_fusion.5), channel_id=1, source_target_pairs={{0,1},{1,0},{2,3},{3,2},{4,5},{5,4},{6,7},{7,6},{8,9},{9,8},{10,11... | collective-permute-start | bytes 294920 | tf_op jit(solution)/shard_map/ppermute | solution.py:38
Sparse Core Ops, SparseCore 0:
  9.9 89.9 all-gather.1
  179.7 53.9 reduce-scatter.1

commit v6 on v4

--- a/solution.py
+++ b/solution.py
@@ -15,14 +15,21 @@
 VOC = ("vz", "vy")
 
 
+def rounds_of(n):
+    pairs = []
+    d = 1
+    while 2 * d < n:
+        pairs.append([(i, i ^ d) for i in range(n)])
+        d *= 2
+    if n > 1:
+        pairs.append([(i, n - 1 - i) for i in range(n)])
+    return pairs
+
+
 def butterfly(x, axes_sizes):
     for ax, n in axes_sizes:
-        d = 1
-        while d < n:
-            x = jax.tree.map(
-                lambda a: a + lax.ppermute(a, ax, [(i, i ^ d) for i in range(n)]), x
-            )
-            d *= 2
+        for perm in rounds_of(n):
+            x = jax.tree.map(lambda a: a + lax.ppermute(a, ax, perm), x)
     return x
 
 
@@ -34,7 +41,11 @@
         bit = (me // d) % 2
         keep = lax.dynamic_slice_in_dim(x, bit * h, h, 0)
         send = lax.dynamic_slice_in_dim(x, (1 - bit) * h, h, 0)
-        x = keep + lax.ppermute(send, ax, [(i, i ^ d) for i in range(n)])
+        if d == n // 2:
+            perm = [(i, n - 1 - i) for i in range(n)]
+        else:
+            perm = [(i, i ^ d) for i in range(n)]
+        x = keep + lax.ppermute(send, ax, perm)
         d //= 2
     return x
 

time: 246 us -> 242 us (0.984)
  starting transfers between devices: 21.9 us -> 17.7 us
    ppermute x10, starting transfers between devices: 21.7 us -> 17.5 us  [the longest x8 14.4 us: butterfly(): x = jax.tree.map(lambda a: a + lax.ppermute(a, ax, perm), x)]
where the time goes in v6:
time: 242 us
  waiting for transfers between devices  179 us (74%)
  matrix products  21.9 us (9%)
  starting transfers between devices  17.7 us (7%)
  between operations  15.6 us (6%)
  other arithmetic  4.57 us (2%)
  local copies, waits for them, and re-layouts  2.96 us (1%)
    all_gather x1, waiting for transfers between devices, per_device(): full_head = lax.all_gather(head_weight, SEQ, axis=0, tiled=True)  91.6 us
    reduce_scatter x1, waiting for transfers between devices, per_device(): lax.psum_scatter(partial, 'vz', scatter_dimension=0, tiled=True)  57.4 us
    ppermute x8, waiting for transfers between devices, butterfly(): x = jax.tree.map(lambda a: a + lax.ppermute(a, ax, perm), x)  20 us
    ppermute x8, starting transfers between devices, butterfly(): x = jax.tree.map(lambda a: a + lax.ppermute(a, ax, perm), x)  14.4 us
    dot_general x1, matrix products, per_device(): lax.dot_general(full_head, dlogits, (((1,), (1,)), ((), ())), preferred_e...  10.2 us
    ppermute x2, waiting for transfers between devices, halving_scatter(): x = keep + lax.ppermute(send, ax, perm)  8.18 us
    dot_general x1, matrix products, per_device(): logits = jnp.dot(hidden, full_head, preferred_element_type=jnp.float32)  8.11 us
  transfers between devices with their start and end apart: 13, of which 13 were waited for; matrix products, arithmetic and copies ran while one was open for 1% of the time, Pallas kernels for 0%

profile of v6, /device:TPU:2, one launch (start us, length us, event | category | flops | bytes accessed | tf_op | source)
XLA Modules:
  0.0 241.9 jit_solution(2208679486816508375)
XLA Ops:
  7.2 0.0 copy-start
  7.2 0.0 copy-start.2
  7.2 0.0 all-gather.2.cloned.1.call-start
  7.2 0.7 all-gather.2.cloned.1.call-update
  7.9 0.0 reduce-scatter.2.cloned.1.call-start
  8.0 0.0 copy-done.2
  8.0 0.1 copy.9
  8.1 0.1 reduce-window.8
  8.1 0.1 reduce
  8.3 91.6 %all-gather.2.cloned.1.call-done = bf16[4096,2048]{1,0:T(8,128)(2,1)} async-done(((bf16[512,2048]{1,0:T(8,128)(2,1)}), bf16[4096,2048]{1,0:T(8,128)(2,1)}) %all-gather.2.cloned.1.call-update) | async-done | bytes 16777232 | tf_op jit(solution)/shard_map/all_gather | solution.py:81
  99.9 0.0 copy-done
  99.9 8.1 %fusion.35 = f32[256,2048]{1,0:T(8,128)S(1)} fusion(bf16[256,4096]{1,0:T(8,128)(2,1)S(1)} %copy-done, bf16[4096,2048]{1,0:T(8,128)(2,1)} %all-gather.2.cloned.1.call-done), kind=kOutput, calls=%fused_computation.63 | convolution fusion | flops 4294967296 | bytes 20971520 | tf_op jit(solution)/shard_map/dot_general | solution.py:82
  108.0 0.0 copy-start.5
  108.0 1.3 copy-done.5
  109.4 0.0 copy-start.1
  109.4 0.0 copy-start.4
  109.4 0.0 copy-start.3
  109.4 1.2 fusion.3
  110.6 0.3 collective-permute-start
  110.9 1.3 collective-permute-done
  112.2 1.0 collective-permute-start.1
  113.2 4.7 %collective-permute-done.1 = f32[32,1024]{1,0:T(8,128)S(1)} collective-permute-done((f32[32,1024]{1,0:T(8,128)S(1)}, f32[32,1024]{1,0:T(8,128)S(1)}, u32[]{:S(2)}, u32[]{:S(2)}) %collective-permute-start.1) | collective-permute-done | bytes 131104 | tf_op jit(solution)/shard_map/ppermute | solution.py:32
  118.0 1.3 collective-permute-start.2
  119.3 3.8 %collective-permute-done.2 = f32[32,1024]{1,0:T(8,128)S(1)} collective-permute-done((f32[32,1024]{1,0:T(8,128)S(1)}, f32[32,1024]{1,0:T(8,128)S(1)}, u32[]{:S(2)}, u32[]{:S(2)}) %collective-permute-start.2) | collective-permute-done | bytes 131104 | tf_op jit(solution)/shard_map/ppermute | solution.py:32
  123.1 0.1 collective-permute-start.3
  123.2 1.3 collective-permute-done.3
  124.5 0.1 fusion.8
  124.6 0.0 copy-done.1
  124.6 0.6 fusion.18
  125.9 0.0 copy-start.6
  125.9 0.0 copy-done.4
  125.9 0.4 convolution_bitcast_fusion.1
  126.3 0.1 pad_maximum_fusion
  126.3 1.6 collective-permute-start.4
  127.9 2.2 collective-permute-done.4
  130.1 2.7 %collective-permute-start.5 = (f32[17,32]{1,0:T(8,128)S(1)}, f32[17,32]{1,0:T(8,128)S(1)}, u32[]{:S(2)}, u32[]{:S(2)}) collective-permute-start(f32[17,32]{1,0:T(8,128)S(1)} %fusion.34), channel_id=1, source_target_pairs={{0,3},{1,2},{2,1},{3,0},{4,7},{5,6},{6,5},{7,4},{8,11},{9,10},{10,... | collective-permute-start | bytes 6536 | tf_op jit(solution)/shard_map/ppermute | solution.py:32
  132.9 2.2 collective-permute-done.5
  135.0 1.6 collective-permute-start.6
  136.6 2.1 collective-permute-done.6
  138.7 2.5 %collective-permute-start.7 = (f32[17,32]{1,0:T(8,128)S(1)}, f32[17,32]{1,0:T(8,128)S(1)}, u32[]{:S(2)}, u32[]{:S(2)}) collective-permute-start(f32[17,32]{1,0:T(8,128)S(1)} %add.105), channel_id=1, source_target_pairs={{0,8},{4,12},{8,0},{12,4},{16,24},{20,28},{24,16},{28,20},{1,9},{5... | collective-permute-start | bytes 6536 | tf_op jit(solution)/shard_map/ppermute | solution.py:32
  141.3 2.0 collective-permute-done.7
  143.3 3.3 %collective-permute-start.8 = (f32[17,32]{1,0:T(8,128)S(1)}, f32[17,32]{1,0:T(8,128)S(1)}, u32[]{:S(2)}, u32[]{:S(2)}) collective-permute-start(f32[17,32]{1,0:T(8,128)S(1)} %add.106), channel_id=1, source_target_pairs={{0,28},{4,24},{8,20},{12,16},{16,12},{20,8},{24,4},{28,0},{1,29},{... | collective-permute-start | bytes 6536 | tf_op jit(solution)/shard_map/ppermute | solution.py:32
  146.7 1.7 collective-permute-done.8
  148.4 0.0 copy-done.3
  148.4 0.4 fusion.2
  148.8 0.0 copy-done.6
  148.8 1.6 fusion.1
  150.4 10.2 %convolution_bitcast_fusion = f32[4096,256]{0,1:T(8,128)} fusion(bf16[256,2048]{1,0:T(8,128)(2,1)S(1)} %fusion.1, bf16[4096,2048]{1,0:T(8,128)(2,1)} %all-gather.2.cloned.1.call-done), kind=kOutput, calls=%fused_computation | convolution fusion | flops 4294967296 | bytes 22020096 | tf_op jit(solution)/shard_map/dot_general | solution.py:117
  160.6 0.0 reduce-scatter.2.cloned.1.call-update
  160.7 57.4 %reduce-scatter.2.cloned.1.call-done = f32[512,256]{0,1:T(8,128)} async-done(((f32[4096,256]{0,1:T(8,128)}), f32[512,256]{0,1:T(8,128)}) %reduce-scatter.2.cloned.1.call-update) | async-done | bytes 524304 | tf_op jit(solution)/shard_map/reduce_scatter | solution.py:121
  218.1 1.0 constant_dynamic-slice_fusion.1
  219.1 2.8 %collective-permute-start.9 = (f32[256,256]{0,1:T(8,128)S(1)}, f32[256,256]{0,1:T(8,128)S(1)}, u32[]{:S(2)}, u32[]{:S(2)}) collective-permute-start(f32[256,256]{0,1:T(8,128)S(1)} %constant_dynamic-slice_fusion.1), channel_id=1, source_target_pairs={{0,3},{1,2},{2,1},{3,0},{4,7},{5,6},{6,5},{7,4},{8,11},{9,10},{10,... | collective-permute-start | bytes 786440 | tf_op jit(solution)/shard_map/ppermute | solution.py:48
  221.9 6.5 %collective-permute-done.9 = f32[256,256]{0,1:T(8,128)S(1)} collective-permute-done((f32[256,256]{0,1:T(8,128)S(1)}, f32[256,256]{0,1:T(8,128)S(1)}, u32[]{:S(2)}, u32[]{:S(2)}) %collective-permute-start.9) | collective-permute-done | bytes 262176 | tf_op jit(solution)/shard_map/ppermute | solution.py:48
  228.3 1.0 dynamic-slice_add_fusion
  229.4 0.3 collective-permute-start.10
  229.7 0.6 subtract_reduce_fusion
  230.3 0.5 slice.9
  231.5 1.2 pad_maximum_fusion.1
  232.7 1.7 collective-permute-done.10
  234.4 0.6 fusion.11
  (15 shorter events, 0.2 us)
Async XLA Ops:
  7.2 92.7 %copy-start = (bf16[256,4096]{1,0:T(8,128)(2,1)S(1)}, bf16[256,4096]{1,0:T(8,128)(2,1)}, u32[]{:S(2)}) copy-start(bf16[256,4096]{1,0:T(8,128)(2,1)} %param.6) | copy-start | bytes 6291460
  7.2 0.8 copy-start.2
  7.2 92.7 %all-gather.2.cloned.1.call-start = ((), (), s32[]{:S(2)}) async-start(), calls=%async_computation.1 | async-start | bytes 18874368 | tf_op jit(solution)/shard_map/all_gather | solution.py:81
  7.9 210.2 %reduce-scatter.2.cloned.1.call-start = ((), (), s32[]{:S(2)}) async-start(), calls=%async_computation.2 | async-start | bytes 4718592 | tf_op jit(solution)/shard_map/reduce_scatter | solution.py:121
  108.0 1.4 copy-start.5
  109.4 15.2 %copy-start.1 = (s32[2048]{0:T(1024)S(1)}, s32[2048]{0:T(1024)}, u32[]{:S(2)}) copy-start(s32[2048]{0:T(1024)} %param.11) | copy-start | bytes 24580
  109.4 16.5 %copy-start.4 = (f32[16,2048]{1,0:T(8,128)S(1)}, f32[16,2048]{1,0:T(8,128)}, u32[]{:S(2)}) copy-start(f32[16,2048]{1,0:T(8,128)} %param.8) | copy-start | bytes 393220
  109.4 39.0 %copy-start.3 = (s32[32]{0:T(128)S(1)}, s32[32]{0:T(128)}, u32[]{:S(2)}) copy-start(s32[32]{0:T(128)} %param.10) | copy-start | bytes 388
  110.6 1.6 collective-permute-start
  112.2 5.7 %collective-permute-start.1 = (f32[32,1024]{1,0:T(8,128)S(1)}, f32[32,1024]{1,0:T(8,128)S(1)}, u32[]{:S(2)}, u32[]{:S(2)}) collective-permute-start(f32[32,1024]{1,0:T(8,128)S(1)} %dynamic-slice_add_fusion.1), channel_id=1, source_target_pairs={{0,64},{64,0},{128,192},{192,128},{1,65},{65,1},{129,193},{193,129... | collective-permute-start | bytes 393224 | tf_op jit(solution)/shard_map/ppermute | solution.py:32
  118.0 5.1 %collective-permute-start.2 = (f32[32,1024]{1,0:T(8,128)S(1)}, f32[32,1024]{1,0:T(8,128)S(1)}, u32[]{:S(2)}, u32[]{:S(2)}) collective-permute-start(f32[32,1024]{1,0:T(8,128)S(1)} %add.99), channel_id=1, source_target_pairs={{0,192},{64,128},{128,64},{192,0},{1,193},{65,129},{129,65},{193,1... | collective-permute-start | bytes 393224 | tf_op jit(solution)/shard_map/ppermute | solution.py:32
  123.1 1.4 collective-permute-start.3
  125.9 22.9 %copy-start.6 = (f32[256,2048]{1,0:T(8,128)S(1)}, f32[256,2048]{1,0:T(8,128)}, u32[]{:S(2)}) copy-start(f32[256,2048]{1,0:T(8,128)} %copy-done.5) | copy-start | bytes 6291460
  126.3 3.8 %collective-permute-start.4 = (f32[17,32]{1,0:T(8,128)S(1)}, f32[17,32]{1,0:T(8,128)S(1)}, u32[]{:S(2)}, u32[]{:S(2)}) collective-permute-start(f32[17,32]{1,0:T(8,128)S(1)} %pad_maximum_fusion), channel_id=1, source_target_pairs={{0,1},{1,0},{2,3},{3,2},{4,5},{5,4},{6,7},{7,6},{8,9},{9,8},{10,11... | collective-permute-start | bytes 6536 | tf_op jit(solution)/shard_map/ppermute | solution.py:32
  130.1 4.9 %collective-permute-start.5 = (f32[17,32]{1,0:T(8,128)S(1)}, f32[17,32]{1,0:T(8,128)S(1)}, u32[]{:S(2)}, u32[]{:S(2)}) collective-permute-start(f32[17,32]{1,0:T(8,128)S(1)} %fusion.34), channel_id=1, source_target_pairs={{0,3},{1,2},{2,1},{3,0},{4,7},{5,6},{6,5},{7,4},{8,11},{9,10},{10,... | collective-permute-start | bytes 6536 | tf_op jit(solution)/shard_map/ppermute | solution.py:32
  135.0 3.7 %collective-permute-start.6 = (f32[17,32]{1,0:T(8,128)S(1)}, f32[17,32]{1,0:T(8,128)S(1)}, u32[]{:S(2)}, u32[]{:S(2)}) collective-permute-start(f32[17,32]{1,0:T(8,128)S(1)} %add.104), channel_id=1, source_target_pairs={{0,4},{4,0},{8,12},{12,8},{16,20},{20,16},{24,28},{28,24},{1,5},{5... | collective-permute-start | bytes 6536 | tf_op jit(solution)/shard_map/ppermute | solution.py:32
  138.7 4.6 %collective-permute-start.7 = (f32[17,32]{1,0:T(8,128)S(1)}, f32[17,32]{1,0:T(8,128)S(1)}, u32[]{:S(2)}, u32[]{:S(2)}) collective-permute-start(f32[17,32]{1,0:T(8,128)S(1)} %add.105), channel_id=1, source_target_pairs={{0,8},{4,12},{8,0},{12,4},{16,24},{20,28},{24,16},{28,20},{1,9},{5... | collective-permute-start | bytes 6536 | tf_op jit(solution)/shard_map/ppermute | solution.py:32
  143.3 5.0 %collective-permute-start.8 = (f32[17,32]{1,0:T(8,128)S(1)}, f32[17,32]{1,0:T(8,128)S(1)}, u32[]{:S(2)}, u32[]{:S(2)}) collective-permute-start(f32[17,32]{1,0:T(8,128)S(1)} %add.106), channel_id=1, source_target_pairs={{0,28},{4,24},{8,20},{12,16},{16,12},{20,8},{24,4},{28,0},{1,29},{... | collective-permute-start | bytes 6536 | tf_op jit(solution)/shard_map/ppermute | solution.py:32
  219.1 9.3 %collective-permute-start.9 = (f32[256,256]{0,1:T(8,128)S(1)}, f32[256,256]{0,1:T(8,128)S(1)}, u32[]{:S(2)}, u32[]{:S(2)}) collective-permute-start(f32[256,256]{0,1:T(8,128)S(1)} %constant_dynamic-slice_fusion.1), channel_id=1, source_target_pairs={{0,3},{1,2},{2,1},{3,0},{4,7},{5,6},{6,5},{7,4},{8,11},{9,10},{10,... | collective-permute-start | bytes 786440 | tf_op jit(solution)/shard_map/ppermute | solution.py:48
  229.4 5.1 %collective-permute-start.10 = (f32[128,256]{0,1:T(8,128)S(1)}, f32[128,256]{0,1:T(8,128)S(1)}, u32[]{:S(2)}, u32[]{:S(2)}) collective-permute-start(f32[128,256]{0,1:T(8,128)S(1)} %constant_dynamic-slice_fusion), channel_id=1, source_target_pairs={{0,1},{1,0},{2,3},{3,2},{4,5},{5,4},{6,7},{7,6},{8,9},{9,8},{10,11... | collective-permute-start | bytes 393224 | tf_op jit(solution)/shard_map/ppermute | solution.py:48
Sparse Core Ops, SparseCore 0:
  9.9 89.9 all-gather.1
  160.8 57.2 reduce-scatter.1

commit v7 on v6

--- a/solution.py
+++ b/solution.py
@@ -50,6 +50,40 @@
     return x
 
 
+def two_way_butterfly(x, ax, n):
+    if n != 4:
+        return butterfly(x, [(ax, n)])
+    xor1 = [(i, i ^ 1) for i in range(n)]
+    mirror = [(i, n - 1 - i) for i in range(n)]
+    half = x.shape[-1] // 2
+    a, b = x[..., :half], x[..., half:]
+    a = a + lax.ppermute(a, ax, xor1)
+    b = b + lax.ppermute(b, ax, mirror)
+    a = a + lax.ppermute(a, ax, mirror)
+    b = b + lax.ppermute(b, ax, xor1)
+    return jnp.concatenate([a, b], axis=-1)
+
+
+def two_way_scatter(x, ax, n):
+    if n != 4:
+        return halving_scatter(x, ax, n)
+    me = lax.axis_index(ax)
+    q = x.shape[0] // n
+    half = x.shape[1] // 2
+    first = halving_scatter(x[:, :half], ax, n)
+    b = x[:, half:]
+    b = jnp.concatenate([b[0:q], b[3 * q:4 * q], b[q:2 * q], b[2 * q:3 * q]], axis=0)
+    group = jnp.where((me == 0) | (me == 3), 0, 1)
+    keep = lax.dynamic_slice_in_dim(b, group * 2 * q, 2 * q, 0)
+    send = lax.dynamic_slice_in_dim(b, (1 - group) * 2 * q, 2 * q, 0)
+    b = keep + lax.ppermute(send, ax, [(i, i ^ 1) for i in range(n)])
+    pos = me // 2
+    keep = lax.dynamic_slice_in_dim(b, pos * q, q, 0)
+    send = lax.dynamic_slice_in_dim(b, (1 - pos) * q, q, 0)
+    b = keep + lax.ppermute(send, ax, [(i, n - 1 - i) for i in range(n)])
+    return jnp.concatenate([first, b], axis=1)
+
+
 def softmax_terms(scores, pair_rows):
     onehot = (jnp.arange(scores.shape[0], dtype=jnp.int32)[:, None] == pair_rows[None, :]).astype(
         jnp.float32
@@ -88,8 +122,8 @@
     chip_sums = butterfly(local_sums, [("sc", n_sc)])
     core = lax.axis_index("sc")
     half_cols = vocab_cols // n_sc
-    mine = butterfly(
-        lax.dynamic_slice_in_dim(chip_sums, core * half_cols, half_cols, 1), [("sx", n_sx)]
+    mine = two_way_butterfly(
+        lax.dynamic_slice_in_dim(chip_sums, core * half_cols, half_cols, 1), "sx", n_sx
     )
     theirs = lax.ppermute(mine, "sc", [(0, 1), (1, 0)])
     totals = jnp.where(
@@ -117,7 +151,7 @@
     partial = lax.dot_general(
         full_head, dlogits, (((1,), (1,)), ((), ())), preferred_element_type=jnp.float32
     )
-    grad_cols = halving_scatter(
+    grad_cols = two_way_scatter(
         lax.psum_scatter(partial, "vz", scatter_dimension=0, tiled=True), "vy", n_vy
     )
     losses = jnp.stack([contrast, flops_value])

time: 242 us -> 244 us (level)
  starting transfers between devices: 17.7 us -> 21.6 us
  waiting for transfers between devices: 179 us -> 176 us
    ppermute x0 -> x6, waiting for transfers between devices: none -> 14.2 us  [the longest x1 4.89 us: two_way_scatter(): b = keep + lax.ppermute(send, ax, [(i, n - 1 - i) for i in range(n)])]
    ppermute x8 -> x6, waiting for transfers between devices: 20 us -> 11.5 us  [butterfly(): x = jax.tree.map(lambda a: a + lax.ppermute(a, ax, perm), x)]
    ppermute x0 -> x6, starting transfers between devices: none -> 6.18 us  [the longest x1 3.51 us: two_way_butterfly(): b = b + lax.ppermute(b, ax, xor1)]
    ppermute x2, waiting for transfers between devices: 8.18 us -> 2.04 us  [halving_scatter(): x = keep + lax.ppermute(send, ax, perm)]
    reduce_scatter x1, waiting for transfers between devices: 57.4 us -> 54.3 us  [per_device(): lax.psum_scatter(partial, 'vz', scatter_dimension=0, tiled=True)]
    slice x0 -> x4, local copies, waits for them, and re-layouts: none -> 2.77 us  [the longest x1 0.97 us: two_way_scatter(): first = halving_scatter(x[:, :half], ax, n)]
    ppermute x8 -> x6, starting transfers between devices: 14.4 us -> 12 us  [butterfly(): x = jax.tree.map(lambda a: a + lax.ppermute(a, ax, perm), x)]
  transfers between devices with their start and end apart: 13 -> 17, of which waited for: 13 -> 17; matrix products, arithmetic and copies ran while one was open for 1% -> 2% of each run, Pallas kernels for 0% -> 0%
where the time goes in v7:
time: 244 us; the launch traced here: 243 us
  waiting for transfers between devices  176 us (72%)
  matrix products  21.9 us (9%)
  starting transfers between devices  21.6 us (9%)
  between operations  15.7 us (6%)
  local copies, waits for them, and re-layouts  4.82 us (2%)
  other arithmetic  3.67 us (2%)
    all_gather x1, waiting for transfers between devices, per_device(): full_head = lax.all_gather(head_weight, SEQ, axis=0, tiled=True)  91.6 us
    reduce_scatter x1, waiting for transfers between devices, per_device(): lax.psum_scatter(partial, 'vz', scatter_dimension=0, tiled=True)  54.3 us
    ppermute x6, starting transfers between devices, butterfly(): x = jax.tree.map(lambda a: a + lax.ppermute(a, ax, perm), x)  12 us
    ppermute x6, waiting for transfers between devices, butterfly(): x = jax.tree.map(lambda a: a + lax.ppermute(a, ax, perm), x)  11.5 us
    dot_general x1, matrix products, per_device(): lax.dot_general(full_head, dlogits, (((1,), (1,)), ((), ())), preferred_e...  10.2 us
    dot_general x1, matrix products, per_device(): logits = jnp.dot(hidden, full_head, preferred_element_type=jnp.float32)  8.11 us
    ppermute x1, waiting for transfers between devices, two_way_scatter(): b = keep + lax.ppermute(send, ax, [(i, n - 1 - i) for i in range(n)])  4.89 us
  transfers between devices with their start and end apart: 17, of which 17 were waited for; matrix products, arithmetic and copies ran while one was open for 2% of the time, Pallas kernels for 0%

profile of v7, /device:TPU:2, one launch (start us, length us, event | category | flops | bytes accessed | tf_op | source)
XLA Modules:
  0.0 243.5 jit_solution(3613961121332395439)
XLA Ops:
  7.2 0.0 copy-start
  7.2 0.0 copy-start.2
  7.2 0.0 all-gather.2.cloned.1.call-start
  7.2 0.7 all-gather.2.cloned.1.call-update
  7.9 0.0 reduce-scatter.2.cloned.1.call-start
  8.0 0.0 copy-done.2
  8.0 0.1 copy.9
  8.1 0.1 reduce-window.8
  8.1 0.1 reduce
  8.3 91.6 %all-gather.2.cloned.1.call-done = bf16[4096,2048]{1,0:T(8,128)(2,1)} async-done(((bf16[512,2048]{1,0:T(8,128)(2,1)}), bf16[4096,2048]{1,0:T(8,128)(2,1)}) %all-gather.2.cloned.1.call-update) | async-done | bytes 16777232 | tf_op jit(solution)/shard_map/all_gather | solution.py:115
  99.9 0.0 copy-done
  99.9 8.1 %fusion.35 = f32[256,2048]{1,0:T(8,128)S(1)} fusion(bf16[256,4096]{1,0:T(8,128)(2,1)S(1)} %copy-done, bf16[4096,2048]{1,0:T(8,128)(2,1)} %all-gather.2.cloned.1.call-done), kind=kOutput, calls=%fused_computation.72 | convolution fusion | flops 4294967296 | bytes 20971520 | tf_op jit(solution)/shard_map/dot_general | solution.py:116
  108.0 0.0 copy-start.5
  108.0 1.3 copy-done.5
  109.4 1.2 fusion.3
  110.6 0.0 copy-start.3
  110.6 0.3 collective-permute-start
  110.9 1.3 collective-permute-done
  112.3 1.0 collective-permute-start.1
  113.3 0.6 collective-permute-start.3
  113.9 2.8 %collective-permute-done.1 = f32[32,512]{1,0:T(8,128)S(1)} collective-permute-done((f32[32,512]{1,0:T(8,128)S(1)}, f32[32,512]{1,0:T(8,128)S(1)}, u32[]{:S(2)}, u32[]{:S(2)}) %collective-permute-start.1) | collective-permute-done | bytes 65568 | tf_op jit(solution)/shard_map/ppermute | solution.py:60
  116.6 0.9 collective-permute-done.3
  117.6 0.7 collective-permute-start.2
  118.2 3.5 %collective-permute-start.4 = (f32[32,512]{1,0:T(8,128)S(1)}, f32[32,512]{1,0:T(8,128)S(1)}, u32[]{:S(2)}, u32[]{:S(2)}) collective-permute-start(f32[32,512]{1,0:T(8,128)S(1)} %get-tuple-element.7), channel_id=1, source_target_pairs={{0,64},{64,0},{128,192},{192,128},{1,65},{65,1},{129,193},{193,129... | collective-permute-start | bytes 196616 | tf_op jit(solution)/shard_map/ppermute | solution.py:63
  121.7 0.2 collective-permute-done.2
  121.9 2.1 collective-permute-done.4
  124.0 0.1 collective-permute-start.5
  124.1 1.3 collective-permute-done.5
  125.5 0.1 fusion.8
  125.6 0.0 copy-done.1
  125.6 0.6 fusion.17
  126.9 0.4 convolution_bitcast_fusion.1
  127.2 0.1 pad_maximum_fusion.2
  127.3 1.6 collective-permute-start.6
  128.9 2.2 collective-permute-done.6
  131.1 2.7 %collective-permute-start.7 = (f32[17,32]{1,0:T(8,128)S(1)}, f32[17,32]{1,0:T(8,128)S(1)}, u32[]{:S(2)}, u32[]{:S(2)}) collective-permute-start(f32[17,32]{1,0:T(8,128)S(1)} %fusion.32), channel_id=1, source_target_pairs={{0,3},{1,2},{2,1},{3,0},{4,7},{5,6},{6,5},{7,4},{8,11},{9,10},{10,... | collective-permute-start | bytes 6536 | tf_op jit(solution)/shard_map/ppermute | solution.py:32
  133.8 2.2 collective-permute-done.7
  136.0 1.6 collective-permute-start.8
  137.6 2.1 collective-permute-done.8
  139.7 2.5 %collective-permute-start.9 = (f32[17,32]{1,0:T(8,128)S(1)}, f32[17,32]{1,0:T(8,128)S(1)}, u32[]{:S(2)}, u32[]{:S(2)}) collective-permute-start(f32[17,32]{1,0:T(8,128)S(1)} %add.131), channel_id=1, source_target_pairs={{0,8},{4,12},{8,0},{12,4},{16,24},{20,28},{24,16},{28,20},{1,9},{5... | collective-permute-start | bytes 6536 | tf_op jit(solution)/shard_map/ppermute | solution.py:32
  142.2 2.1 collective-permute-done.9
  144.3 3.3 %collective-permute-start.10 = (f32[17,32]{1,0:T(8,128)S(1)}, f32[17,32]{1,0:T(8,128)S(1)}, u32[]{:S(2)}, u32[]{:S(2)}) collective-permute-start(f32[17,32]{1,0:T(8,128)S(1)} %add.132), channel_id=1, source_target_pairs={{0,28},{4,24},{8,20},{12,16},{16,12},{20,8},{24,4},{28,0},{1,29},{... | collective-permute-start | bytes 6536 | tf_op jit(solution)/shard_map/ppermute | solution.py:32
  147.6 1.7 collective-permute-done.10
  149.3 0.4 fusion.2
  149.8 0.0 copy-done.6
  149.8 1.6 fusion.1
  151.4 10.2 %convolution_bitcast_fusion = f32[4096,256]{0,1:T(8,128)} fusion(bf16[256,2048]{1,0:T(8,128)(2,1)S(1)} %fusion.1, bf16[4096,2048]{1,0:T(8,128)(2,1)} %all-gather.2.cloned.1.call-done), kind=kOutput, calls=%fused_computation | convolution fusion | flops 4294967296 | bytes 22020096 | tf_op jit(solution)/shard_map/dot_general | solution.py:151
  161.6 0.0 reduce-scatter.2.cloned.1.call-update
  161.7 0.5 slice.46
  162.2 0.6 subtract_reduce_fusion
  163.5 1.2 pad_maximum_fusion.3
  164.7 54.3 %reduce-scatter.2.cloned.1.call-done = f32[512,256]{0,1:T(8,128)} async-done(((f32[4096,256]{0,1:T(8,128)}), f32[512,256]{0,1:T(8,128)}) %reduce-scatter.2.cloned.1.call-update) | async-done | bytes 524304 | tf_op jit(solution)/shard_map/reduce_scatter | solution.py:155
  219.0 1.0 slice.42
  220.0 2.8 %collective-permute-start.11 = (f32[256,128]{0,1:T(8,128)S(1)}, f32[256,128]{0,1:T(8,128)S(1)}, u32[]{:S(2)}, u32[]{:S(2)}) collective-permute-start(f32[256,128]{0,1:T(8,128)S(1)} %constant_dynamic-slice_fusion.3), channel_id=1, source_target_pairs={{0,3},{1,2},{2,1},{3,0},{4,7},{5,6},{6,5},{7,4},{8,11},{9,10},{10,... | collective-permute-start | bytes 393224 | tf_op jit(solution)/shard_map/ppermute | solution.py:48
  222.8 0.9 fusion.33
  223.7 0.9 slice.45
  224.7 0.3 collective-permute-start.13
  225.0 1.5 collective-permute-done.11
  226.5 0.4 collective-permute-start.12
  226.9 3.4 %collective-permute-done.13 = f32[256,128]{0,1:T(8,128)S(1)} collective-permute-done((f32[256,128]{0,1:T(8,128)S(1)}, f32[256,128]{0,1:T(8,128)S(1)}, u32[]{:S(2)}, u32[]{:S(2)}) %collective-permute-start.13) | collective-permute-done | bytes 131104 | tf_op jit(solution)/shard_map/ppermute | solution.py:79
  230.4 0.1 collective-permute-start.14
  230.5 0.6 collective-permute-done.12
  231.1 4.9 %collective-permute-done.14 = f32[128,128]{0,1:T(8,128)S(1)} collective-permute-done((f32[128,128]{0,1:T(8,128)S(1)}, f32[128,128]{0,1:T(8,128)S(1)}, u32[]{:S(2)}, u32[]{:S(2)}) %collective-permute-start.14) | collective-permute-done | bytes 65568 | tf_op jit(solution)/shard_map/ppermute | solution.py:83
  236.0 0.6 maximum_bitcast_fusion
  (31 shorter events, 0.3 us)
Async XLA Ops:
  7.2 92.7 %copy-start = (bf16[256,4096]{1,0:T(8,128)(2,1)S(1)}, bf16[256,4096]{1,0:T(8,128)(2,1)}, u32[]{:S(2)}) copy-start(bf16[256,4096]{1,0:T(8,128)(2,1)} %param.6) | copy-start | bytes 6291460
  7.2 0.8 copy-start.2
  7.2 92.7 %all-gather.2.cloned.1.call-start = ((), (), s32[]{:S(2)}) async-start(), calls=%async_computation.1 | async-start | bytes 18874368 | tf_op jit(solution)/shard_map/all_gather | solution.py:115
  7.9 211.1 %reduce-scatter.2.cloned.1.call-start = ((), (), s32[]{:S(2)}) async-start(), calls=%async_computation.2 | async-start | bytes 4718592 | tf_op jit(solution)/shard_map/reduce_scatter | solution.py:155
  108.0 1.4 copy-start.5
  109.4 16.2 %copy-start.1 = (s32[2048]{0:T(1024)S(1)}, s32[2048]{0:T(1024)}, u32[]{:S(2)}) copy-start(s32[2048]{0:T(1024)} %param.11) | copy-start | bytes 24580
  109.4 17.5 %copy-start.4 = (f32[16,2048]{1,0:T(8,128)S(1)}, f32[16,2048]{1,0:T(8,128)}, u32[]{:S(2)}) copy-start(f32[16,2048]{1,0:T(8,128)} %param.8) | copy-start | bytes 393220
  110.6 38.7 %copy-start.3 = (s32[32]{0:T(128)S(1)}, s32[32]{0:T(128)}, u32[]{:S(2)}) copy-start(s32[32]{0:T(128)} %param.10) | copy-start | bytes 388
  110.6 1.6 collective-permute-start
  112.3 4.4 %collective-permute-start.1 = (f32[32,512]{1,0:T(8,128)S(1)}, f32[32,512]{1,0:T(8,128)S(1)}, u32[]{:S(2)}, u32[]{:S(2)}) collective-permute-start(f32[32,512]{1,0:T(8,128)S(1)} %get-tuple-element.8), channel_id=1, source_target_pairs={{0,64},{64,0},{128,192},{192,128},{1,65},{65,1},{129,193},{193,129... | collective-permute-start | bytes 196616 | tf_op jit(solution)/shard_map/ppermute | solution.py:60
  113.3 4.3 %collective-permute-start.3 = (f32[32,512]{1,0:T(8,128)S(1)}, f32[32,512]{1,0:T(8,128)S(1)}, u32[]{:S(2)}, u32[]{:S(2)}) collective-permute-start(f32[32,512]{1,0:T(8,128)S(1)} %get-tuple-element.9), channel_id=1, source_target_pairs={{0,192},{64,128},{128,64},{192,0},{1,193},{65,129},{129,65},{193,1... | collective-permute-start | bytes 196616 | tf_op jit(solution)/shard_map/ppermute | solution.py:61
  117.6 4.4 %collective-permute-start.2 = (f32[32,512]{1,0:T(8,128)S(1)}, f32[32,512]{1,0:T(8,128)S(1)}, u32[]{:S(2)}, u32[]{:S(2)}) collective-permute-start(f32[32,512]{1,0:T(8,128)S(1)} %get-tuple-element.6), channel_id=1, source_target_pairs={{0,192},{64,128},{128,64},{192,0},{1,193},{65,129},{129,65},{193,1... | collective-permute-start | bytes 196616 | tf_op jit(solution)/shard_map/ppermute | solution.py:62
  118.2 5.7 %collective-permute-start.4 = (f32[32,512]{1,0:T(8,128)S(1)}, f32[32,512]{1,0:T(8,128)S(1)}, u32[]{:S(2)}, u32[]{:S(2)}) collective-permute-start(f32[32,512]{1,0:T(8,128)S(1)} %get-tuple-element.7), channel_id=1, source_target_pairs={{0,64},{64,0},{128,192},{192,128},{1,65},{65,1},{129,193},{193,129... | collective-permute-start | bytes 196616 | tf_op jit(solution)/shard_map/ppermute | solution.py:63
  124.0 1.4 collective-permute-start.5
  126.8 22.9 %copy-start.6 = (f32[256,2048]{1,0:T(8,128)S(1)}, f32[256,2048]{1,0:T(8,128)}, u32[]{:S(2)}) copy-start(f32[256,2048]{1,0:T(8,128)} %copy-done.5) | copy-start | bytes 6291460
  127.3 3.8 %collective-permute-start.6 = (f32[17,32]{1,0:T(8,128)S(1)}, f32[17,32]{1,0:T(8,128)S(1)}, u32[]{:S(2)}, u32[]{:S(2)}) collective-permute-start(f32[17,32]{1,0:T(8,128)S(1)} %pad_maximum_fusion.2), channel_id=1, source_target_pairs={{0,1},{1,0},{2,3},{3,2},{4,5},{5,4},{6,7},{7,6},{8,9},{9,8},{10,11... | collective-permute-start | bytes 6536 | tf_op jit(solution)/shard_map/ppermute | solution.py:32
  131.1 4.9 %collective-permute-start.7 = (f32[17,32]{1,0:T(8,128)S(1)}, f32[17,32]{1,0:T(8,128)S(1)}, u32[]{:S(2)}, u32[]{:S(2)}) collective-permute-start(f32[17,32]{1,0:T(8,128)S(1)} %fusion.32), channel_id=1, source_target_pairs={{0,3},{1,2},{2,1},{3,0},{4,7},{5,6},{6,5},{7,4},{8,11},{9,10},{10,... | collective-permute-start | bytes 6536 | tf_op jit(solution)/shard_map/ppermute | solution.py:32
  136.0 3.7 %collective-permute-start.8 = (f32[17,32]{1,0:T(8,128)S(1)}, f32[17,32]{1,0:T(8,128)S(1)}, u32[]{:S(2)}, u32[]{:S(2)}) collective-permute-start(f32[17,32]{1,0:T(8,128)S(1)} %add.130), channel_id=1, source_target_pairs={{0,4},{4,0},{8,12},{12,8},{16,20},{20,16},{24,28},{28,24},{1,5},{5... | collective-permute-start | bytes 6536 | tf_op jit(solution)/shard_map/ppermute | solution.py:32
  139.7 4.6 %collective-permute-start.9 = (f32[17,32]{1,0:T(8,128)S(1)}, f32[17,32]{1,0:T(8,128)S(1)}, u32[]{:S(2)}, u32[]{:S(2)}) collective-permute-start(f32[17,32]{1,0:T(8,128)S(1)} %add.131), channel_id=1, source_target_pairs={{0,8},{4,12},{8,0},{12,4},{16,24},{20,28},{24,16},{28,20},{1,9},{5... | collective-permute-start | bytes 6536 | tf_op jit(solution)/shard_map/ppermute | solution.py:32
  144.3 5.0 %collective-permute-start.10 = (f32[17,32]{1,0:T(8,128)S(1)}, f32[17,32]{1,0:T(8,128)S(1)}, u32[]{:S(2)}, u32[]{:S(2)}) collective-permute-start(f32[17,32]{1,0:T(8,128)S(1)} %add.132), channel_id=1, source_target_pairs={{0,28},{4,24},{8,20},{12,16},{16,12},{20,8},{24,4},{28,0},{1,29},{... | collective-permute-start | bytes 6536 | tf_op jit(solution)/shard_map/ppermute | solution.py:32
  220.0 6.5 %collective-permute-start.11 = (f32[256,128]{0,1:T(8,128)S(1)}, f32[256,128]{0,1:T(8,128)S(1)}, u32[]{:S(2)}, u32[]{:S(2)}) collective-permute-start(f32[256,128]{0,1:T(8,128)S(1)} %constant_dynamic-slice_fusion.3), channel_id=1, source_target_pairs={{0,3},{1,2},{2,1},{3,0},{4,7},{5,6},{6,5},{7,4},{8,11},{9,10},{10,... | collective-permute-start | bytes 393224 | tf_op jit(solution)/shard_map/ppermute | solution.py:48
  224.7 5.7 %collective-permute-start.13 = (f32[256,128]{0,1:T(8,128)S(1)}, f32[256,128]{0,1:T(8,128)S(1)}, u32[]{:S(2)}, u32[]{:S(2)}) collective-permute-start(f32[256,128]{0,1:T(8,128)S(1)} %constant_dynamic-slice_fusion.1), channel_id=1, source_target_pairs={{0,1},{1,0},{2,3},{3,2},{4,5},{5,4},{6,7},{7,6},{8,9},{9,8},{10,11... | collective-permute-start | bytes 393224 | tf_op jit(solution)/shard_map/ppermute | solution.py:79
  226.5 4.5 %collective-permute-start.12 = (f32[128,128]{0,1:T(8,128)S(1)}, f32[128,128]{0,1:T(8,128)S(1)}, u32[]{:S(2)}, u32[]{:S(2)}) collective-permute-start(f32[128,128]{0,1:T(8,128)S(1)} %constant_dynamic-slice_fusion.2), channel_id=1, source_target_pairs={{0,1},{1,0},{2,3},{3,2},{4,5},{5,4},{6,7},{7,6},{8,9},{9,8},{10,11... | collective-permute-start | bytes 196616 | tf_op jit(solution)/shard_map/ppermute | solution.py:48
  230.4 5.6 %collective-permute-start.14 = (f32[128,128]{0,1:T(8,128)S(1)}, f32[128,128]{0,1:T(8,128)S(1)}, u32[]{:S(2)}, u32[]{:S(2)}) collective-permute-start(f32[128,128]{0,1:T(8,128)S(1)} %constant_dynamic-slice_fusion), channel_id=1, source_target_pairs={{0,3},{1,2},{2,1},{3,0},{4,7},{5,6},{6,5},{7,4},{8,11},{9,10},{10,... | collective-permute-start | bytes 196616 | tf_op jit(solution)/shard_map/ppermute | solution.py:83
Sparse Core Ops, SparseCore 0:
  9.9 89.9 all-gather.1
  161.7 57.2 reduce-scatter.1

commit v8 on v6

--- a/solution.py
+++ b/solution.py
@@ -16,6 +16,13 @@
 
 
 def rounds_of(n):
+    if n == 8:
+        second = {0: 6, 6: 0, 1: 7, 7: 1, 2: 4, 4: 2, 3: 5, 5: 3}
+        return [
+            [(i, i ^ 1) for i in range(n)],
+            [(i, second[i]) for i in range(n)],
+            [(i, i ^ 2) for i in range(n)],
+        ]
     pairs = []
     d = 1
     while 2 * d < n:
@@ -85,12 +92,12 @@
     fourth = squared * squared
     powered = fourth * fourth
     local_sums = jnp.dot(member, powered, precision=highest)
-    chip_sums = butterfly(local_sums, [("sc", n_sc)])
     core = lax.axis_index("sc")
     half_cols = vocab_cols // n_sc
-    mine = butterfly(
-        lax.dynamic_slice_in_dim(chip_sums, core * half_cols, half_cols, 1), [("sx", n_sx)]
-    )
+    own_half = lax.dynamic_slice_in_dim(local_sums, core * half_cols, half_cols, 1)
+    other_half = lax.dynamic_slice_in_dim(local_sums, (1 - core) * half_cols, half_cols, 1)
+    chip_half = own_half + lax.ppermute(other_half, "sc", [(0, 1), (1, 0)])
+    mine = butterfly(chip_half, [("sx", n_sx)])
     theirs = lax.ppermute(mine, "sc", [(0, 1), (1, 0)])
     totals = jnp.where(
         core == 0,

time: 242 us -> 241 us (level)
    ppermute x8 -> x7, waiting for transfers between devices: 20 us -> 18.8 us  [butterfly(): x = jax.tree.map(lambda a: a + lax.ppermute(a, ax, perm), x)]
    ppermute x8 -> x7, starting transfers between devices: 14.4 us -> 14.8 us  [butterfly(): x = jax.tree.map(lambda a: a + lax.ppermute(a, ax, perm), x)]
where the time goes in v8:
time: 241 us; the launch traced here: 240 us
  waiting for transfers between devices  178 us (74%)
  matrix products  21.9 us (9%)
  starting transfers between devices  18.5 us (8%)
  between operations  15.6 us (6%)
  other arithmetic  4.57 us (2%)
    all_gather x1, waiting for transfers between devices, per_device(): full_head = lax.all_gather(head_weight, SEQ, axis=0, tiled=True)  91.6 us
    reduce_scatter x1, waiting for transfers between devices, per_device(): lax.psum_scatter(partial, 'vz', scatter_dimension=0, tiled=True)  56.5 us
    ppermute x7, waiting for transfers between devices, butterfly(): x = jax.tree.map(lambda a: a + lax.ppermute(a, ax, perm), x)  18.8 us
    ppermute x7, starting transfers between devices, butterfly(): x = jax.tree.map(lambda a: a + lax.ppermute(a, ax, perm), x)  14.8 us
    dot_general x1, matrix products, per_device(): lax.dot_general(full_head, dlogits, (((1,), (1,)), ((), ())), preferred_e...  10.2 us
    dot_general x1, matrix products, per_device(): logits = jnp.dot(hidden, full_head, preferred_element_type=jnp.float32)  8.11 us
    ppermute x2, waiting for transfers between devices, halving_scatter(): x = keep + lax.ppermute(send, ax, perm)  8.1 us
  transfers between devices with their start and end apart: 13, of which 13 were waited for; matrix products, arithmetic and copies ran while one was open for 1% of the time, Pallas kernels for 0%

profile of v8, /device:TPU:2, one launch (start us, length us, event | category | flops | bytes accessed | tf_op | source)
XLA Modules:
  0.0 240.4 jit_solution(1090597962932252126)
XLA Ops:
  7.2 0.0 copy-start
  7.2 0.0 copy-start.2
  7.2 0.0 all-gather.2.cloned.1.call-start
  7.2 0.7 all-gather.2.cloned.1.call-update
  7.9 0.0 reduce-scatter.2.cloned.1.call-start
  8.0 0.0 copy-done.2
  8.0 0.1 copy.9
  8.1 0.1 reduce-window.8
  8.1 0.1 reduce
  8.3 91.6 %all-gather.2.cloned.1.call-done = bf16[4096,2048]{1,0:T(8,128)(2,1)} async-done(((bf16[512,2048]{1,0:T(8,128)(2,1)}), bf16[4096,2048]{1,0:T(8,128)(2,1)}) %all-gather.2.cloned.1.call-update) | async-done | bytes 16777232 | tf_op jit(solution)/shard_map/all_gather | solution.py:88
  99.9 0.0 copy-done
  99.9 8.1 %fusion.35 = f32[256,2048]{1,0:T(8,128)S(1)} fusion(bf16[256,4096]{1,0:T(8,128)(2,1)S(1)} %copy-done, bf16[4096,2048]{1,0:T(8,128)(2,1)} %all-gather.2.cloned.1.call-done), kind=kOutput, calls=%fused_computation.64 | convolution fusion | flops 4294967296 | bytes 20971520 | tf_op jit(solution)/shard_map/dot_general | solution.py:89
  108.0 0.0 copy-start.5
  108.0 0.0 copy-start.1
  108.0 0.0 copy-start.4
  108.1 0.0 copy-start.3
  108.1 1.2 fusion.3
  109.3 0.1 copy-done.5
  109.4 0.3 collective-permute-start
  109.7 1.1 collective-permute-done
  110.8 1.0 collective-permute-start.1
  111.8 4.7 %collective-permute-done.1 = f32[32,1024]{1,0:T(8,128)S(1)} collective-permute-done((f32[32,1024]{1,0:T(8,128)S(1)}, f32[32,1024]{1,0:T(8,128)S(1)}, u32[]{:S(2)}, u32[]{:S(2)}) %collective-permute-start.1) | collective-permute-done | bytes 131104 | tf_op jit(solution)/shard_map/ppermute | solution.py:39
  116.6 1.3 collective-permute-start.2
  117.9 3.8 %collective-permute-done.2 = f32[32,1024]{1,0:T(8,128)S(1)} collective-permute-done((f32[32,1024]{1,0:T(8,128)S(1)}, f32[32,1024]{1,0:T(8,128)S(1)}, u32[]{:S(2)}, u32[]{:S(2)}) %collective-permute-start.2) | collective-permute-done | bytes 131104 | tf_op jit(solution)/shard_map/ppermute | solution.py:39
  121.7 0.1 collective-permute-start.3
  121.8 1.3 collective-permute-done.3
  123.1 0.1 fusion.8
  123.2 0.0 copy-done.1
  123.2 0.6 fusion.18
  124.5 0.0 copy-start.6
  124.5 0.0 copy-done.4
  124.5 0.4 convolution_bitcast_fusion.1
  124.9 0.1 pad_maximum_fusion
  125.0 1.6 collective-permute-start.4
  126.5 2.2 collective-permute-done.4
  128.7 2.7 %collective-permute-start.5 = (f32[17,32]{1,0:T(8,128)S(1)}, f32[17,32]{1,0:T(8,128)S(1)}, u32[]{:S(2)}, u32[]{:S(2)}) collective-permute-start(f32[17,32]{1,0:T(8,128)S(1)} %fusion.34), channel_id=1, source_target_pairs={{0,3},{1,2},{2,1},{3,0},{4,7},{5,6},{6,5},{7,4},{8,11},{9,10},{10,... | collective-permute-start | bytes 6536 | tf_op jit(solution)/shard_map/ppermute | solution.py:39
  131.5 2.2 collective-permute-done.5
  133.7 1.6 collective-permute-start.6
  135.2 2.1 collective-permute-done.6
  137.4 4.1 %collective-permute-start.7 = (f32[17,32]{1,0:T(8,128)S(1)}, f32[17,32]{1,0:T(8,128)S(1)}, u32[]{:S(2)}, u32[]{:S(2)}) collective-permute-start(f32[17,32]{1,0:T(8,128)S(1)} %add.109), channel_id=1, source_target_pairs={{0,24},{4,28},{8,16},{12,20},{16,8},{20,12},{24,0},{28,4},{1,25},{... | collective-permute-start | bytes 6536 | tf_op jit(solution)/shard_map/ppermute | solution.py:39
  141.5 1.7 collective-permute-done.7
  143.2 2.5 %collective-permute-start.8 = (f32[17,32]{1,0:T(8,128)S(1)}, f32[17,32]{1,0:T(8,128)S(1)}, u32[]{:S(2)}, u32[]{:S(2)}) collective-permute-start(f32[17,32]{1,0:T(8,128)S(1)} %add.110), channel_id=1, source_target_pairs={{0,8},{4,12},{8,0},{12,4},{16,24},{20,28},{24,16},{28,20},{1,9},{5... | collective-permute-start | bytes 6536 | tf_op jit(solution)/shard_map/ppermute | solution.py:39
  145.7 2.0 collective-permute-done.8
  147.8 0.0 copy-done.3
  147.8 0.4 fusion.2
  148.3 0.0 copy-done.6
  148.3 1.6 fusion.1
  149.9 10.2 %convolution_bitcast_fusion = f32[4096,256]{0,1:T(8,128)} fusion(bf16[256,2048]{1,0:T(8,128)(2,1)S(1)} %fusion.1, bf16[4096,2048]{1,0:T(8,128)(2,1)} %all-gather.2.cloned.1.call-done), kind=kOutput, calls=%fused_computation | convolution fusion | flops 4294967296 | bytes 22020096 | tf_op jit(solution)/shard_map/dot_general | solution.py:124
  160.1 0.0 reduce-scatter.2.cloned.1.call-update
  160.1 56.5 %reduce-scatter.2.cloned.1.call-done = f32[512,256]{0,1:T(8,128)} async-done(((f32[4096,256]{0,1:T(8,128)}), f32[512,256]{0,1:T(8,128)}) %reduce-scatter.2.cloned.1.call-update) | async-done | bytes 524304 | tf_op jit(solution)/shard_map/reduce_scatter | solution.py:128
  216.6 1.0 constant_dynamic-slice_fusion.1
  217.5 2.8 %collective-permute-start.9 = (f32[256,256]{0,1:T(8,128)S(1)}, f32[256,256]{0,1:T(8,128)S(1)}, u32[]{:S(2)}, u32[]{:S(2)}) collective-permute-start(f32[256,256]{0,1:T(8,128)S(1)} %constant_dynamic-slice_fusion.1), channel_id=1, source_target_pairs={{0,3},{1,2},{2,1},{3,0},{4,7},{5,6},{6,5},{7,4},{8,11},{9,10},{10,... | collective-permute-start | bytes 786440 | tf_op jit(solution)/shard_map/ppermute | solution.py:55
  220.4 6.4 %collective-permute-done.9 = f32[256,256]{0,1:T(8,128)S(1)} collective-permute-done((f32[256,256]{0,1:T(8,128)S(1)}, f32[256,256]{0,1:T(8,128)S(1)}, u32[]{:S(2)}, u32[]{:S(2)}) %collective-permute-start.9) | collective-permute-done | bytes 262176 | tf_op jit(solution)/shard_map/ppermute | solution.py:55
  226.8 1.0 dynamic-slice_add_fusion
  227.8 0.4 collective-permute-start.10
  228.2 0.6 subtract_reduce_fusion
  228.8 0.5 slice.9
  230.0 1.2 pad_maximum_fusion.1
  231.2 1.7 collective-permute-done.10
  232.9 0.6 fusion.11
  (16 shorter events, 0.2 us)
Async XLA Ops:
  7.2 92.7 %copy-start = (bf16[256,4096]{1,0:T(8,128)(2,1)S(1)}, bf16[256,4096]{1,0:T(8,128)(2,1)}, u32[]{:S(2)}) copy-start(bf16[256,4096]{1,0:T(8,128)(2,1)} %param.6) | copy-start | bytes 6291460
  7.2 0.8 copy-start.2
  7.2 92.7 %all-gather.2.cloned.1.call-start = ((), (), s32[]{:S(2)}) async-start(), calls=%async_computation.1 | async-start | bytes 18874368 | tf_op jit(solution)/shard_map/all_gather | solution.py:88
  7.9 208.7 %reduce-scatter.2.cloned.1.call-start = ((), (), s32[]{:S(2)}) async-start(), calls=%async_computation.2 | async-start | bytes 4718592 | tf_op jit(solution)/shard_map/reduce_scatter | solution.py:128
  108.0 1.4 copy-start.5
  108.0 15.2 %copy-start.1 = (s32[2048]{0:T(1024)S(1)}, s32[2048]{0:T(1024)}, u32[]{:S(2)}) copy-start(s32[2048]{0:T(1024)} %param.11) | copy-start | bytes 24580
  108.0 16.5 %copy-start.4 = (f32[16,2048]{1,0:T(8,128)S(1)}, f32[16,2048]{1,0:T(8,128)}, u32[]{:S(2)}) copy-start(f32[16,2048]{1,0:T(8,128)} %param.8) | copy-start | bytes 393220
  108.1 39.7 %copy-start.3 = (s32[32]{0:T(128)S(1)}, s32[32]{0:T(128)}, u32[]{:S(2)}) copy-start(s32[32]{0:T(128)} %param.10) | copy-start | bytes 388
  109.4 1.4 collective-permute-start
  110.8 5.7 %collective-permute-start.1 = (f32[32,1024]{1,0:T(8,128)S(1)}, f32[32,1024]{1,0:T(8,128)S(1)}, u32[]{:S(2)}, u32[]{:S(2)}) collective-permute-start(f32[32,1024]{1,0:T(8,128)S(1)} %dynamic-slice_add_fusion.1), channel_id=1, source_target_pairs={{0,64},{64,0},{128,192},{192,128},{1,65},{65,1},{129,193},{193,129... | collective-permute-start | bytes 393224 | tf_op jit(solution)/shard_map/ppermute | solution.py:39
  116.6 5.1 %collective-permute-start.2 = (f32[32,1024]{1,0:T(8,128)S(1)}, f32[32,1024]{1,0:T(8,128)S(1)}, u32[]{:S(2)}, u32[]{:S(2)}) collective-permute-start(f32[32,1024]{1,0:T(8,128)S(1)} %add.103), channel_id=1, source_target_pairs={{0,192},{64,128},{128,64},{192,0},{1,193},{65,129},{129,65},{193,1... | collective-permute-start | bytes 393224 | tf_op jit(solution)/shard_map/ppermute | solution.py:39
  121.7 1.4 collective-permute-start.3
  124.5 23.8 %copy-start.6 = (f32[256,2048]{1,0:T(8,128)S(1)}, f32[256,2048]{1,0:T(8,128)}, u32[]{:S(2)}) copy-start(f32[256,2048]{1,0:T(8,128)} %copy-done.5) | copy-start | bytes 6291460
  125.0 3.8 %collective-permute-start.4 = (f32[17,32]{1,0:T(8,128)S(1)}, f32[17,32]{1,0:T(8,128)S(1)}, u32[]{:S(2)}, u32[]{:S(2)}) collective-permute-start(f32[17,32]{1,0:T(8,128)S(1)} %pad_maximum_fusion), channel_id=1, source_target_pairs={{0,1},{1,0},{2,3},{3,2},{4,5},{5,4},{6,7},{7,6},{8,9},{9,8},{10,11... | collective-permute-start | bytes 6536 | tf_op jit(solution)/shard_map/ppermute | solution.py:39
  128.7 4.9 %collective-permute-start.5 = (f32[17,32]{1,0:T(8,128)S(1)}, f32[17,32]{1,0:T(8,128)S(1)}, u32[]{:S(2)}, u32[]{:S(2)}) collective-permute-start(f32[17,32]{1,0:T(8,128)S(1)} %fusion.34), channel_id=1, source_target_pairs={{0,3},{1,2},{2,1},{3,0},{4,7},{5,6},{6,5},{7,4},{8,11},{9,10},{10,... | collective-permute-start | bytes 6536 | tf_op jit(solution)/shard_map/ppermute | solution.py:39
  133.7 3.7 %collective-permute-start.6 = (f32[17,32]{1,0:T(8,128)S(1)}, f32[17,32]{1,0:T(8,128)S(1)}, u32[]{:S(2)}, u32[]{:S(2)}) collective-permute-start(f32[17,32]{1,0:T(8,128)S(1)} %add.108), channel_id=1, source_target_pairs={{0,4},{4,0},{8,12},{12,8},{16,20},{20,16},{24,28},{28,24},{1,5},{5... | collective-permute-start | bytes 6536 | tf_op jit(solution)/shard_map/ppermute | solution.py:39
  137.4 5.8 %collective-permute-start.7 = (f32[17,32]{1,0:T(8,128)S(1)}, f32[17,32]{1,0:T(8,128)S(1)}, u32[]{:S(2)}, u32[]{:S(2)}) collective-permute-start(f32[17,32]{1,0:T(8,128)S(1)} %add.109), channel_id=1, source_target_pairs={{0,24},{4,28},{8,16},{12,20},{16,8},{20,12},{24,0},{28,4},{1,25},{... | collective-permute-start | bytes 6536 | tf_op jit(solution)/shard_map/ppermute | solution.py:39
  143.2 4.6 %collective-permute-start.8 = (f32[17,32]{1,0:T(8,128)S(1)}, f32[17,32]{1,0:T(8,128)S(1)}, u32[]{:S(2)}, u32[]{:S(2)}) collective-permute-start(f32[17,32]{1,0:T(8,128)S(1)} %add.110), channel_id=1, source_target_pairs={{0,8},{4,12},{8,0},{12,4},{16,24},{20,28},{24,16},{28,20},{1,9},{5... | collective-permute-start | bytes 6536 | tf_op jit(solution)/shard_map/ppermute | solution.py:39
  217.5 9.3 %collective-permute-start.9 = (f32[256,256]{0,1:T(8,128)S(1)}, f32[256,256]{0,1:T(8,128)S(1)}, u32[]{:S(2)}, u32[]{:S(2)}) collective-permute-start(f32[256,256]{0,1:T(8,128)S(1)} %constant_dynamic-slice_fusion.1), channel_id=1, source_target_pairs={{0,3},{1,2},{2,1},{3,0},{4,7},{5,6},{6,5},{7,4},{8,11},{9,10},{10,... | collective-permute-start | bytes 786440 | tf_op jit(solution)/shard_map/ppermute | solution.py:55
  227.8 5.1 %collective-permute-start.10 = (f32[128,256]{0,1:T(8,128)S(1)}, f32[128,256]{0,1:T(8,128)S(1)}, u32[]{:S(2)}, u32[]{:S(2)}) collective-permute-start(f32[128,256]{0,1:T(8,128)S(1)} %constant_dynamic-slice_fusion), channel_id=1, source_target_pairs={{0,1},{1,0},{2,3},{3,2},{4,5},{5,4},{6,7},{7,6},{8,9},{9,8},{10,11... | collective-permute-start | bytes 393224 | tf_op jit(solution)/shard_map/ppermute | solution.py:55
Sparse Core Ops, SparseCore 0:
  9.9 89.9 all-gather.1
  160.2 56.3 reduce-scatter.1

commit v9 on v8

--- a/solution.py
+++ b/solution.py
@@ -16,13 +16,6 @@
 
 
 def rounds_of(n):
-    if n == 8:
-        second = {0: 6, 6: 0, 1: 7, 7: 1, 2: 4, 4: 2, 3: 5, 5: 3}
-        return [
-            [(i, i ^ 1) for i in range(n)],
-            [(i, second[i]) for i in range(n)],
-            [(i, i ^ 2) for i in range(n)],
-        ]
     pairs = []
     d = 1
     while 2 * d < n:

time: 241 us -> 241 us (level)
  no operation moved by 1% of the time
where the time goes in v9:
time: 241 us
  waiting for transfers between devices  179 us (74%)
  matrix products  21.9 us (9%)
  starting transfers between devices  17.7 us (7%)
  between operations  15.6 us (6%)
  other arithmetic  4.57 us (2%)
    all_gather x1, waiting for transfers between devices, per_device(): full_head = lax.all_gather(head_weight, SEQ, axis=0, tiled=True)  91.6 us
    reduce_scatter x1, waiting for transfers between devices, per_device(): lax.psum_scatter(partial, 'vz', scatter_dimension=0, tiled=True)  57.4 us
    ppermute x7, waiting for transfers between devices, butterfly(): x = jax.tree.map(lambda a: a + lax.ppermute(a, ax, perm), x)  18.8 us
    ppermute x7, starting transfers between devices, butterfly(): x = jax.tree.map(lambda a: a + lax.ppermute(a, ax, perm), x)  14 us
    dot_general x1, matrix products, per_device(): lax.dot_general(full_head, dlogits, (((1,), (1,)), ((), ())), preferred_e...  10.2 us
    ppermute x2, waiting for transfers between devices, halving_scatter(): x = keep + lax.ppermute(send, ax, perm)  8.12 us
    dot_general x1, matrix products, per_device(): logits = jnp.dot(hidden, full_head, preferred_element_type=jnp.float32)  8.11 us
  transfers between devices with their start and end apart: 13, of which 13 were waited for; matrix products, arithmetic and copies ran while one was open for 1% of the time, Pallas kernels for 0%

profile of v9, /device:TPU:2, one launch (start us, length us, event | category | flops | bytes accessed | tf_op | source)
XLA Modules:
  0.0 240.5 jit_solution(16863495469572626074)
XLA Ops:
  7.2 0.0 copy-start
  7.2 0.0 copy-start.2
  7.2 0.0 all-gather.2.cloned.1.call-start
  7.2 0.7 all-gather.2.cloned.1.call-update
  7.9 0.0 reduce-scatter.2.cloned.1.call-start
  8.0 0.0 copy-done.2
  8.0 0.1 copy.9
  8.1 0.1 reduce-window.8
  8.1 0.1 reduce
  8.3 91.6 %all-gather.2.cloned.1.call-done = bf16[4096,2048]{1,0:T(8,128)(2,1)} async-done(((bf16[512,2048]{1,0:T(8,128)(2,1)}), bf16[4096,2048]{1,0:T(8,128)(2,1)}) %all-gather.2.cloned.1.call-update) | async-done | bytes 16777232 | tf_op jit(solution)/shard_map/all_gather | solution.py:81
  99.9 0.0 copy-done
  99.9 8.1 %fusion.35 = f32[256,2048]{1,0:T(8,128)S(1)} fusion(bf16[256,4096]{1,0:T(8,128)(2,1)S(1)} %copy-done, bf16[4096,2048]{1,0:T(8,128)(2,1)} %all-gather.2.cloned.1.call-done), kind=kOutput, calls=%fused_computation.64 | convolution fusion | flops 4294967296 | bytes 20971520 | tf_op jit(solution)/shard_map/dot_general | solution.py:82
  108.0 0.0 copy-start.5
  108.0 0.0 copy-start.1
  108.0 0.0 copy-start.4
  108.1 0.0 copy-start.3
  108.1 1.2 fusion.3
  109.3 0.1 copy-done.5
  109.4 0.3 collective-permute-start
  109.7 1.1 collective-permute-done
  110.8 1.0 collective-permute-start.1
  111.8 4.7 %collective-permute-done.1 = f32[32,1024]{1,0:T(8,128)S(1)} collective-permute-done((f32[32,1024]{1,0:T(8,128)S(1)}, f32[32,1024]{1,0:T(8,128)S(1)}, u32[]{:S(2)}, u32[]{:S(2)}) %collective-permute-start.1) | collective-permute-done | bytes 131104 | tf_op jit(solution)/shard_map/ppermute | solution.py:32
  116.6 1.3 collective-permute-start.2
  117.9 3.8 %collective-permute-done.2 = f32[32,1024]{1,0:T(8,128)S(1)} collective-permute-done((f32[32,1024]{1,0:T(8,128)S(1)}, f32[32,1024]{1,0:T(8,128)S(1)}, u32[]{:S(2)}, u32[]{:S(2)}) %collective-permute-start.2) | collective-permute-done | bytes 131104 | tf_op jit(solution)/shard_map/ppermute | solution.py:32
  121.7 0.1 collective-permute-start.3
  121.8 1.3 collective-permute-done.3
  123.1 0.1 fusion.8
  123.2 0.0 copy-done.1
  123.2 0.6 fusion.18
  124.5 0.0 copy-start.6
  124.5 0.0 copy-done.4
  124.5 0.4 convolution_bitcast_fusion.1
  124.9 0.1 pad_maximum_fusion
  125.0 1.6 collective-permute-start.4
  126.5 2.2 collective-permute-done.4
  128.7 2.7 %collective-permute-start.5 = (f32[17,32]{1,0:T(8,128)S(1)}, f32[17,32]{1,0:T(8,128)S(1)}, u32[]{:S(2)}, u32[]{:S(2)}) collective-permute-start(f32[17,32]{1,0:T(8,128)S(1)} %fusion.34), channel_id=1, source_target_pairs={{0,3},{1,2},{2,1},{3,0},{4,7},{5,6},{6,5},{7,4},{8,11},{9,10},{10,... | collective-permute-start | bytes 6536 | tf_op jit(solution)/shard_map/ppermute | solution.py:32
  131.5 2.2 collective-permute-done.5
  133.7 1.6 collective-permute-start.6
  135.2 2.1 collective-permute-done.6
  137.4 2.5 %collective-permute-start.7 = (f32[17,32]{1,0:T(8,128)S(1)}, f32[17,32]{1,0:T(8,128)S(1)}, u32[]{:S(2)}, u32[]{:S(2)}) collective-permute-start(f32[17,32]{1,0:T(8,128)S(1)} %add.109), channel_id=1, source_target_pairs={{0,8},{4,12},{8,0},{12,4},{16,24},{20,28},{24,16},{28,20},{1,9},{5... | collective-permute-start | bytes 6536 | tf_op jit(solution)/shard_map/ppermute | solution.py:32
  139.9 2.0 collective-permute-done.7
  142.0 3.3 %collective-permute-start.8 = (f32[17,32]{1,0:T(8,128)S(1)}, f32[17,32]{1,0:T(8,128)S(1)}, u32[]{:S(2)}, u32[]{:S(2)}) collective-permute-start(f32[17,32]{1,0:T(8,128)S(1)} %add.110), channel_id=1, source_target_pairs={{0,28},{4,24},{8,20},{12,16},{16,12},{20,8},{24,4},{28,0},{1,29},{... | collective-permute-start | bytes 6536 | tf_op jit(solution)/shard_map/ppermute | solution.py:32
  145.3 1.7 collective-permute-done.8
  147.0 0.0 copy-done.3
  147.0 0.4 fusion.2
  147.4 0.0 copy-done.6
  147.4 1.6 fusion.1
  149.0 10.2 %convolution_bitcast_fusion = f32[4096,256]{0,1:T(8,128)} fusion(bf16[256,2048]{1,0:T(8,128)(2,1)S(1)} %fusion.1, bf16[4096,2048]{1,0:T(8,128)(2,1)} %all-gather.2.cloned.1.call-done), kind=kOutput, calls=%fused_computation | convolution fusion | flops 4294967296 | bytes 22020096 | tf_op jit(solution)/shard_map/dot_general | solution.py:117
  159.2 0.0 reduce-scatter.2.cloned.1.call-update
  159.3 57.4 %reduce-scatter.2.cloned.1.call-done = f32[512,256]{0,1:T(8,128)} async-done(((f32[4096,256]{0,1:T(8,128)}), f32[512,256]{0,1:T(8,128)}) %reduce-scatter.2.cloned.1.call-update) | async-done | bytes 524304 | tf_op jit(solution)/shard_map/reduce_scatter | solution.py:121
  216.7 1.0 constant_dynamic-slice_fusion.1
  217.7 2.8 %collective-permute-start.9 = (f32[256,256]{0,1:T(8,128)S(1)}, f32[256,256]{0,1:T(8,128)S(1)}, u32[]{:S(2)}, u32[]{:S(2)}) collective-permute-start(f32[256,256]{0,1:T(8,128)S(1)} %constant_dynamic-slice_fusion.1), channel_id=1, source_target_pairs={{0,3},{1,2},{2,1},{3,0},{4,7},{5,6},{6,5},{7,4},{8,11},{9,10},{10,... | collective-permute-start | bytes 786440 | tf_op jit(solution)/shard_map/ppermute | solution.py:48
  220.5 6.4 %collective-permute-done.9 = f32[256,256]{0,1:T(8,128)S(1)} collective-permute-done((f32[256,256]{0,1:T(8,128)S(1)}, f32[256,256]{0,1:T(8,128)S(1)}, u32[]{:S(2)}, u32[]{:S(2)}) %collective-permute-start.9) | collective-permute-done | bytes 262176 | tf_op jit(solution)/shard_map/ppermute | solution.py:48
  227.0 1.0 dynamic-slice_add_fusion
  228.0 0.4 collective-permute-start.10
  228.3 0.6 subtract_reduce_fusion
  228.9 0.5 slice.9
  230.1 1.2 pad_maximum_fusion.1
  231.3 1.7 collective-permute-done.10
  233.0 0.6 fusion.11
  (16 shorter events, 0.2 us)
Async XLA Ops:
  7.2 92.7 %copy-start = (bf16[256,4096]{1,0:T(8,128)(2,1)S(1)}, bf16[256,4096]{1,0:T(8,128)(2,1)}, u32[]{:S(2)}) copy-start(bf16[256,4096]{1,0:T(8,128)(2,1)} %param.6) | copy-start | bytes 6291460
  7.2 0.8 copy-start.2
  7.2 92.7 %all-gather.2.cloned.1.call-start = ((), (), s32[]{:S(2)}) async-start(), calls=%async_computation.1 | async-start | bytes 18874368 | tf_op jit(solution)/shard_map/all_gather | solution.py:81
  7.9 208.8 %reduce-scatter.2.cloned.1.call-start = ((), (), s32[]{:S(2)}) async-start(), calls=%async_computation.2 | async-start | bytes 4718592 | tf_op jit(solution)/shard_map/reduce_scatter | solution.py:121
  108.0 1.4 copy-start.5
  108.0 15.2 %copy-start.1 = (s32[2048]{0:T(1024)S(1)}, s32[2048]{0:T(1024)}, u32[]{:S(2)}) copy-start(s32[2048]{0:T(1024)} %param.11) | copy-start | bytes 24580
  108.0 16.5 %copy-start.4 = (f32[16,2048]{1,0:T(8,128)S(1)}, f32[16,2048]{1,0:T(8,128)}, u32[]{:S(2)}) copy-start(f32[16,2048]{1,0:T(8,128)} %param.8) | copy-start | bytes 393220
  108.1 38.9 %copy-start.3 = (s32[32]{0:T(128)S(1)}, s32[32]{0:T(128)}, u32[]{:S(2)}) copy-start(s32[32]{0:T(128)} %param.10) | copy-start | bytes 388
  109.4 1.4 collective-permute-start
  110.8 5.7 %collective-permute-start.1 = (f32[32,1024]{1,0:T(8,128)S(1)}, f32[32,1024]{1,0:T(8,128)S(1)}, u32[]{:S(2)}, u32[]{:S(2)}) collective-permute-start(f32[32,1024]{1,0:T(8,128)S(1)} %dynamic-slice_add_fusion.1), channel_id=1, source_target_pairs={{0,64},{64,0},{128,192},{192,128},{1,65},{65,1},{129,193},{193,129... | collective-permute-start | bytes 393224 | tf_op jit(solution)/shard_map/ppermute | solution.py:32
  116.6 5.1 %collective-permute-start.2 = (f32[32,1024]{1,0:T(8,128)S(1)}, f32[32,1024]{1,0:T(8,128)S(1)}, u32[]{:S(2)}, u32[]{:S(2)}) collective-permute-start(f32[32,1024]{1,0:T(8,128)S(1)} %add.103), channel_id=1, source_target_pairs={{0,192},{64,128},{128,64},{192,0},{1,193},{65,129},{129,65},{193,1... | collective-permute-start | bytes 393224 | tf_op jit(solution)/shard_map/ppermute | solution.py:32
  121.7 1.4 collective-permute-start.3
  124.5 22.9 %copy-start.6 = (f32[256,2048]{1,0:T(8,128)S(1)}, f32[256,2048]{1,0:T(8,128)}, u32[]{:S(2)}) copy-start(f32[256,2048]{1,0:T(8,128)} %copy-done.5) | copy-start | bytes 6291460
  125.0 3.8 %collective-permute-start.4 = (f32[17,32]{1,0:T(8,128)S(1)}, f32[17,32]{1,0:T(8,128)S(1)}, u32[]{:S(2)}, u32[]{:S(2)}) collective-permute-start(f32[17,32]{1,0:T(8,128)S(1)} %pad_maximum_fusion), channel_id=1, source_target_pairs={{0,1},{1,0},{2,3},{3,2},{4,5},{5,4},{6,7},{7,6},{8,9},{9,8},{10,11... | collective-permute-start | bytes 6536 | tf_op jit(solution)/shard_map/ppermute | solution.py:32
  128.7 4.9 %collective-permute-start.5 = (f32[17,32]{1,0:T(8,128)S(1)}, f32[17,32]{1,0:T(8,128)S(1)}, u32[]{:S(2)}, u32[]{:S(2)}) collective-permute-start(f32[17,32]{1,0:T(8,128)S(1)} %fusion.34), channel_id=1, source_target_pairs={{0,3},{1,2},{2,1},{3,0},{4,7},{5,6},{6,5},{7,4},{8,11},{9,10},{10,... | collective-permute-start | bytes 6536 | tf_op jit(solution)/shard_map/ppermute | solution.py:32
  133.7 3.7 %collective-permute-start.6 = (f32[17,32]{1,0:T(8,128)S(1)}, f32[17,32]{1,0:T(8,128)S(1)}, u32[]{:S(2)}, u32[]{:S(2)}) collective-permute-start(f32[17,32]{1,0:T(8,128)S(1)} %add.108), channel_id=1, source_target_pairs={{0,4},{4,0},{8,12},{12,8},{16,20},{20,16},{24,28},{28,24},{1,5},{5... | collective-permute-start | bytes 6536 | tf_op jit(solution)/shard_map/ppermute | solution.py:32
  137.4 4.6 %collective-permute-start.7 = (f32[17,32]{1,0:T(8,128)S(1)}, f32[17,32]{1,0:T(8,128)S(1)}, u32[]{:S(2)}, u32[]{:S(2)}) collective-permute-start(f32[17,32]{1,0:T(8,128)S(1)} %add.109), channel_id=1, source_target_pairs={{0,8},{4,12},{8,0},{12,4},{16,24},{20,28},{24,16},{28,20},{1,9},{5... | collective-permute-start | bytes 6536 | tf_op jit(solution)/shard_map/ppermute | solution.py:32
  142.0 5.0 %collective-permute-start.8 = (f32[17,32]{1,0:T(8,128)S(1)}, f32[17,32]{1,0:T(8,128)S(1)}, u32[]{:S(2)}, u32[]{:S(2)}) collective-permute-start(f32[17,32]{1,0:T(8,128)S(1)} %add.110), channel_id=1, source_target_pairs={{0,28},{4,24},{8,20},{12,16},{16,12},{20,8},{24,4},{28,0},{1,29},{... | collective-permute-start | bytes 6536 | tf_op jit(solution)/shard_map/ppermute | solution.py:32
  217.7 9.3 %collective-permute-start.9 = (f32[256,256]{0,1:T(8,128)S(1)}, f32[256,256]{0,1:T(8,128)S(1)}, u32[]{:S(2)}, u32[]{:S(2)}) collective-permute-start(f32[256,256]{0,1:T(8,128)S(1)} %constant_dynamic-slice_fusion.1), channel_id=1, source_target_pairs={{0,3},{1,2},{2,1},{3,0},{4,7},{5,6},{6,5},{7,4},{8,11},{9,10},{10,... | collective-permute-start | bytes 786440 | tf_op jit(solution)/shard_map/ppermute | solution.py:48
  228.0 5.1 %collective-permute-start.10 = (f32[128,256]{0,1:T(8,128)S(1)}, f32[128,256]{0,1:T(8,128)S(1)}, u32[]{:S(2)}, u32[]{:S(2)}) collective-permute-start(f32[128,256]{0,1:T(8,128)S(1)} %constant_dynamic-slice_fusion), channel_id=1, source_target_pairs={{0,1},{1,0},{2,3},{3,2},{4,5},{5,4},{6,7},{7,6},{8,9},{9,8},{10,11... | collective-permute-start | bytes 393224 | tf_op jit(solution)/shard_map/ppermute | solution.py:48
Sparse Core Ops, SparseCore 0:
  9.9 89.9 all-gather.1
  159.4 57.3 reduce-scatter.1

commit v10 on v8

--- a/solution.py
+++ b/solution.py
@@ -91,6 +91,9 @@
     squared = lifted * lifted
     fourth = squared * squared
     powered = fourth * fourth
+    masked_seventh = lax.optimization_barrier(
+        jnp.where(logits > 0, fourth * squared * lifted, 0.0)
+    )
     local_sums = jnp.dot(member, powered, precision=highest)
     core = lax.axis_index("sc")
     half_cols = vocab_cols // n_sc
@@ -119,8 +122,7 @@
     dpooled = jnp.dot(dscores.T, queries, precision=highest) + flops_grad * weights_df * col_mean
     factor = dpooled / totals
     spread = lax.dot_general(member, factor, (((0,), (0,)), ((), ())), precision=highest)
-    seventh = fourth * squared * lifted
-    dlogits = jnp.where(logits > 0, spread * seventh, 0.0).astype(jnp.bfloat16)
+    dlogits = jnp.where(masked_seventh > 0, spread * masked_seventh, 0.0).astype(jnp.bfloat16)
     partial = lax.dot_general(
         full_head, dlogits, (((1,), (1,)), ((), ())), preferred_element_type=jnp.float32
     )

time: 241 us -> 242 us (level)
  no operation moved by 1% of the time
where the time goes in v10:
time: 242 us
  waiting for transfers between devices  178 us (74%)
  matrix products  23.4 us (10%)
  starting transfers between devices  18.5 us (8%)
  between operations  15.6 us (6%)
  other arithmetic  4.57 us (2%)
    all_gather x1, waiting for transfers between devices, per_device(): full_head = lax.all_gather(head_weight, SEQ, axis=0, tiled=True)  91.6 us
    reduce_scatter x1, waiting for transfers between devices, per_device(): lax.psum_scatter(partial, 'vz', scatter_dimension=0, tiled=True)  56.5 us
    ppermute x7, waiting for transfers between devices, butterfly(): x = jax.tree.map(lambda a: a + lax.ppermute(a, ax, perm), x)  18.8 us
    ppermute x7, starting transfers between devices, butterfly(): x = jax.tree.map(lambda a: a + lax.ppermute(a, ax, perm), x)  14.8 us
    dot_general x1, matrix products, per_device(): lax.dot_general(full_head, dlogits, (((1,), (1,)), ((), ())), preferred_e...  10.2 us
    dot_general x1, matrix products, per_device(): logits = jnp.dot(hidden, full_head, preferred_element_type=jnp.float32)  10 us
    ppermute x2, waiting for transfers between devices, halving_scatter(): x = keep + lax.ppermute(send, ax, perm)  8.16 us
  transfers between devices with their start and end apart: 13, of which 13 were waited for; matrix products, arithmetic and copies ran while one was open for 1% of the time, Pallas kernels for 0%

profile of v10, /device:TPU:2, one launch (start us, length us, event | category | flops | bytes accessed | tf_op | source)
XLA Modules:
  0.0 241.8 jit_solution(2550403479183046102)
XLA Ops:
  7.2 0.0 copy-start
  7.2 0.0 copy-start.3
  7.2 0.0 all-gather.2.cloned.1.call-start
  7.2 0.7 all-gather.2.cloned.1.call-update
  7.9 0.0 reduce-scatter.2.cloned.1.call-start
  8.0 0.0 copy-done.3
  8.0 0.1 copy.9
  8.1 0.1 reduce-window.8
  8.1 0.1 reduce
  8.3 91.6 %all-gather.2.cloned.1.call-done = bf16[4096,2048]{1,0:T(8,128)(2,1)} async-done(((bf16[512,2048]{1,0:T(8,128)(2,1)}), bf16[4096,2048]{1,0:T(8,128)(2,1)}) %all-gather.2.cloned.1.call-update) | async-done | bytes 16777232 | tf_op jit(solution)/shard_map/all_gather | solution.py:88
  99.9 0.0 copy-done
  99.9 10.0 %fusion.4 = (f32[256,2048]{1,0:T(8,128)}, f32[256,2048]{1,0:T(8,128)S(1)}) fusion(bf16[256,4096]{1,0:T(8,128)(2,1)S(1)} %copy-done, bf16[4096,2048]{1,0:T(8,128)(2,1)} %all-gather.2.cloned.1.call-done), kind=kOutput, calls=%fused_computation.9 | convolution fusion | flops 4299161600 | bytes 23068672 | tf_op jit(solution)/shard_map/dot_general | solution.py:89
  109.9 0.0 copy-start.2
  109.9 0.0 copy-start.5
  109.9 0.0 copy-start.4
  109.9 1.2 fusion.5
  111.2 0.3 collective-permute-start
  111.5 1.1 collective-permute-done
  112.6 1.0 collective-permute-start.1
  113.6 4.7 %collective-permute-done.1 = f32[32,1024]{1,0:T(8,128)S(1)} collective-permute-done((f32[32,1024]{1,0:T(8,128)S(1)}, f32[32,1024]{1,0:T(8,128)S(1)}, u32[]{:S(2)}, u32[]{:S(2)}) %collective-permute-start.1) | collective-permute-done | bytes 131104 | tf_op jit(solution)/shard_map/ppermute | solution.py:39
  118.4 1.3 collective-permute-start.2
  119.6 3.8 %collective-permute-done.2 = f32[32,1024]{1,0:T(8,128)S(1)} collective-permute-done((f32[32,1024]{1,0:T(8,128)S(1)}, f32[32,1024]{1,0:T(8,128)S(1)}, u32[]{:S(2)}, u32[]{:S(2)}) %collective-permute-start.2) | collective-permute-done | bytes 131104 | tf_op jit(solution)/shard_map/ppermute | solution.py:39
  123.5 0.1 collective-permute-start.3
  123.6 1.3 collective-permute-done.3
  124.9 0.1 fusion.9
  125.0 0.0 copy-done.2
  125.0 0.6 fusion.19
  126.3 0.0 copy-start.1
  126.3 0.0 copy-done.5
  126.3 0.4 convolution_bitcast_fusion.1
  126.7 0.1 pad_maximum_fusion
  126.7 1.6 collective-permute-start.4
  128.3 2.2 collective-permute-done.4
  130.5 2.7 %collective-permute-start.5 = (f32[17,32]{1,0:T(8,128)S(1)}, f32[17,32]{1,0:T(8,128)S(1)}, u32[]{:S(2)}, u32[]{:S(2)}) collective-permute-start(f32[17,32]{1,0:T(8,128)S(1)} %fusion.35), channel_id=1, source_target_pairs={{0,3},{1,2},{2,1},{3,0},{4,7},{5,6},{6,5},{7,4},{8,11},{9,10},{10,... | collective-permute-start | bytes 6536 | tf_op jit(solution)/shard_map/ppermute | solution.py:39
  133.3 2.2 collective-permute-done.5
  135.4 1.6 collective-permute-start.6
  137.0 2.1 collective-permute-done.6
  139.1 4.1 %collective-permute-start.7 = (f32[17,32]{1,0:T(8,128)S(1)}, f32[17,32]{1,0:T(8,128)S(1)}, u32[]{:S(2)}, u32[]{:S(2)}) collective-permute-start(f32[17,32]{1,0:T(8,128)S(1)} %add.109), channel_id=1, source_target_pairs={{0,24},{4,28},{8,16},{12,20},{16,8},{20,12},{24,0},{28,4},{1,25},{... | collective-permute-start | bytes 6536 | tf_op jit(solution)/shard_map/ppermute | solution.py:39
  143.3 1.7 collective-permute-done.7
  145.0 2.5 %collective-permute-start.8 = (f32[17,32]{1,0:T(8,128)S(1)}, f32[17,32]{1,0:T(8,128)S(1)}, u32[]{:S(2)}, u32[]{:S(2)}) collective-permute-start(f32[17,32]{1,0:T(8,128)S(1)} %add.110), channel_id=1, source_target_pairs={{0,8},{4,12},{8,0},{12,4},{16,24},{20,28},{24,16},{28,20},{1,9},{5... | collective-permute-start | bytes 6536 | tf_op jit(solution)/shard_map/ppermute | solution.py:39
  147.5 2.1 collective-permute-done.8
  149.6 0.0 copy-done.4
  149.6 0.4 fusion.2
  150.1 0.0 copy-done.1
  150.1 1.2 fusion.1
  151.3 10.2 %convolution_bitcast_fusion = f32[4096,256]{0,1:T(8,128)} fusion(bf16[256,2048]{1,0:T(8,128)(2,1)S(1)} %fusion.1, bf16[4096,2048]{1,0:T(8,128)(2,1)} %all-gather.2.cloned.1.call-done), kind=kOutput, calls=%fused_computation | convolution fusion | flops 4294967296 | bytes 22020096 | tf_op jit(solution)/shard_map/dot_general | solution.py:126
  161.4 0.0 reduce-scatter.2.cloned.1.call-update
  161.5 56.5 %reduce-scatter.2.cloned.1.call-done = f32[512,256]{0,1:T(8,128)} async-done(((f32[4096,256]{0,1:T(8,128)}), f32[512,256]{0,1:T(8,128)}) %reduce-scatter.2.cloned.1.call-update) | async-done | bytes 524304 | tf_op jit(solution)/shard_map/reduce_scatter | solution.py:130
  218.0 1.0 constant_dynamic-slice_fusion.1
  218.9 2.8 %collective-permute-start.9 = (f32[256,256]{0,1:T(8,128)S(1)}, f32[256,256]{0,1:T(8,128)S(1)}, u32[]{:S(2)}, u32[]{:S(2)}) collective-permute-start(f32[256,256]{0,1:T(8,128)S(1)} %constant_dynamic-slice_fusion.1), channel_id=1, source_target_pairs={{0,3},{1,2},{2,1},{3,0},{4,7},{5,6},{6,5},{7,4},{8,11},{9,10},{10,... | collective-permute-start | bytes 786440 | tf_op jit(solution)/shard_map/ppermute | solution.py:55
  221.7 6.5 %collective-permute-done.9 = f32[256,256]{0,1:T(8,128)S(1)} collective-permute-done((f32[256,256]{0,1:T(8,128)S(1)}, f32[256,256]{0,1:T(8,128)S(1)}, u32[]{:S(2)}, u32[]{:S(2)}) %collective-permute-start.9) | collective-permute-done | bytes 262176 | tf_op jit(solution)/shard_map/ppermute | solution.py:55
  228.2 1.0 dynamic-slice_add_fusion
  229.2 0.4 collective-permute-start.10
  229.6 0.6 subtract_reduce_fusion
  230.2 0.5 slice.9
  231.3 1.2 pad_maximum_fusion.1
  232.6 1.7 collective-permute-done.10
  234.3 0.6 fusion.12
  (16 shorter events, 0.2 us)
Async XLA Ops:
  7.2 92.7 %copy-start = (bf16[256,4096]{1,0:T(8,128)(2,1)S(1)}, bf16[256,4096]{1,0:T(8,128)(2,1)}, u32[]{:S(2)}) copy-start(bf16[256,4096]{1,0:T(8,128)(2,1)} %param.6) | copy-start | bytes 6291460
  7.2 0.8 copy-start.3
  7.2 92.7 %all-gather.2.cloned.1.call-start = ((), (), s32[]{:S(2)}) async-start(), calls=%async_computation.1 | async-start | bytes 18874368 | tf_op jit(solution)/shard_map/all_gather | solution.py:88
  7.9 210.0 %reduce-scatter.2.cloned.1.call-start = ((), (), s32[]{:S(2)}) async-start(), calls=%async_computation.2 | async-start | bytes 4718592 | tf_op jit(solution)/shard_map/reduce_scatter | solution.py:130
  109.9 15.1 %copy-start.2 = (s32[2048]{0:T(1024)S(1)}, s32[2048]{0:T(1024)}, u32[]{:S(2)}) copy-start(s32[2048]{0:T(1024)} %param.11) | copy-start | bytes 24580
  109.9 16.4 %copy-start.5 = (f32[16,2048]{1,0:T(8,128)S(1)}, f32[16,2048]{1,0:T(8,128)}, u32[]{:S(2)}) copy-start(f32[16,2048]{1,0:T(8,128)} %param.8) | copy-start | bytes 393220
  109.9 39.6 %copy-start.4 = (s32[32]{0:T(128)S(1)}, s32[32]{0:T(128)}, u32[]{:S(2)}) copy-start(s32[32]{0:T(128)} %param.10) | copy-start | bytes 388
  111.2 1.4 collective-permute-start
  112.6 5.7 %collective-permute-start.1 = (f32[32,1024]{1,0:T(8,128)S(1)}, f32[32,1024]{1,0:T(8,128)S(1)}, u32[]{:S(2)}, u32[]{:S(2)}) collective-permute-start(f32[32,1024]{1,0:T(8,128)S(1)} %dynamic-slice_add_fusion.1), channel_id=1, source_target_pairs={{0,64},{64,0},{128,192},{192,128},{1,65},{65,1},{129,193},{193,129... | collective-permute-start | bytes 393224 | tf_op jit(solution)/shard_map/ppermute | solution.py:39
  118.4 5.1 %collective-permute-start.2 = (f32[32,1024]{1,0:T(8,128)S(1)}, f32[32,1024]{1,0:T(8,128)S(1)}, u32[]{:S(2)}, u32[]{:S(2)}) collective-permute-start(f32[32,1024]{1,0:T(8,128)S(1)} %add.103), channel_id=1, source_target_pairs={{0,192},{64,128},{128,64},{192,0},{1,193},{65,129},{129,65},{193,1... | collective-permute-start | bytes 393224 | tf_op jit(solution)/shard_map/ppermute | solution.py:39
  123.5 1.4 collective-permute-start.3
  126.3 23.8 %copy-start.1 = (f32[256,2048]{1,0:T(8,128)S(1)}, f32[256,2048]{1,0:T(8,128)}, u32[]{:S(2)}) copy-start(f32[256,2048]{1,0:T(8,128)} %get-tuple-element.6) | copy-start | bytes 6291460
  126.7 3.8 %collective-permute-start.4 = (f32[17,32]{1,0:T(8,128)S(1)}, f32[17,32]{1,0:T(8,128)S(1)}, u32[]{:S(2)}, u32[]{:S(2)}) collective-permute-start(f32[17,32]{1,0:T(8,128)S(1)} %pad_maximum_fusion), channel_id=1, source_target_pairs={{0,1},{1,0},{2,3},{3,2},{4,5},{5,4},{6,7},{7,6},{8,9},{9,8},{10,11... | collective-permute-start | bytes 6536 | tf_op jit(solution)/shard_map/ppermute | solution.py:39
  130.5 4.9 %collective-permute-start.5 = (f32[17,32]{1,0:T(8,128)S(1)}, f32[17,32]{1,0:T(8,128)S(1)}, u32[]{:S(2)}, u32[]{:S(2)}) collective-permute-start(f32[17,32]{1,0:T(8,128)S(1)} %fusion.35), channel_id=1, source_target_pairs={{0,3},{1,2},{2,1},{3,0},{4,7},{5,6},{6,5},{7,4},{8,11},{9,10},{10,... | collective-permute-start | bytes 6536 | tf_op jit(solution)/shard_map/ppermute | solution.py:39
  135.4 3.7 %collective-permute-start.6 = (f32[17,32]{1,0:T(8,128)S(1)}, f32[17,32]{1,0:T(8,128)S(1)}, u32[]{:S(2)}, u32[]{:S(2)}) collective-permute-start(f32[17,32]{1,0:T(8,128)S(1)} %add.108), channel_id=1, source_target_pairs={{0,4},{4,0},{8,12},{12,8},{16,20},{20,16},{24,28},{28,24},{1,5},{5... | collective-permute-start | bytes 6536 | tf_op jit(solution)/shard_map/ppermute | solution.py:39
  139.1 5.8 %collective-permute-start.7 = (f32[17,32]{1,0:T(8,128)S(1)}, f32[17,32]{1,0:T(8,128)S(1)}, u32[]{:S(2)}, u32[]{:S(2)}) collective-permute-start(f32[17,32]{1,0:T(8,128)S(1)} %add.109), channel_id=1, source_target_pairs={{0,24},{4,28},{8,16},{12,20},{16,8},{20,12},{24,0},{28,4},{1,25},{... | collective-permute-start | bytes 6536 | tf_op jit(solution)/shard_map/ppermute | solution.py:39
  145.0 4.6 %collective-permute-start.8 = (f32[17,32]{1,0:T(8,128)S(1)}, f32[17,32]{1,0:T(8,128)S(1)}, u32[]{:S(2)}, u32[]{:S(2)}) collective-permute-start(f32[17,32]{1,0:T(8,128)S(1)} %add.110), channel_id=1, source_target_pairs={{0,8},{4,12},{8,0},{12,4},{16,24},{20,28},{24,16},{28,20},{1,9},{5... | collective-permute-start | bytes 6536 | tf_op jit(solution)/shard_map/ppermute | solution.py:39
  218.9 9.3 %collective-permute-start.9 = (f32[256,256]{0,1:T(8,128)S(1)}, f32[256,256]{0,1:T(8,128)S(1)}, u32[]{:S(2)}, u32[]{:S(2)}) collective-permute-start(f32[256,256]{0,1:T(8,128)S(1)} %constant_dynamic-slice_fusion.1), channel_id=1, source_target_pairs={{0,3},{1,2},{2,1},{3,0},{4,7},{5,6},{6,5},{7,4},{8,11},{9,10},{10,... | collective-permute-start | bytes 786440 | tf_op jit(solution)/shard_map/ppermute | solution.py:55
  229.2 5.1 %collective-permute-start.10 = (f32[128,256]{0,1:T(8,128)S(1)}, f32[128,256]{0,1:T(8,128)S(1)}, u32[]{:S(2)}, u32[]{:S(2)}) collective-permute-start(f32[128,256]{0,1:T(8,128)S(1)} %constant_dynamic-slice_fusion), channel_id=1, source_target_pairs={{0,1},{1,0},{2,3},{3,2},{4,5},{5,4},{6,7},{7,6},{8,9},{9,8},{10,11... | collective-permute-start | bytes 393224 | tf_op jit(solution)/shard_map/ppermute | solution.py:55
Sparse Core Ops, SparseCore 0:
  9.9 89.9 all-gather.1
  161.6 56.3 reduce-scatter.1
